TPU v7x, 128 devices: a whole 4x4x4 slice. The times are simulated.
128 devices in a mesh: section: 4 (over x), expert: 32 (over z, y, core).
Axes of the slice: x: 4, y: 4, z: 4, core: 2. Of those that a mesh axis runs over, the one named last changes fastest.
Arguments:
- hidden_in: bfloat16 [4, 4096, 2880], P('section', 'expert')
- norm_gain: float32 [4, 2880], P('section'), may hold values from 0.25 to 1.75
- out_grad: bfloat16 [4, 4096, 2880], P('section', 'expert'), may hold values from -6 to 6
- expert_ids: int32 [4, 4096, 4], P('section', 'expert'), may hold values from 0 to 31, all different within a row; in each aligned block of 128 rows (0 to 127, 128 to 255, ..., all dimensions but the last counted through in order) at most 20 rows name the same one
- route_weights: float32 [4, 4096, 4], P('section', 'expert'), may hold values from 0 to 1, as said below
- w_gate_up: bfloat16 [4, 32, 2880, 2880], P('section', 'expert'), may hold values from -0.109375 to 0.109375
- w_down: bfloat16 [4, 32, 1440, 2880], P('section', 'expert'), may hold values from -0.15625 to 0.15625
Outputs:
- input_grad: bfloat16 [4, 4096, 2880], P('section', 'expert')
Inputs may be any that keep to these rules, and one draw needn't show every extreme that they name: `expert_ids`: each token names 4 different experts. The 128 tokens of one index of expert in one section name any one expert at most 20 times, a bound that some block reaches. `route_weights`: each token's 4 weights are positive and sum to one.
All inputs are finite; a program needn't handle non-finite values.
Results may differ from a plain program's by a relative error of at most 0.0047.
Values may be sent and summed in bfloat16 or wider, within the bound.
No kernel may reach another device: no remote copies, remote signals or barrier semaphores. Data moves between devices by JAX's collectives and lax.ppermute only.
A program may use at most 128 MiB of HBM per device.

v0:
```python
import jax
import jax.numpy as jnp
from jax import lax
from jax.sharding import PartitionSpec as P

glu_alpha = 1.702
norm_eps = 1e-05


def shifted(value, axis, steps):
    count = lax.axis_size(axis)
    pairs = [(source, (source + steps) % count) for source in range(count)]
    return lax.ppermute(value, axis, pairs)


def expert_backward(rows_in, grad_rows, gate_up, down_proj):
    preact = jnp.dot(rows_in, gate_up, preferred_element_type=jnp.float32)
    dact = lax.dot_general(
        grad_rows, down_proj, (((1,), (1,)), ((), ())), preferred_element_type=jnp.float32
    )
    half = down_proj.shape[0]
    gate = preact[:, :half]
    up_part = preact[:, half:]
    sig = jax.nn.sigmoid(glu_alpha * gate)
    dgate = dact * (up_part + 1.0) * (sig + glu_alpha * gate * sig * (1.0 - sig))
    dup = dact * gate * sig
    dpre = jnp.concatenate([dgate, dup], axis=1).astype(jnp.bfloat16)
    result = lax.dot_general(
        dpre, gate_up, (((1,), (1,)), ((), ())), preferred_element_type=jnp.float32
    )
    return result.astype(jnp.bfloat16)


def slab_backward(inputs_slab, grads_slab, gate_up, down_proj):
    sources, slot_count, feat_width = inputs_slab.shape
    flat_out = expert_backward(
        inputs_slab.reshape(sources * slot_count, feat_width),
        grads_slab.reshape(sources * slot_count, feat_width),
        gate_up,
        down_proj,
    )
    return flat_out.reshape(sources, slot_count, feat_width)


def send_back(slab):
    return lax.all_to_all(slab, "expert", split_axis=0, concat_axis=0, tiled=True)


def per_device(hidden_in, norm_gain, out_grad, expert_ids, route_weights, w_gate_up, w_down):
    tokens = hidden_in[0]
    gain_vector_row = norm_gain[0]
    incoming_gradient = out_grad[0]
    routes = expert_ids[0]
    weights = route_weights[0]
    gate_up = w_gate_up[0, 0]
    down_proj = w_down[0, 0]
    tok_count = tokens.shape[0]
    feat_width = tokens.shape[1]
    top_count = routes.shape[1]
    experts = lax.axis_size("expert")
    capacity = max(2, tok_count * top_count * 5 // (4 * experts))
    input_single_precision = tokens.astype(jnp.float32)
    inverse_root_mean = lax.rsqrt(
        jnp.mean(input_single_precision * input_single_precision, axis=-1, keepdims=True) + norm_eps
    )
    normalized_input = input_single_precision * inverse_root_mean
    rescaled_input = (normalized_input * gain_vector_row[None, :]).astype(jnp.bfloat16)
    flat_ids = routes.reshape(-1)
    assign = flat_ids.shape[0]
    one_hot = (flat_ids[:, None] == jnp.arange(experts, dtype=jnp.int32)[None, :]).astype(jnp.int32)
    slot_rank = jnp.sum((jnp.cumsum(one_hot, axis=0) - one_hot) * one_hot, axis=1)
    slot_index = flat_ids * capacity + slot_rank
    source_of = (
        jnp.full((experts * capacity,), assign, jnp.int32)
        .at[slot_index]
        .set(jnp.arange(assign, dtype=jnp.int32))
    )
    token_of = source_of // top_count
    normed_pad = jnp.concatenate([rescaled_input, jnp.zeros((1, feat_width), jnp.bfloat16)], axis=0)
    grad_pad = jnp.concatenate(
        [incoming_gradient.astype(jnp.float32), jnp.zeros((1, feat_width), jnp.float32)], axis=0
    )
    weight_pad = jnp.concatenate([weights.reshape(-1), jnp.zeros((1,), jnp.float32)])
    inputs_slab = normed_pad[token_of].reshape(experts, capacity, feat_width)
    grads_slab = (
        (weight_pad[source_of][:, None] * grad_pad[token_of])
        .astype(jnp.bfloat16)
        .reshape(experts, capacity, feat_width)
    )
    arrived_inputs = lax.all_to_all(inputs_slab, "expert", split_axis=0, concat_axis=0, tiled=True)
    arrived_grads = lax.all_to_all(grads_slab, "expert", split_axis=0, concat_axis=0, tiled=True)
    returned = send_back(slab_backward(arrived_inputs, arrived_grads, gate_up, down_proj))
    gathered = returned.reshape(experts * capacity, feat_width)[slot_index].astype(jnp.float32)
    dnorm = jnp.sum(gathered.reshape(tok_count, top_count, feat_width), axis=1)
    normalized_input_gradient = dnorm * gain_vector_row[None, :]
    projected_rows = jnp.mean(normalized_input_gradient * normalized_input, axis=-1, keepdims=True)
    section_gradient = (
        incoming_gradient.astype(jnp.float32)
        + inverse_root_mean * (normalized_input_gradient - normalized_input * projected_rows)
    ).astype(jnp.bfloat16)
    return shifted(section_gradient[None], "section", -1)


def solution(mesh):
    return jax.shard_map(
        per_device,
        mesh=mesh,
        in_specs=(
            P("section", "expert", None),
            P("section", None),
            P("section", "expert", None),
            P("section", "expert", None),
            P("section", "expert", None),
            P("section", "expert", None, None),
            P("section", "expert", None, None),
        ),
        out_specs=P("section", "expert", None),
        check_vma=False,
    )
```

profile of v0, /device:TPU:6, one launch (start us, length us, event | category | flops | bytes accessed | tf_op | source)
XLA Modules:
  0.0 307.6 jit_solution(7512824774346328776)
XLA Ops:
  0.0 0.8 copy.27
  1.7 1.2 reduce-window.6
  3.5 2.4 scatter_custom_fusion
  6.0 1.5 copy.24
  8.8 4.6 %gather_fusion.2 = bf16[640,2880]{1,0:T(8,128)(2,1)} fusion(bf16[129,2880]{1,0:T(8,128)(2,1)S(1)} %concatenate.18, s32[1024]{0:T(1024)S(1)} %get-tuple-element.9), kind=kCustom, calls=%fused_computation.2 | custom fusion | bytes 7375360 | tf_op jit(solution)/shard_map/gather | solution.py:84
  13.3 6.5 %reshape.142 = bf16[32,20,2880]{2,1,0:T(8,128)(2,1)} reshape(bf16[640,2880]{1,0:T(8,128)(2,1)} %gather_fusion.2) | data formatting | bytes 7372800 | tf_op jit(solution)/shard_map/reshape | solution.py:84
  19.9 8.6 %all-to-all-start.1 = ((bf16[32,20,2880]{2,1,0:T(8,128)(2,1)}), bf16[32,20,2880]{2,1,0:T(8,128)(2,1)}, u32[]{:S(2)}, u32[]{:S(2)}) async-start(bf16[32,20,2880]{2,1,0:T(8,128)(2,1)} %reshape.142), calls=%async_computation.1 | async-start | bytes 9043968 | tf_op jit(solution)/shard_map/all_to_all | solution.py:90
  28.9 5.6 %gather_fusion.1 = f32[640,2880]{1,0:T(8,128)} fusion(f32[129,2880]{1,0:T(8,128)S(1)} %pad_convert_fusion, s32[1024]{0:T(1024)S(1)} %get-tuple-element.9), kind=kCustom, calls=%fused_computation.1 | custom fusion | bytes 14748160 | tf_op jit(solution)/shard_map/gather | solution.py:86
  34.5 8.3 %gather.16 = f32[32,20,2880]{2,1,0:T(8,128)} reshape(f32[640,2880]{1,0:T(8,128)} %gather_fusion.1) | data formatting | bytes 14745600 | tf_op jit(solution)/shard_map/gather | solution.py:86
  43.1 2.8 gather_fusion
  46.0 6.7 %multiply_convert_fusion = bf16[32,20,2880]{2,1,0:T(8,128)(2,1)} fusion(f32[32,20,2880]{2,1,0:T(8,128)} %gather.16, f32[32,20]{1,0:T(8,128)S(1)} %mul.120), kind=kLoop, calls=%fused_computation.9 | loop fusion | flops 3686400 | bytes 11061760 | tf_op jit(solution)/shard_map/convert_element_type | solution.py:87
  52.6 33.3 %all-to-all-done.1 = bf16[32,20,2880]{2,1,0:T(8,128)(2,1)} async-done(((bf16[32,20,2880]{2,1,0:T(8,128)(2,1)}), bf16[32,20,2880]{2,1,0:T(8,128)(2,1)}, u32[]{:S(2)}, u32[]{:S(2)}) %all-to-all-start.1) | async-done | bytes 3686432 | tf_op jit(solution)/shard_map/all_to_all | solution.py:90
  85.9 5.0 %all-to-all-start = ((bf16[32,20,2880]{2,1,0:T(8,128)(2,1)}), bf16[32,20,2880]{2,1,0:T(8,128)(2,1)}, u32[]{:S(2)}, u32[]{:S(2)}) async-start(bf16[32,20,2880]{2,1,0:T(8,128)(2,1)} %multiply_convert_fusion), calls=%async_computation | async-start | bytes 9043968 | tf_op jit(solution)/shard_map/all_to_all | solution.py:91
  91.0 6.3 %reshape.143 = bf16[640,2880]{1,0:T(8,128)(2,1)} reshape(bf16[32,20,2880]{2,1,0:T(8,128)(2,1)} %all-to-all-done.1) | data formatting | bytes 7372800 | tf_op jit(solution)/shard_map/reshape | solution.py:37
  97.3 20.0 %fusion.2 = f32[640,2880]{0,1:T(8,128)} fusion(bf16[640,2880]{1,0:T(8,128)(2,1)} %reshape.143, bf16[1,1,2880,2880]{3,2,1,0:T(8,128)(2,1)} %param.12), kind=kOutput, calls=%fused_computation.7 | convolution fusion | flops 10616832000 | bytes 27648000 | tf_op jit(solution)/shard_map/dot_general | solution.py:17
  117.3 31.0 %all-to-all-done = bf16[32,20,2880]{2,1,0:T(8,128)(2,1)} async-done(((bf16[32,20,2880]{2,1,0:T(8,128)(2,1)}), bf16[32,20,2880]{2,1,0:T(8,128)(2,1)}, u32[]{:S(2)}, u32[]{:S(2)}) %all-to-all-start) | async-done | bytes 3686432 | tf_op jit(solution)/shard_map/all_to_all | solution.py:91
  148.3 6.5 %reshape.141 = bf16[640,2880]{1,0:T(8,128)(2,1)} reshape(bf16[32,20,2880]{2,1,0:T(8,128)(2,1)} %all-to-all-done) | data formatting | bytes 7372800 | tf_op jit(solution)/shard_map/reshape | solution.py:38
  154.8 13.2 %fusion.11 = (bf16[640,1440]{0,1:T(8,128)(2,1)S(1)}, bf16[640,1440]{0,1:T(8,128)(2,1)S(1)}) fusion(f32[640,2880]{0,1:T(8,128)} %fusion.2, bf16[640,2880]{1,0:T(8,128)(2,1)} %reshape.141, bf16[1,1,1440,2880]{3,2,1,0:T(8,128)(2,1)} %param.13), kind=kOutput, calls=%fused_computation.16 | convolution fusion | flops 5322240000 | bytes 23040000 | tf_op jit(solution)/shard_map/dot_general | solution.py:18
  168.0 15.7 %fusion.6 = bf16[640,2880]{0,1:T(8,128)(2,1)} fusion(bf16[1,1,2880,2880]{3,2,1,0:T(8,128)(2,1)S(1)} %bitcast.61, bf16[640,1440]{0,1:T(8,128)(2,1)S(1)} %get-tuple-element.6, bf16[640,1440]{0,1:T(8,128)(2,1)S(1)} %get-tuple-element.5), kind=kOutput, calls=%fused_computation.12 | convolution fusion | flops 10626048000 | bytes 23961600 | tf_op jit(solution)/shard_map/dot_general | solution.py:28
  183.8 6.2 %copy.31 = bf16[640,2880]{1,0:T(8,128)(2,1)} copy(bf16[640,2880]{0,1:T(8,128)(2,1)} %fusion.6) | data formatting | bytes 7372800 | tf_op jit(solution)/shard_map/convert_element_type | solution.py:31
  190.0 6.5 %reshape.144 = bf16[32,20,2880]{2,1,0:T(8,128)(2,1)} reshape(bf16[640,2880]{1,0:T(8,128)(2,1)} %copy.31) | data formatting | bytes 7372800 | tf_op jit(solution)/shard_map/reshape | solution.py:42
  196.5 5.1 %all-to-all-start.2 = ((bf16[32,20,2880]{2,1,0:T(8,128)(2,1)}), bf16[32,20,2880]{2,1,0:T(8,128)(2,1)}, u32[]{:S(2)}, u32[]{:S(2)}) async-start(bf16[32,20,2880]{2,1,0:T(8,128)(2,1)} %reshape.144), calls=%async_computation.2 | async-start | bytes 9043968 | tf_op jit(solution)/shard_map/all_to_all | solution.py:46
  201.6 57.2 %all-to-all-done.2 = bf16[32,20,2880]{2,1,0:T(8,128)(2,1)} async-done(((bf16[32,20,2880]{2,1,0:T(8,128)(2,1)}), bf16[32,20,2880]{2,1,0:T(8,128)(2,1)}, u32[]{:S(2)}, u32[]{:S(2)}) %all-to-all-start.2) | async-done | bytes 3686432 | tf_op jit(solution)/shard_map/all_to_all | solution.py:46
  258.8 6.5 %reshape.145 = bf16[640,2880]{1,0:T(8,128)(2,1)} reshape(bf16[32,20,2880]{2,1,0:T(8,128)(2,1)} %all-to-all-done.2) | data formatting | bytes 7372800 | tf_op jit(solution)/shard_map/reshape | solution.py:93
  265.3 9.3 %gather_fusion.3 = bf16[512,2880]{1,0:T(8,128)(2,1)} fusion(bf16[640,2880]{1,0:T(8,128)(2,1)} %reshape.145, s32[1024]{0:T(1024)S(1)} %pad_clamp_fusion), kind=kCustom, calls=%fused_computation.3 | custom fusion | bytes 5900288 | tf_op jit(solution)/shard_map/gather | solution.py:93
  274.6 6.5 %reshape.147 = f32[128,4,2880]{2,1,0:T(4,128)} reshape(bf16[512,2880]{1,0:T(8,128)(2,1)} %gather_fusion.3) | data formatting | bytes 8847360 | tf_op jit(solution)/shard_map/convert_element_type | solution.py:93
  281.1 6.3 %reduce_sum.43 = f32[128,2880]{1,0:T(8,128)S(1)} reduce(f32[128,4,2880]{2,1,0:T(4,128)} %reshape.147, f32[]{:T(128)} %constant.17.clone.1), dimensions={1}, to_apply=%region_5.6 | reduce | flops 1105920 | bytes 7372804 | tf_op jit(solution)/shard_map/reduce_sum | solution.py:94
  287.8 1.4 fusion.26
  289.3 1.5 copy.32
  290.8 0.9 collective-permute-start
  291.6 15.1 %collective-permute-done = bf16[1,128,2880]{1,2,0:T(8,128)(2,1)S(1)} collective-permute-done((bf16[1,128,2880]{1,2,0:T(8,128)(2,1)S(1)}, bf16[1,128,2880]{1,2,0:T(8,128)(2,1)S(1)}, u32[]{:S(2)}, u32[]{:S(2)}) %collective-permute-start) | collective-permute-done | bytes 737312 | tf_op jit(solution)/shard_map/ppermute | solution.py:13
  306.7 0.9 copy.36
  (43 shorter events, 4.0 us)
Async XLA Ops:
  19.9 8.6 %copy-start = (bf16[1,128,2880]{1,2,0:T(8,128)(2,1)S(1)}, bf16[1,128,2880]{1,2,0:T(8,128)(2,1)}, u32[]{:S(2)}) copy-start(bf16[1,128,2880]{1,2,0:T(8,128)(2,1)} %param.9) | copy-start | bytes 2211844
  19.9 66.1 %all-to-all-start.1 = ((bf16[32,20,2880]{2,1,0:T(8,128)(2,1)}), bf16[32,20,2880]{2,1,0:T(8,128)(2,1)}, u32[]{:S(2)}, u32[]{:S(2)}) async-start(bf16[32,20,2880]{2,1,0:T(8,128)(2,1)} %reshape.142), calls=%async_computation.1 | async-start | bytes 9043968 | tf_op jit(solution)/shard_map/all_to_all | solution.py:90
  34.5 8.3 %copy-start.1 = (f32[1,128,4]{1,2,0:T(4,128)S(1)}, f32[1,128,4]{1,2,0:T(4,128)}, u32[]{:S(2)}) copy-start(f32[1,128,4]{1,2,0:T(4,128)} %param.11) | copy-start | bytes 6148
  85.9 62.3 %all-to-all-start = ((bf16[32,20,2880]{2,1,0:T(8,128)(2,1)}), bf16[32,20,2880]{2,1,0:T(8,128)(2,1)}, u32[]{:S(2)}, u32[]{:S(2)}) async-start(bf16[32,20,2880]{2,1,0:T(8,128)(2,1)} %multiply_convert_fusion), calls=%async_computation | async-start | bytes 9043968 | tf_op jit(solution)/shard_map/all_to_all | solution.py:91
  148.3 19.7 %slice-start = ((s8[16957440]{0:T(1024)(128)(4,1)}), s8[180224]{0:T(1024)(128)(4,1)S(1)}, s32[]{:S(2)}) async-start(s8[16957440]{0:T(1024)(128)(4,1)} %bitcast.60), calls=%async_computation.3 | async-start | bytes 360448
  154.8 13.2 %slice-start.1 = ((s8[16957440]{0:T(1024)(128)(4,1)}), s8[4194304]{0:T(1024)(128)(4,1)S(1)}, s32[]{:S(2)}) async-start(s8[16957440]{0:T(1024)(128)(4,1)} %bitcast.60), calls=%async_computation.4 | async-start | bytes 8388608
  154.8 13.2 %slice-start.2 = ((s8[16957440]{0:T(1024)(128)(4,1)}), s8[4194304]{0:T(1024)(128)(4,1)S(1)}, s32[]{:S(2)}) async-start(s8[16957440]{0:T(1024)(128)(4,1)} %bitcast.60), calls=%async_computation.5 | async-start | bytes 8388608
  154.8 13.2 %slice-start.3 = ((s8[16957440]{0:T(1024)(128)(4,1)}), s8[4194304]{0:T(1024)(128)(4,1)S(1)}, s32[]{:S(2)}) async-start(s8[16957440]{0:T(1024)(128)(4,1)} %bitcast.60), calls=%async_computation.6 | async-start | bytes 8388608
  154.8 13.2 %slice-start.4 = ((s8[16957440]{0:T(1024)(128)(4,1)}), s8[4194304]{0:T(1024)(128)(4,1)S(1)}, s32[]{:S(2)}) async-start(s8[16957440]{0:T(1024)(128)(4,1)} %bitcast.60), calls=%async_computation.7 | async-start | bytes 8388608
  196.5 62.3 %all-to-all-start.2 = ((bf16[32,20,2880]{2,1,0:T(8,128)(2,1)}), bf16[32,20,2880]{2,1,0:T(8,128)(2,1)}, u32[]{:S(2)}, u32[]{:S(2)}) async-start(bf16[32,20,2880]{2,1,0:T(8,128)(2,1)} %reshape.144), calls=%async_computation.2 | async-start | bytes 9043968 | tf_op jit(solution)/shard_map/all_to_all | solution.py:46
  290.8 16.0 %collective-permute-start = (bf16[1,128,2880]{1,2,0:T(8,128)(2,1)S(1)}, bf16[1,128,2880]{1,2,0:T(8,128)(2,1)S(1)}, u32[]{:S(2)}, u32[]{:S(2)}) collective-permute-start(bf16[1,128,2880]{1,2,0:T(8,128)(2,1)S(1)} %copy.32), channel_id=1, source_target_pairs={{0,96},{32,0},{64,32},{96,64},{1,97},{33,1},{65,33},{97,65},{2,98}... | collective-permute-start | bytes 2211848 | tf_op jit(solution)/shard_map/ppermute | solution.py:13
where the time goes:
time: 310 us; the launch traced here: 308 us
  waiting for transfers between devices  137 us (44%)
  local copies, waits for them, and re-layouts  84.1 us (27%)
  matrix products  48.9 us (16%)
  starting transfers between devices  19.6 us (6%)
  other arithmetic  18.2 us (6%)
    all_to_all x1, waiting for transfers between devices, send_back(): lax.all_to_all(slab, 'expert', split_axis=0, concat_axis=0, tiled=True)  57.2 us
    all_to_all x1, waiting for transfers between devices, per_device(): lax.all_to_all(inputs_slab, 'expert', split_axis=0, concat_axis=0, tiled=...  33.3 us
    all_to_all x1, waiting for transfers between devices, per_device(): lax.all_to_all(grads_slab, 'expert', split_axis=0, concat_axis=0, tiled=T...  31 us
    dot_general x1, matrix products, expert_backward(): preact = jnp.dot(rows_in, gate_up, preferred_element_type=jnp.float32)  20 us
    dot_general x1, matrix products, expert_backward(): lax.dot_general(dpre, gate_up, (((1,), (1,)), ((), ())), preferred_elemen...  15.7 us
    ppermute x1, waiting for transfers between devices, shifted(): return lax.ppermute(value, axis, pairs)  15.1 us
    gather x2, local copies, waits for them, and re-layouts, per_device(): grad_pad[token_of]  13.9 us
    dot_general x1, matrix products, expert_backward(): lax.dot_general(grad_rows, down_proj, (((1,), (1,)), ((), ())), preferred...  13.2 us
  transfers between devices with their start and end apart: 4, of which 4 were waited for; matrix products, arithmetic and copies ran while one was open for 16% of the time, Pallas kernels for 0%

commit v1 on v0

--- a/solution.py
+++ b/solution.py
@@ -5,6 +5,7 @@
 
 glu_alpha = 1.702
 norm_eps = 1e-05
+ROW_TILE = 8
 
 
 def shifted(value, axis, steps):
@@ -31,18 +32,7 @@
     return result.astype(jnp.bfloat16)
 
 
-def slab_backward(inputs_slab, grads_slab, gate_up, down_proj):
-    sources, slot_count, feat_width = inputs_slab.shape
-    flat_out = expert_backward(
-        inputs_slab.reshape(sources * slot_count, feat_width),
-        grads_slab.reshape(sources * slot_count, feat_width),
-        gate_up,
-        down_proj,
-    )
-    return flat_out.reshape(sources, slot_count, feat_width)
-
-
-def send_back(slab):
+def exchange(slab):
     return lax.all_to_all(slab, "expert", split_axis=0, concat_axis=0, tiled=True)
 
 
@@ -54,17 +44,19 @@
     weights = route_weights[0]
     gate_up = w_gate_up[0, 0]
     down_proj = w_down[0, 0]
-    tok_count = tokens.shape[0]
-    feat_width = tokens.shape[1]
+    tok_count, feat_width = tokens.shape
     top_count = routes.shape[1]
     experts = lax.axis_size("expert")
-    capacity = max(2, tok_count * top_count * 5 // (4 * experts))
+    bound = max(2, tok_count * top_count * 5 // (4 * experts))
+    capacity = -(-bound // ROW_TILE) * ROW_TILE
+
     input_single_precision = tokens.astype(jnp.float32)
     inverse_root_mean = lax.rsqrt(
         jnp.mean(input_single_precision * input_single_precision, axis=-1, keepdims=True) + norm_eps
     )
     normalized_input = input_single_precision * inverse_root_mean
     rescaled_input = (normalized_input * gain_vector_row[None, :]).astype(jnp.bfloat16)
+
     flat_ids = routes.reshape(-1)
     assign = flat_ids.shape[0]
     one_hot = (flat_ids[:, None] == jnp.arange(experts, dtype=jnp.int32)[None, :]).astype(jnp.int32)
@@ -77,21 +69,24 @@
     )
     token_of = source_of // top_count
     normed_pad = jnp.concatenate([rescaled_input, jnp.zeros((1, feat_width), jnp.bfloat16)], axis=0)
-    grad_pad = jnp.concatenate(
-        [incoming_gradient.astype(jnp.float32), jnp.zeros((1, feat_width), jnp.float32)], axis=0
-    )
+    grad_pad = jnp.concatenate([incoming_gradient, jnp.zeros((1, feat_width), jnp.bfloat16)], axis=0)
     weight_pad = jnp.concatenate([weights.reshape(-1), jnp.zeros((1,), jnp.float32)])
     inputs_slab = normed_pad[token_of].reshape(experts, capacity, feat_width)
     grads_slab = (
-        (weight_pad[source_of][:, None] * grad_pad[token_of])
+        (weight_pad[source_of][:, None] * grad_pad[token_of].astype(jnp.float32))
         .astype(jnp.bfloat16)
         .reshape(experts, capacity, feat_width)
     )
-    arrived_inputs = lax.all_to_all(inputs_slab, "expert", split_axis=0, concat_axis=0, tiled=True)
-    arrived_grads = lax.all_to_all(grads_slab, "expert", split_axis=0, concat_axis=0, tiled=True)
-    returned = send_back(slab_backward(arrived_inputs, arrived_grads, gate_up, down_proj))
-    gathered = returned.reshape(experts * capacity, feat_width)[slot_index].astype(jnp.float32)
-    dnorm = jnp.sum(gathered.reshape(tok_count, top_count, feat_width), axis=1)
+    arrived_inputs = exchange(inputs_slab).reshape(experts * capacity, feat_width)
+    arrived_grads = exchange(grads_slab).reshape(experts * capacity, feat_width)
+    computed = expert_backward(arrived_inputs, arrived_grads, gate_up, down_proj)
+    returned = exchange(computed.reshape(experts, capacity, feat_width)).reshape(
+        experts * capacity, feat_width
+    )
+    slots_by_token = slot_index.reshape(tok_count, top_count)
+    dnorm = returned[slots_by_token[:, 0]].astype(jnp.float32)
+    for k in range(1, top_count):
+        dnorm = dnorm + returned[slots_by_token[:, k]].astype(jnp.float32)
     normalized_input_gradient = dnorm * gain_vector_row[None, :]
     projected_rows = jnp.mean(normalized_input_gradient * normalized_input, axis=-1, keepdims=True)
     section_gradient = (

time: 310 us -> 288 us (0.929)
  local copies, waits for them, and re-layouts: 84.1 us -> 48.4 us
  waiting for transfers between devices: 137 us -> 151 us
  other arithmetic: 18.2 us -> 13.7 us
  matrix products: 48.9 us -> 53.2 us
    reshape x5 -> x0, local copies, waits for them, and re-layouts: 32.4 us -> none  [the longest x1 6.55 us: slab_backward(): grads_slab.reshape(sources * slot_count, feat_width)]
    all_to_all x3, waiting for transfers between devices: 121 us -> 136 us  [exchange(): lax.all_to_all(slab, 'expert', split_axis=0, concat_axis=0, tiled=True)]
    convert_element_type x1 -> x0, local copies, waits for them, and re-layouts: 6.54 us -> none  [per_device(): returned.reshape(experts * capacity, feat_width)[slot_index]]
    reduce_sum x1 -> x0, other arithmetic: 6.3 us -> none  [per_device(): dnorm = jnp.sum(gathered.reshape(tok_count, top_count, feat_width), axis=1)]
    gather x4 -> x6, local copies, waits for them, and re-layouts: 26 us -> 28.4 us  [the longest x3 14.9 us: per_device(): dnorm = dnorm + returned[slots_by_token[:, k]].astype(jnp.float32)]
  transfers between devices with their start and end apart: 4 -> 4, of which waited for: 4 -> 4; matrix products, arithmetic and copies ran while one was open for 16% -> 13% of each run, Pallas kernels for 0% -> 0%
where the time goes in v1:
time: 288 us; the launch traced here: 286 us
  waiting for transfers between devices  151 us (52%)
  matrix products  53.2 us (18%)
  local copies, waits for them, and re-layouts  48.4 us (17%)
  starting transfers between devices  19.6 us (7%)
  other arithmetic  13.7 us (5%)
    all_to_all x3, waiting for transfers between devices, exchange(): lax.all_to_all(slab, 'expert', split_axis=0, concat_axis=0, tiled=True)  136 us
    dot_general x1, matrix products, expert_backward(): preact = jnp.dot(rows_in, gate_up, preferred_element_type=jnp.float32)  21.4 us
    all_to_all x3, starting transfers between devices, exchange(): lax.all_to_all(slab, 'expert', split_axis=0, concat_axis=0, tiled=True)  18.7 us
    dot_general x1, matrix products, expert_backward(): lax.dot_general(dpre, gate_up, (((1,), (1,)), ((), ())), preferred_elemen...  17.9 us
    ppermute x1, waiting for transfers between devices, shifted(): return lax.ppermute(value, axis, pairs)  15.1 us
    gather x3, local copies, waits for them, and re-layouts, per_device(): dnorm = dnorm + returned[slots_by_token[:, k]].astype(jnp.float32)  14.9 us
    dot_general x1, matrix products, expert_backward(): lax.dot_general(grad_rows, down_proj, (((1,), (1,)), ((), ())), preferred...  13.9 us
    convert_element_type x1, local copies, waits for them, and re-layouts, expert_backward(): return result.astype(jnp.bfloat16)  6.59 us
  transfers between devices with their start and end apart: 4, of which 4 were waited for; matrix products, arithmetic and copies ran while one was open for 13% of the time, Pallas kernels for 0%

profile of v1, /device:TPU:6, one launch (start us, length us, event | category | flops | bytes accessed | tf_op | source)
XLA Modules:
  0.0 285.8 jit_solution(15305563027179867207)
XLA Ops:
  0.0 0.8 copy.36
  1.0 1.2 reduce-window.6
  2.7 2.4 scatter_custom_fusion
  5.2 1.5 copy.34
  6.6 0.2 fusion.22
  6.9 0.7 reduce.1
  7.6 0.2 fusion.20
  8.0 4.9 %gather_fusion.2 = bf16[768,2880]{1,0:T(8,128)(2,1)} fusion(bf16[129,2880]{1,0:T(8,128)(2,1)S(1)} %concatenate.15, s32[1024]{0:T(1024)S(1)} %get-tuple-element.13), kind=kCustom, calls=%fused_computation.2 | custom fusion | bytes 8850432 | tf_op jit(solution)/shard_map/gather | solution.py:74
  12.8 8.6 %all-to-all-start.1 = ((bf16[32,24,2880]{2,1,0:T(8,128)(2,1)}), bf16[32,24,2880]{2,1,0:T(8,128)(2,1)}, u32[]{:S(2)}, u32[]{:S(2)}) async-start(bf16[32,24,2880]{2,1,0:T(8,128)(2,1)} %bitcast.67), calls=%async_computation.1 | async-start | bytes 9043968 | tf_op jit(solution)/shard_map/all_to_all | solution.py:36
  21.7 3.2 %gather_fusion = f32[768]{0:T(1024)S(1)} fusion(f32[513]{0:T(1024)S(1)} %pad_maximum_fusion, s32[1024]{0:T(1024)S(1)} %get-tuple-element.14), kind=kCustom, calls=%fused_computation | custom fusion | bytes 9216 | tf_op jit(solution)/shard_map/gather | solution.py:76
  25.0 0.4 copy.33
  25.4 4.8 %gather_fusion.1 = bf16[768,2880]{1,0:T(8,128)(2,1)} fusion(bf16[129,2880]{1,0:T(8,128)(2,1)S(1)} %concatenate.14, s32[1024]{0:T(1024)S(1)} %get-tuple-element.13), kind=kCustom, calls=%fused_computation.1 | custom fusion | bytes 8850432 | tf_op jit(solution)/shard_map/gather | solution.py:76
  30.2 5.7 %fusion.4 = bf16[32,24,2880]{2,1,0:T(8,128)(2,1)} fusion(bf16[32,24,2880]{2,1,0:T(8,128)(2,1)} %bitcast.68, f32[32,24]{1,0:T(8,128)S(1)} %mul.124), kind=kLoop, calls=%fused_computation.13 | loop fusion | flops 6635520 | bytes 8850432 | tf_op jit(solution)/shard_map/convert_element_type | solution.py:77
  36.0 42.9 %all-to-all-done.1 = bf16[32,24,2880]{2,1,0:T(8,128)(2,1)} async-done(((bf16[32,24,2880]{2,1,0:T(8,128)(2,1)}), bf16[32,24,2880]{2,1,0:T(8,128)(2,1)}, u32[]{:S(2)}, u32[]{:S(2)}) %all-to-all-start.1) | async-done | bytes 4423712 | tf_op jit(solution)/shard_map/all_to_all | solution.py:36
  78.9 5.0 %all-to-all-start = ((bf16[32,24,2880]{2,1,0:T(8,128)(2,1)}), bf16[32,24,2880]{2,1,0:T(8,128)(2,1)}, u32[]{:S(2)}, u32[]{:S(2)}) async-start(bf16[32,24,2880]{2,1,0:T(8,128)(2,1)} %fusion.4), calls=%async_computation | async-start | bytes 9043968 | tf_op jit(solution)/shard_map/all_to_all | solution.py:36
  83.9 21.4 %fusion.2 = f32[768,2880]{0,1:T(8,128)} fusion(bf16[768,2880]{1,0:T(8,128)(2,1)} %bitcast.9, bf16[1,1,2880,2880]{3,2,1,0:T(8,128)(2,1)} %param.12), kind=kOutput, calls=%fused_computation.10 | convolution fusion | flops 12740198400 | bytes 29859840 | tf_op jit(solution)/shard_map/dot_general | solution.py:18
  105.3 35.9 %all-to-all-done = bf16[32,24,2880]{2,1,0:T(8,128)(2,1)} async-done(((bf16[32,24,2880]{2,1,0:T(8,128)(2,1)}), bf16[32,24,2880]{2,1,0:T(8,128)(2,1)}, u32[]{:S(2)}, u32[]{:S(2)}) %all-to-all-start) | async-done | bytes 4423712 | tf_op jit(solution)/shard_map/all_to_all | solution.py:36
  141.2 13.9 %fusion.12 = (bf16[768,1440]{0,1:T(8,128)(2,1)S(1)}, bf16[768,1440]{0,1:T(8,128)(2,1)S(1)}) fusion(f32[768,2880]{0,1:T(8,128)} %fusion.2, bf16[768,2880]{1,0:T(8,128)(2,1)} %bitcast.6, bf16[1,1,1440,2880]{3,2,1,0:T(8,128)(2,1)} %param.13), kind=kOutput, calls=%fused_computation.20 | convolution fusion | flops 6386688000 | bytes 25989120 | tf_op jit(solution)/shard_map/dot_general | solution.py:19
  155.1 17.9 %fusion.7 = bf16[768,2880]{0,1:T(8,128)(2,1)} fusion(bf16[1,1,2880,2880]{3,2,1,0:T(8,128)(2,1)} %param.12, bf16[768,1440]{0,1:T(8,128)(2,1)S(1)} %get-tuple-element.10, bf16[768,1440]{0,1:T(8,128)(2,1)S(1)} %get-tuple-element.9), kind=kOutput, calls=%fused_computation.16 | convolution fusion | flops 12751257600 | bytes 25436160 | tf_op jit(solution)/shard_map/dot_general | solution.py:29
  173.1 6.6 %copy.41 = bf16[768,2880]{1,0:T(8,128)(2,1)} copy(bf16[768,2880]{0,1:T(8,128)(2,1)} %fusion.7) | data formatting | bytes 8847360 | tf_op jit(solution)/shard_map/convert_element_type | solution.py:32
  179.6 5.1 %all-to-all-start.2 = ((bf16[32,24,2880]{2,1,0:T(8,128)(2,1)}), bf16[32,24,2880]{2,1,0:T(8,128)(2,1)}, u32[]{:S(2)}, u32[]{:S(2)}) async-start(bf16[32,24,2880]{2,1,0:T(8,128)(2,1)} %bitcast.66), calls=%async_computation.2 | async-start | bytes 9043968 | tf_op jit(solution)/shard_map/all_to_all | solution.py:36
  185.1 56.9 %all-to-all-done.2 = bf16[32,24,2880]{2,1,0:T(8,128)(2,1)} async-done(((bf16[32,24,2880]{2,1,0:T(8,128)(2,1)}), bf16[32,24,2880]{2,1,0:T(8,128)(2,1)}, u32[]{:S(2)}, u32[]{:S(2)}) %all-to-all-start.2) | async-done | bytes 4423712 | tf_op jit(solution)/shard_map/all_to_all | solution.py:36
  242.0 4.7 %gather_fusion.6 = bf16[128,2880]{1,0:T(8,128)(2,1)S(1)} fusion(bf16[768,2880]{1,0:T(8,128)(2,1)} %bitcast.12, s32[1024]{0:T(1024)S(1)} %get-tuple-element.15), kind=kCustom, calls=%fused_computation.6 | custom fusion | bytes 1475072 | tf_op jit(solution)/shard_map/gather | solution.py:89
  246.7 4.7 %gather_fusion.5 = bf16[128,2880]{1,0:T(8,128)(2,1)S(1)} fusion(bf16[768,2880]{1,0:T(8,128)(2,1)} %bitcast.12, s32[1024]{0:T(1024)S(1)} %get-tuple-element.16), kind=kCustom, calls=%fused_computation.5 | custom fusion | bytes 1475072 | tf_op jit(solution)/shard_map/gather | solution.py:89
  251.3 5.5 %gather_fusion.4 = bf16[128,2880]{1,0:T(8,128)(2,1)} fusion(bf16[768,2880]{1,0:T(8,128)(2,1)} %bitcast.12, s32[1024]{0:T(1024)S(1)} %get-tuple-element.17), kind=kCustom, calls=%fused_computation.4 | custom fusion | bytes 1475072 | tf_op jit(solution)/shard_map/gather | solution.py:89
  256.9 5.5 %gather_fusion.3 = bf16[128,2880]{1,0:T(8,128)(2,1)} fusion(bf16[768,2880]{1,0:T(8,128)(2,1)} %bitcast.12, s32[1024]{0:T(1024)S(1)} %get-tuple-element.18), kind=kCustom, calls=%fused_computation.3 | custom fusion | bytes 1475072 | tf_op jit(solution)/shard_map/gather | solution.py:87
  262.4 2.0 fusion.21
  264.4 3.0 %fusion.27 = bf16[1,128,2880]{2,1,0:T(8,128)(2,1)} fusion(bf16[1,128,2880]{2,1,0:T(8,128)(2,1)S(1)} %copy.34, bf16[1,128,2880]{2,1,0:T(8,128)(2,1)S(1)} %copy.33, f32[128]{0:T(128)S(1)} %broadcast_multiply_fusion.1, f32[2880]{0:T(1024)S(1)} %reduce.1, f32[128]{0:T(128)S(1)} %add_rsqrt_fusion, bf16[128,2880]{1,0:T(8,128)(2,1)S(1)} %gather_fusion.6, ...), kind=kLoop, calls=%fused_computation.40 | loop fusion | flops 5898240 | bytes 5173504 | tf_op jit(solution)/shard_map/convert_element_type | solution.py:95
  267.5 1.5 copy.42
  269.0 0.9 collective-permute-start
  269.8 15.1 %collective-permute-done = bf16[1,128,2880]{1,2,0:T(8,128)(2,1)S(1)} collective-permute-done((bf16[1,128,2880]{1,2,0:T(8,128)(2,1)S(1)}, bf16[1,128,2880]{1,2,0:T(8,128)(2,1)S(1)}, u32[]{:S(2)}, u32[]{:S(2)}) %collective-permute-start) | collective-permute-done | bytes 737312 | tf_op jit(solution)/shard_map/ppermute | solution.py:14
  284.9 0.9 copy.46
  (30 shorter events, 1.5 us)
Async XLA Ops:
  12.8 8.6 %copy-start.1 = (f32[1,128,4]{1,2,0:T(4,128)S(1)}, f32[1,128,4]{1,2,0:T(4,128)}, u32[]{:S(2)}) copy-start(f32[1,128,4]{1,2,0:T(4,128)} %param.11) | copy-start | bytes 6148
  12.8 66.1 %all-to-all-start.1 = ((bf16[32,24,2880]{2,1,0:T(8,128)(2,1)}), bf16[32,24,2880]{2,1,0:T(8,128)(2,1)}, u32[]{:S(2)}, u32[]{:S(2)}) async-start(bf16[32,24,2880]{2,1,0:T(8,128)(2,1)} %bitcast.67), calls=%async_computation.1 | async-start | bytes 9043968 | tf_op jit(solution)/shard_map/all_to_all | solution.py:36
  21.4 3.5 %copy-start = (bf16[1,128,2880]{1,2,0:T(8,128)(2,1)S(1)}, bf16[1,128,2880]{1,2,0:T(8,128)(2,1)}, u32[]{:S(2)}) copy-start(bf16[1,128,2880]{1,2,0:T(8,128)(2,1)} %param.9) | copy-start | bytes 2211844
  78.9 62.3 %all-to-all-start = ((bf16[32,24,2880]{2,1,0:T(8,128)(2,1)}), bf16[32,24,2880]{2,1,0:T(8,128)(2,1)}, u32[]{:S(2)}, u32[]{:S(2)}) async-start(bf16[32,24,2880]{2,1,0:T(8,128)(2,1)} %fusion.4), calls=%async_computation | async-start | bytes 9043968 | tf_op jit(solution)/shard_map/all_to_all | solution.py:36
  179.6 62.3 %all-to-all-start.2 = ((bf16[32,24,2880]{2,1,0:T(8,128)(2,1)}), bf16[32,24,2880]{2,1,0:T(8,128)(2,1)}, u32[]{:S(2)}, u32[]{:S(2)}) async-start(bf16[32,24,2880]{2,1,0:T(8,128)(2,1)} %bitcast.66), calls=%async_computation.2 | async-start | bytes 9043968 | tf_op jit(solution)/shard_map/all_to_all | solution.py:36
  269.0 16.0 %collective-permute-start = (bf16[1,128,2880]{1,2,0:T(8,128)(2,1)S(1)}, bf16[1,128,2880]{1,2,0:T(8,128)(2,1)S(1)}, u32[]{:S(2)}, u32[]{:S(2)}) collective-permute-start(bf16[1,128,2880]{1,2,0:T(8,128)(2,1)S(1)} %copy.42), channel_id=1, source_target_pairs={{0,96},{32,0},{64,32},{96,64},{1,97},{33,1},{65,33},{97,65},{2,98}... | collective-permute-start | bytes 2211848 | tf_op jit(solution)/shard_map/ppermute | solution.py:14

commit v2 on v1

--- a/solution.py
+++ b/solution.py
@@ -1,6 +1,7 @@
 import jax
 import jax.numpy as jnp
 from jax import lax
+from jax.experimental.layout import Layout, with_layout_constraint
 from jax.sharding import PartitionSpec as P
 
 glu_alpha = 1.702
@@ -26,10 +27,14 @@
     dgate = dact * (up_part + 1.0) * (sig + glu_alpha * gate * sig * (1.0 - sig))
     dup = dact * gate * sig
     dpre = jnp.concatenate([dgate, dup], axis=1).astype(jnp.bfloat16)
-    result = lax.dot_general(
-        dpre, gate_up, (((1,), (1,)), ((), ())), preferred_element_type=jnp.float32
+    result_t = lax.dot_general(
+        gate_up, dpre, (((1,), (1,)), ((), ())), preferred_element_type=jnp.float32
     )
-    return result.astype(jnp.bfloat16)
+    return row_major(result_t.astype(jnp.bfloat16).T)
+
+
+def row_major(value):
+    return with_layout_constraint(value, Layout(tuple(range(value.ndim))))
 
 
 def exchange(slab):
@@ -58,35 +63,36 @@
     rescaled_input = (normalized_input * gain_vector_row[None, :]).astype(jnp.bfloat16)
 
     flat_ids = routes.reshape(-1)
-    assign = flat_ids.shape[0]
     one_hot = (flat_ids[:, None] == jnp.arange(experts, dtype=jnp.int32)[None, :]).astype(jnp.int32)
     slot_rank = jnp.sum((jnp.cumsum(one_hot, axis=0) - one_hot) * one_hot, axis=1)
-    slot_index = flat_ids * capacity + slot_rank
-    source_of = (
-        jnp.full((experts * capacity,), assign, jnp.int32)
-        .at[slot_index]
-        .set(jnp.arange(assign, dtype=jnp.int32))
+    slot_index = (flat_ids * capacity + slot_rank).reshape(tok_count, top_count)
+    slot_ids = jnp.arange(experts * capacity, dtype=jnp.int32)
+    hits = slot_index[:, :, None] == slot_ids[None, None, :]
+    placement = jnp.any(hits, axis=1)
+    slot_weight = jnp.sum(jnp.where(hits, weights[:, :, None], 0.0), axis=(0, 1))
+    placement_bf16 = placement.astype(jnp.bfloat16)
+    pick = (((0,), (0,)), ((), ()))
+    inputs_slab = lax.dot_general(
+        rescaled_input, placement_bf16, pick, preferred_element_type=jnp.float32
+    ).astype(jnp.bfloat16).T
+    inputs_slab = row_major(inputs_slab)
+    grads_slab = (
+        lax.dot_general(incoming_gradient, placement_bf16, pick, preferred_element_type=jnp.float32)
+        * slot_weight[None, :]
+    ).astype(jnp.bfloat16).T
+    grads_slab = row_major(grads_slab)
+    arrived_inputs = exchange(inputs_slab.reshape(experts, capacity, feat_width))
+    arrived_grads = exchange(grads_slab.reshape(experts, capacity, feat_width))
+    computed = expert_backward(
+        arrived_inputs.reshape(experts * capacity, feat_width),
+        arrived_grads.reshape(experts * capacity, feat_width),
+        gate_up,
+        down_proj,
     )
-    token_of = source_of // top_count
-    normed_pad = jnp.concatenate([rescaled_input, jnp.zeros((1, feat_width), jnp.bfloat16)], axis=0)
-    grad_pad = jnp.concatenate([incoming_gradient, jnp.zeros((1, feat_width), jnp.bfloat16)], axis=0)
-    weight_pad = jnp.concatenate([weights.reshape(-1), jnp.zeros((1,), jnp.float32)])
-    inputs_slab = normed_pad[token_of].reshape(experts, capacity, feat_width)
-    grads_slab = (
-        (weight_pad[source_of][:, None] * grad_pad[token_of].astype(jnp.float32))
-        .astype(jnp.bfloat16)
-        .reshape(experts, capacity, feat_width)
-    )
-    arrived_inputs = exchange(inputs_slab).reshape(experts * capacity, feat_width)
-    arrived_grads = exchange(grads_slab).reshape(experts * capacity, feat_width)
-    computed = expert_backward(arrived_inputs, arrived_grads, gate_up, down_proj)
     returned = exchange(computed.reshape(experts, capacity, feat_width)).reshape(
         experts * capacity, feat_width
     )
-    slots_by_token = slot_index.reshape(tok_count, top_count)
-    dnorm = returned[slots_by_token[:, 0]].astype(jnp.float32)
-    for k in range(1, top_count):
-        dnorm = dnorm + returned[slots_by_token[:, k]].astype(jnp.float32)
+    dnorm = jnp.dot(placement_bf16, returned, preferred_element_type=jnp.float32)
     normalized_input_gradient = dnorm * gain_vector_row[None, :]
     projected_rows = jnp.mean(normalized_input_gradient * normalized_input, axis=-1, keepdims=True)
     section_gradient = (

time: 288 us -> 252 us (0.88)
  blocking collectives: 0 us -> 57.7 us
  local copies, waits for them, and re-layouts: 48.4 us -> 2.27 us
  waiting for transfers between devices: 151 us -> 109 us
  matrix products: 53.2 us -> 63.8 us
  other arithmetic: 13.7 us -> 4.51 us
  starting transfers between devices: 19.6 us -> 14.5 us
    all_to_all x0 -> x1, blocking collectives: none -> 57.7 us  [exchange(): lax.all_to_all(slab, 'expert', split_axis=0, concat_axis=0, tiled=True)]
    all_to_all x3 -> x2, waiting for transfers between devices: 136 us -> 89.6 us  [exchange(): lax.all_to_all(slab, 'expert', split_axis=0, concat_axis=0, tiled=True)]
    gather x7 -> x0, local copies, waits for them, and re-layouts: 33.3 us -> none  [the longest x3 14.9 us: per_device(): dnorm = dnorm + returned[slots_by_token[:, k]].astype(jnp.float32)]
    dot_general x1 -> x4, matrix products: 17.9 us -> 28.6 us  [the longest x1 18.4 us: expert_backward(): lax.dot_general(gate_up, dpre, (((1,), (1,)), ((), ())), preferred_elemen...]
    convert_element_type x3 -> x0, other arithmetic: 9.02 us -> none  [the longest x1 5.73 us: per_device(): grads_slab = (weight_pad[source_of][:, None] * grad_pad[token_of].astype(...]
    convert_element_type x2 -> x0, local copies, waits for them, and re-layouts: 8.08 us -> none  [the longest x1 6.59 us: expert_backward(): return result.astype(jnp.bfloat16)]
    all_to_all x3 -> x2, starting transfers between devices: 18.7 us -> 13.6 us  [exchange(): lax.all_to_all(slab, 'expert', split_axis=0, concat_axis=0, tiled=True)]
    ppermute x1, waiting for transfers between devices: 15.1 us -> 19.1 us  [shifted(): return lax.ppermute(value, axis, pairs)]
  transfers between devices with their start and end apart: 4 -> 3, of which waited for: 4 -> 3; matrix products, arithmetic and copies ran while one was open for 13% -> 10% of each run, Pallas kernels for 0% -> 0%
where the time goes in v2:
time: 252 us
  waiting for transfers between devices  109 us (43%)
  matrix products  63.8 us (25%)
  blocking collectives  57.7 us (23%)
  starting transfers between devices  14.5 us (6%)
  other arithmetic  4.51 us (2%)
    all_to_all x2, waiting for transfers between devices, exchange(): lax.all_to_all(slab, 'expert', split_axis=0, concat_axis=0, tiled=True)  89.6 us
    all_to_all x1, blocking collectives, exchange(): lax.all_to_all(slab, 'expert', split_axis=0, concat_axis=0, tiled=True)  57.7 us
    dot_general x1, matrix products, expert_backward(): preact = jnp.dot(rows_in, gate_up, preferred_element_type=jnp.float32)  21.4 us
    ppermute x1, waiting for transfers between devices, shifted(): return lax.ppermute(value, axis, pairs)  19.1 us
    dot_general x1, matrix products, expert_backward(): lax.dot_general(gate_up, dpre, (((1,), (1,)), ((), ())), preferred_elemen...  18.4 us
    dot_general x1, matrix products, expert_backward(): lax.dot_general(grad_rows, down_proj, (((1,), (1,)), ((), ())), preferred...  13.9 us
    all_to_all x2, starting transfers between devices, exchange(): lax.all_to_all(slab, 'expert', split_axis=0, concat_axis=0, tiled=True)  13.6 us
  transfers between devices with their start and end apart: 3, of which 3 were waited for; matrix products, arithmetic and copies ran while one was open for 10% of the time, Pallas kernels for 0%

profile of v2, /device:TPU:6, one launch (start us, length us, event | category | flops | bytes accessed | tf_op | source)
XLA Modules:
  0.0 251.6 jit_solution(17496771945261743160)
XLA Ops:
  0.0 0.8 copy.15
  0.8 0.1 eq.42
  0.9 0.1 eq.38
  1.0 1.5 fusion.25
  2.5 1.2 reduce-window.6
  3.7 0.2 slice_reduce_fusion
  4.0 0.1 fusion.36
  4.1 0.1 reduce_sum.40
  4.2 0.1 copy.19
  4.3 0.3 fusion.18
  4.6 0.7 reduce.1
  5.3 4.6 %convolution_convert_fusion = bf16[768,2880]{1,0:T(8,128)(2,1)} fusion(bf16[1,128,2880]{1,2,0:T(8,128)(2,1)} %param.7, f32[2880]{0:T(1024)S(1)} %reduce.1, f32[128]{0:T(128)S(1)} %add_rsqrt_fusion, pred[128,768]{1,0:T(8,128)(4,1)S(1)} %fusion.18), kind=kOutput, calls=%fused_computation.8 | convolution fusion | flops 570015744 | bytes 5271296 | tf_op jit(solution)/shard_map/dot_general | solution.py:75
  9.9 0.0 copy-start.1
  9.9 8.6 %all-to-all-start.1 = ((bf16[32,24,2880]{2,1,0:T(8,128)(2,1)}), bf16[32,24,2880]{2,1,0:T(8,128)(2,1)}, u32[]{:S(2)}, u32[]{:S(2)}) async-start(bf16[32,24,2880]{2,1,0:T(8,128)(2,1)} %bitcast.60), calls=%async_computation.1 | async-start | bytes 9043968 | tf_op jit(solution)/shard_map/all_to_all | solution.py:41
  18.5 0.0 copy-done.2
  18.5 0.2 select_reduce_fusion
  18.8 0.0 copy-done.1
  18.8 3.6 %multiply_convert_fusion = bf16[768,2880]{1,0:T(8,128)(2,1)} fusion(f32[768]{0:T(1024)S(1)} %select_reduce_fusion, bf16[1,128,2880]{1,2,0:T(8,128)(2,1)S(1)} %copy-done.1, pred[128,768]{1,0:T(8,128)(4,1)S(1)} %fusion.18), kind=kOutput, calls=%fused_computation.4 | convolution fusion | flops 570753024 | bytes 5262336 | tf_op jit(solution)/shard_map/dot_general | solution.py:80
  22.4 53.7 %all-to-all-done.1 = bf16[32,24,2880]{2,1,0:T(8,128)(2,1)} async-done(((bf16[32,24,2880]{2,1,0:T(8,128)(2,1)}), bf16[32,24,2880]{2,1,0:T(8,128)(2,1)}, u32[]{:S(2)}, u32[]{:S(2)}) %all-to-all-start.1) | async-done | bytes 4423712 | tf_op jit(solution)/shard_map/all_to_all | solution.py:41
  76.0 5.0 %all-to-all-start = ((bf16[32,24,2880]{2,1,0:T(8,128)(2,1)}), bf16[32,24,2880]{2,1,0:T(8,128)(2,1)}, u32[]{:S(2)}, u32[]{:S(2)}) async-start(bf16[32,24,2880]{2,1,0:T(8,128)(2,1)} %bitcast.59), calls=%async_computation | async-start | bytes 9043968 | tf_op jit(solution)/shard_map/all_to_all | solution.py:41
  81.1 21.4 %fusion.2 = f32[768,2880]{0,1:T(8,128)} fusion(bf16[768,2880]{1,0:T(8,128)(2,1)} %bitcast.10, bf16[1,1,2880,2880]{3,2,1,0:T(8,128)(2,1)} %param.12), kind=kOutput, calls=%fused_computation.2 | convolution fusion | flops 12740198400 | bytes 29859840 | tf_op jit(solution)/shard_map/dot_general | solution.py:19
  102.4 35.9 %all-to-all-done = bf16[32,24,2880]{2,1,0:T(8,128)(2,1)} async-done(((bf16[32,24,2880]{2,1,0:T(8,128)(2,1)}), bf16[32,24,2880]{2,1,0:T(8,128)(2,1)}, u32[]{:S(2)}, u32[]{:S(2)}) %all-to-all-start) | async-done | bytes 4423712 | tf_op jit(solution)/shard_map/all_to_all | solution.py:41
  138.3 13.9 %fusion.11 = (bf16[768,1440]{0,1:T(8,128)(2,1)S(1)}, bf16[768,1440]{0,1:T(8,128)(2,1)S(1)}) fusion(f32[768,2880]{0,1:T(8,128)} %fusion.2, bf16[768,2880]{1,0:T(8,128)(2,1)} %bitcast.6, bf16[1,1,1440,2880]{3,2,1,0:T(8,128)(2,1)} %param.13), kind=kOutput, calls=%fused_computation.12 | convolution fusion | flops 6386688000 | bytes 25989120 | tf_op jit(solution)/shard_map/dot_general | solution.py:20
  152.3 18.4 %fusion.6 = bf16[768,2880]{1,0:T(8,128)(2,1)S(1)} fusion(bf16[1,1,2880,2880]{3,2,1,0:T(8,128)(2,1)} %param.12, bf16[768,1440]{0,1:T(8,128)(2,1)S(1)} %get-tuple-element.6, bf16[768,1440]{0,1:T(8,128)(2,1)S(1)} %get-tuple-element.5), kind=kOutput, calls=%fused_computation.7 | convolution fusion | flops 12751257600 | bytes 25436160 | tf_op jit(solution)/shard_map/dot_general | solution.py:30
  170.6 0.0 copy-start
  170.7 57.7 %all_to_all.15 = bf16[32,24,2880]{2,1,0:T(8,128)(2,1)S(1)} all-to-all(bf16[32,24,2880]{2,1,0:T(8,128)(2,1)S(1)} %bitcast.62), channel_id=1, replica_groups=mesh['section'=4,'expert'=32] {'expert'}, dimensions={0} | all-to-all | bytes 8847360 | tf_op jit(solution)/shard_map/all_to_all | solution.py:41
  228.3 0.0 copy-done
  228.3 2.0 fusion.20
  230.4 0.4 fusion.26
  230.8 0.9 collective-permute-start
  231.7 19.1 %collective-permute-done = bf16[1,128,2880]{1,2,0:T(8,128)(2,1)S(1)} collective-permute-done((bf16[1,128,2880]{1,2,0:T(8,128)(2,1)S(1)}, bf16[1,128,2880]{1,2,0:T(8,128)(2,1)S(1)}, u32[]{:S(2)}, u32[]{:S(2)}) %collective-permute-start) | collective-permute-done | bytes 737312 | tf_op jit(solution)/shard_map/ppermute | solution.py:15
  250.7 0.9 copy.23
  (7 shorter events, 0.1 us)
Async XLA Ops:
  9.9 8.6 %copy-start.2 = (f32[1,128,4]{1,2,0:T(4,128)S(1)}, f32[1,128,4]{1,2,0:T(4,128)}, u32[]{:S(2)}) copy-start(f32[1,128,4]{1,2,0:T(4,128)} %param.11) | copy-start | bytes 6148
  9.9 8.8 %copy-start.1 = (bf16[1,128,2880]{1,2,0:T(8,128)(2,1)S(1)}, bf16[1,128,2880]{1,2,0:T(8,128)(2,1)}, u32[]{:S(2)}) copy-start(bf16[1,128,2880]{1,2,0:T(8,128)(2,1)} %param.9) | copy-start | bytes 2211844
  9.9 66.1 %all-to-all-start.1 = ((bf16[32,24,2880]{2,1,0:T(8,128)(2,1)}), bf16[32,24,2880]{2,1,0:T(8,128)(2,1)}, u32[]{:S(2)}, u32[]{:S(2)}) async-start(bf16[32,24,2880]{2,1,0:T(8,128)(2,1)} %bitcast.60), calls=%async_computation.1 | async-start | bytes 9043968 | tf_op jit(solution)/shard_map/all_to_all | solution.py:41
  76.0 62.3 %all-to-all-start = ((bf16[32,24,2880]{2,1,0:T(8,128)(2,1)}), bf16[32,24,2880]{2,1,0:T(8,128)(2,1)}, u32[]{:S(2)}, u32[]{:S(2)}) async-start(bf16[32,24,2880]{2,1,0:T(8,128)(2,1)} %bitcast.59), calls=%async_computation | async-start | bytes 9043968 | tf_op jit(solution)/shard_map/all_to_all | solution.py:41
  170.6 57.7 %copy-start = (bf16[1,128,2880]{1,2,0:T(8,128)(2,1)S(1)}, bf16[1,128,2880]{1,2,0:T(8,128)(2,1)}, u32[]{:S(2)}) copy-start(bf16[1,128,2880]{1,2,0:T(8,128)(2,1)} %param.7) | copy-start | bytes 2211844
  230.8 20.0 %collective-permute-start = (bf16[1,128,2880]{1,2,0:T(8,128)(2,1)S(1)}, bf16[1,128,2880]{1,2,0:T(8,128)(2,1)S(1)}, u32[]{:S(2)}, u32[]{:S(2)}) collective-permute-start(bf16[1,128,2880]{1,2,0:T(8,128)(2,1)S(1)} %fusion.26), channel_id=1, source_target_pairs={{0,96},{32,0},{64,32},{96,64},{1,97},{33,1},{65,33},{97,65},{2,98}... | collective-permute-start | bytes 2211848 | tf_op jit(solution)/shard_map/ppermute | solution.py:15

commit v3 on v2

--- a/solution.py
+++ b/solution.py
@@ -7,6 +7,7 @@
 glu_alpha = 1.702
 norm_eps = 1e-05
 ROW_TILE = 8
+LANES = 128
 
 
 def shifted(value, axis, steps):
@@ -37,8 +38,12 @@
     return with_layout_constraint(value, Layout(tuple(range(value.ndim))))
 
 
-def exchange(slab):
-    return lax.all_to_all(slab, "expert", split_axis=0, concat_axis=0, tiled=True)
+def exchange(rows, groups):
+    width = rows.shape[1]
+    per_group = rows.shape[0] // groups
+    dense = rows.reshape(groups, per_group * width // LANES, LANES)
+    moved = lax.all_to_all(dense, "expert", split_axis=0, concat_axis=0, tiled=True)
+    return moved.reshape(groups * per_group, width)
 
 
 def per_device(hidden_in, norm_gain, out_grad, expert_ids, route_weights, w_gate_up, w_down):
@@ -53,7 +58,7 @@
     top_count = routes.shape[1]
     experts = lax.axis_size("expert")
     bound = max(2, tok_count * top_count * 5 // (4 * experts))
-    capacity = -(-bound // ROW_TILE) * ROW_TILE
+    capacity = bound
 
     input_single_precision = tokens.astype(jnp.float32)
     inverse_root_mean = lax.rsqrt(
@@ -81,17 +86,10 @@
         * slot_weight[None, :]
     ).astype(jnp.bfloat16).T
     grads_slab = row_major(grads_slab)
-    arrived_inputs = exchange(inputs_slab.reshape(experts, capacity, feat_width))
-    arrived_grads = exchange(grads_slab.reshape(experts, capacity, feat_width))
-    computed = expert_backward(
-        arrived_inputs.reshape(experts * capacity, feat_width),
-        arrived_grads.reshape(experts * capacity, feat_width),
-        gate_up,
-        down_proj,
-    )
-    returned = exchange(computed.reshape(experts, capacity, feat_width)).reshape(
-        experts * capacity, feat_width
-    )
+    arrived_inputs = exchange(inputs_slab, experts)
+    arrived_grads = exchange(grads_slab, experts)
+    computed = expert_backward(arrived_inputs, arrived_grads, gate_up, down_proj)
+    returned = exchange(computed, experts)
     dnorm = jnp.dot(placement_bf16, returned, preferred_element_type=jnp.float32)
     normalized_input_gradient = dnorm * gain_vector_row[None, :]
     projected_rows = jnp.mean(normalized_input_gradient * normalized_input, axis=-1, keepdims=True)

time: 252 us -> 258 us (1.024)
  local copies, waits for them, and re-layouts: 2.27 us -> 46.3 us
  waiting for transfers between devices: 109 us -> 77.4 us
  blocking collectives: 57.7 us -> 51 us
    reshape x0 -> x6, local copies, waits for them, and re-layouts: none -> 44.1 us  [the longest x3 23.7 us: exchange(): dense = rows.reshape(groups, per_group * width // LANES, LANES)]
    all_to_all x2, waiting for transfers between devices: 89.6 us -> 58.6 us  [exchange(): lax.all_to_all(dense, 'expert', split_axis=0, concat_axis=0, tiled=True)]
    all_to_all x1, blocking collectives: 57.7 us -> 51 us  [exchange(): lax.all_to_all(dense, 'expert', split_axis=0, concat_axis=0, tiled=True)]
  transfers between devices with their start and end apart: 3 -> 3, of which waited for: 3 -> 3; matrix products, arithmetic and copies ran while one was open for 10% -> 15% of each run, Pallas kernels for 0% -> 0%
where the time goes in v3:
time: 258 us; the launch traced here: 257 us
  waiting for transfers between devices  77.4 us (30%)
  matrix products  63.1 us (24%)
  blocking collectives  51 us (20%)
  local copies, waits for them, and re-layouts  46.3 us (18%)
  starting transfers between devices  14.5 us (6%)
  other arithmetic  4.47 us (2%)
    all_to_all x2, waiting for transfers between devices, exchange(): lax.all_to_all(dense, 'expert', split_axis=0, concat_axis=0, tiled=True)  58.6 us
    all_to_all x1, blocking collectives, exchange(): lax.all_to_all(dense, 'expert', split_axis=0, concat_axis=0, tiled=True)  51 us
    reshape x3, local copies, waits for them, and re-layouts, exchange(): dense = rows.reshape(groups, per_group * width // LANES, LANES)  23.7 us
    reshape x3, local copies, waits for them, and re-layouts, exchange(): return moved.reshape(groups * per_group, width)  20.4 us
    dot_general x1, matrix products, expert_backward(): preact = jnp.dot(rows_in, gate_up, preferred_element_type=jnp.float32)  19.9 us
    ppermute x1, waiting for transfers between devices, shifted(): return lax.ppermute(value, axis, pairs)  18.8 us
    dot_general x1, matrix products, expert_backward(): lax.dot_general(gate_up, dpre, (((1,), (1,)), ((), ())), preferred_elemen...  18 us
    dot_general x1, matrix products, expert_backward(): lax.dot_general(grad_rows, down_proj, (((1,), (1,)), ((), ())), preferred...  13.9 us
  transfers between devices with their start and end apart: 3, of which 3 were waited for; matrix products, arithmetic and copies ran while one was open for 15% of the time, Pallas kernels for 0%

profile of v3, /device:TPU:6, one launch (start us, length us, event | category | flops | bytes accessed | tf_op | source)
XLA Modules:
  0.0 256.9 jit_solution(17128347360432936072)
XLA Ops:
  0.0 0.8 copy.15
  0.8 0.1 eq.38
  0.9 0.1 eq.42
  1.0 1.5 fusion.24
  2.5 1.2 reduce-window.6
  3.7 0.2 slice_reduce_fusion
  4.0 0.1 fusion.36
  4.1 0.1 reduce_sum.40
  4.3 0.3 fusion.25
  4.5 0.7 reduce.1
  5.3 4.4 %convolution_convert_fusion = bf16[640,2880]{1,0:T(8,128)(2,1)} fusion(bf16[1,128,2880]{1,2,0:T(8,128)(2,1)} %param.7, f32[2880]{0:T(1024)S(1)} %reduce.1, f32[128]{0:T(128)S(1)} %add_rsqrt_fusion, pred[128,640]{1,0:T(8,128)(4,1)S(1)} %fusion.25), kind=kOutput, calls=%fused_computation.7 | convolution fusion | flops 475258880 | bytes 4517632 | tf_op jit(solution)/shard_map/dot_general | solution.py:80
  9.7 7.9 %reshape.66 = bf16[32,450,128]{2,1,0:T(8,128)(2,1)} reshape(bf16[640,2880]{1,0:T(8,128)(2,1)} %convolution_convert_fusion) | data formatting | bytes 7372800 | tf_op jit(solution)/shard_map/reshape | solution.py:44
  17.6 8.6 %all-to-all-start.1 = ((bf16[32,450,128]{2,1,0:T(8,128)(2,1)}), bf16[32,450,128]{2,1,0:T(8,128)(2,1)}, u32[]{:S(2)}, u32[]{:S(2)}) async-start(bf16[32,450,128]{2,1,0:T(8,128)(2,1)} %reshape.66), calls=%async_computation.1 | async-start | bytes 7471104 | tf_op jit(solution)/shard_map/all_to_all | solution.py:45
  26.2 0.2 select_reduce_fusion
  26.4 3.2 %multiply_convert_fusion = bf16[640,2880]{1,0:T(8,128)(2,1)} fusion(f32[640]{0:T(1024)S(1)} %select_reduce_fusion, bf16[1,128,2880]{1,2,0:T(8,128)(2,1)S(1)} %copy-done.1, pred[128,640]{1,0:T(8,128)(4,1)S(1)} %fusion.25), kind=kOutput, calls=%fused_computation.6 | convolution fusion | flops 475627520 | bytes 4508160 | tf_op jit(solution)/shard_map/dot_general | solution.py:85
  29.6 7.9 %reshape.64 = bf16[32,450,128]{2,1,0:T(8,128)(2,1)} reshape(bf16[640,2880]{1,0:T(8,128)(2,1)} %multiply_convert_fusion) | data formatting | bytes 7372800 | tf_op jit(solution)/shard_map/reshape | solution.py:44
  37.5 37.1 %all-to-all-done.1 = bf16[32,450,128]{2,1,0:T(8,128)(2,1)} async-done(((bf16[32,450,128]{2,1,0:T(8,128)(2,1)}), bf16[32,450,128]{2,1,0:T(8,128)(2,1)}, u32[]{:S(2)}, u32[]{:S(2)}) %all-to-all-start.1) | async-done | bytes 3686432 | tf_op jit(solution)/shard_map/all_to_all | solution.py:45
  74.6 5.0 %all-to-all-start = ((bf16[32,450,128]{2,1,0:T(8,128)(2,1)}), bf16[32,450,128]{2,1,0:T(8,128)(2,1)}, u32[]{:S(2)}, u32[]{:S(2)}) async-start(bf16[32,450,128]{2,1,0:T(8,128)(2,1)} %reshape.64), calls=%async_computation | async-start | bytes 7471104 | tf_op jit(solution)/shard_map/all_to_all | solution.py:45
  79.6 6.8 %reshape.67 = bf16[640,2880]{1,0:T(8,128)(2,1)} reshape(bf16[32,450,128]{2,1,0:T(8,128)(2,1)} %all-to-all-done.1) | data formatting | bytes 7372800 | tf_op jit(solution)/shard_map/reshape | solution.py:46
  86.4 19.9 %fusion.2 = f32[640,2880]{0,1:T(8,128)} fusion(bf16[640,2880]{1,0:T(8,128)(2,1)} %reshape.67, bf16[1,1,2880,2880]{3,2,1,0:T(8,128)(2,1)} %param.12), kind=kOutput, calls=%fused_computation.2 | convolution fusion | flops 10616832000 | bytes 27648000 | tf_op jit(solution)/shard_map/dot_general | solution.py:20
  106.3 21.5 %all-to-all-done = bf16[32,450,128]{2,1,0:T(8,128)(2,1)} async-done(((bf16[32,450,128]{2,1,0:T(8,128)(2,1)}), bf16[32,450,128]{2,1,0:T(8,128)(2,1)}, u32[]{:S(2)}, u32[]{:S(2)}) %all-to-all-start) | async-done | bytes 3686432 | tf_op jit(solution)/shard_map/all_to_all | solution.py:45
  127.8 6.8 %reshape.65 = bf16[640,2880]{1,0:T(8,128)(2,1)} reshape(bf16[32,450,128]{2,1,0:T(8,128)(2,1)} %all-to-all-done) | data formatting | bytes 7372800 | tf_op jit(solution)/shard_map/reshape | solution.py:46
  134.6 13.9 %fusion.11 = (bf16[640,1440]{0,1:T(8,128)(2,1)S(1)}, bf16[640,1440]{0,1:T(8,128)(2,1)}) fusion(f32[640,2880]{0,1:T(8,128)} %fusion.2, bf16[640,2880]{1,0:T(8,128)(2,1)} %reshape.65, bf16[1,1,1440,2880]{3,2,1,0:T(8,128)(2,1)} %param.13), kind=kOutput, calls=%fused_computation.13 | convolution fusion | flops 5322240000 | bytes 23040000 | tf_op jit(solution)/shard_map/dot_general | solution.py:21
  148.5 18.0 %fusion.6 = bf16[640,2880]{1,0:T(8,128)(2,1)} fusion(bf16[1,1,2880,2880]{3,2,1,0:T(8,128)(2,1)} %param.12, bf16[640,1440]{0,1:T(8,128)(2,1)} %get-tuple-element.6, bf16[640,1440]{0,1:T(8,128)(2,1)S(1)} %get-tuple-element.5), kind=kOutput, calls=%fused_computation.8 | convolution fusion | flops 10626048000 | bytes 23961600 | tf_op jit(solution)/shard_map/dot_general | solution.py:31
  166.6 7.9 %reshape.68 = bf16[32,450,128]{2,1,0:T(8,128)(2,1)} reshape(bf16[640,2880]{1,0:T(8,128)(2,1)} %fusion.6) | data formatting | bytes 7372800 | tf_op jit(solution)/shard_map/reshape | solution.py:44
  174.5 51.0 %all_to_all.15 = bf16[32,450,128]{2,1,0:T(8,128)(2,1)} all-to-all(bf16[32,450,128]{2,1,0:T(8,128)(2,1)} %reshape.68), channel_id=1, replica_groups=mesh['section'=4,'expert'=32] {'expert'}, dimensions={0} | all-to-all | bytes 7372800 | tf_op jit(solution)/shard_map/all_to_all | solution.py:45
  225.5 6.8 %reshape.69 = bf16[640,2880]{1,0:T(8,128)(2,1)} reshape(bf16[32,450,128]{2,1,0:T(8,128)(2,1)} %all_to_all.15) | data formatting | bytes 7372800 | tf_op jit(solution)/shard_map/reshape | solution.py:46
  232.3 3.7 %fusion.19 = (f32[128]{0:T(128)S(1)}, f32[128,2880]{0,1:T(8,128)S(1)}) fusion(bf16[1,128,2880]{1,2,0:T(8,128)(2,1)S(1)} %copy-done, f32[128]{0:T(128)S(1)} %add_rsqrt_fusion, f32[2880]{0:T(1024)S(1)} %reduce.1, pred[128,640]{1,0:T(8,128)(4,1)S(1)} %fusion.25, bf16[640,2880]{1,0:T(8,128)(2,1)} %reshape.69), kind=kOutput, calls=%fused_computation.26 | convolution fusion | flops 473702272 | bytes 5992704 | tf_op jit(solution)/shard_map/dot_general | solution.py:93
  236.0 0.4 fusion.26
  236.4 0.9 collective-permute-start
  237.3 18.8 %collective-permute-done = bf16[1,128,2880]{1,2,0:T(8,128)(2,1)S(1)} collective-permute-done((bf16[1,128,2880]{1,2,0:T(8,128)(2,1)S(1)}, bf16[1,128,2880]{1,2,0:T(8,128)(2,1)S(1)}, u32[]{:S(2)}, u32[]{:S(2)}) %collective-permute-start) | collective-permute-done | bytes 737312 | tf_op jit(solution)/shard_map/ppermute | solution.py:16
  256.1 0.9 copy.23
  (13 shorter events, 0.1 us)
Async XLA Ops:
  17.6 8.6 %copy-start.2 = (f32[1,128,4]{1,2,0:T(4,128)S(1)}, f32[1,128,4]{1,2,0:T(4,128)}, u32[]{:S(2)}) copy-start(f32[1,128,4]{1,2,0:T(4,128)} %param.11) | copy-start | bytes 6148
  17.6 8.8 %copy-start.1 = (bf16[1,128,2880]{1,2,0:T(8,128)(2,1)S(1)}, bf16[1,128,2880]{1,2,0:T(8,128)(2,1)}, u32[]{:S(2)}) copy-start(bf16[1,128,2880]{1,2,0:T(8,128)(2,1)} %param.9) | copy-start | bytes 2211844
  17.6 57.0 %all-to-all-start.1 = ((bf16[32,450,128]{2,1,0:T(8,128)(2,1)}), bf16[32,450,128]{2,1,0:T(8,128)(2,1)}, u32[]{:S(2)}, u32[]{:S(2)}) async-start(bf16[32,450,128]{2,1,0:T(8,128)(2,1)} %reshape.66), calls=%async_computation.1 | async-start | bytes 7471104 | tf_op jit(solution)/shard_map/all_to_all | solution.py:45
  74.6 53.3 %all-to-all-start = ((bf16[32,450,128]{2,1,0:T(8,128)(2,1)}), bf16[32,450,128]{2,1,0:T(8,128)(2,1)}, u32[]{:S(2)}, u32[]{:S(2)}) async-start(bf16[32,450,128]{2,1,0:T(8,128)(2,1)} %reshape.64), calls=%async_computation | async-start | bytes 7471104 | tf_op jit(solution)/shard_map/all_to_all | solution.py:45
  225.5 6.8 %copy-start = (bf16[1,128,2880]{1,2,0:T(8,128)(2,1)S(1)}, bf16[1,128,2880]{1,2,0:T(8,128)(2,1)}, u32[]{:S(2)}) copy-start(bf16[1,128,2880]{1,2,0:T(8,128)(2,1)} %param.7) | copy-start | bytes 2211844
  236.4 19.7 %collective-permute-start = (bf16[1,128,2880]{1,2,0:T(8,128)(2,1)S(1)}, bf16[1,128,2880]{1,2,0:T(8,128)(2,1)S(1)}, u32[]{:S(2)}, u32[]{:S(2)}) collective-permute-start(bf16[1,128,2880]{1,2,0:T(8,128)(2,1)S(1)} %fusion.26), channel_id=1, source_target_pairs={{0,96},{32,0},{64,32},{96,64},{1,97},{33,1},{65,33},{97,65},{2,98}... | collective-permute-start | bytes 2211848 | tf_op jit(solution)/shard_map/ppermute | solution.py:16

commit v4 on v2

--- a/solution.py
+++ b/solution.py
@@ -81,6 +81,7 @@
         * slot_weight[None, :]
     ).astype(jnp.bfloat16).T
     grads_slab = row_major(grads_slab)
+    inputs_slab, grads_slab = lax.optimization_barrier((inputs_slab, grads_slab))
     arrived_inputs = exchange(inputs_slab.reshape(experts, capacity, feat_width))
     arrived_grads = exchange(grads_slab.reshape(experts, capacity, feat_width))
     computed = expert_backward(

time: 252 us -> 251 us (level)
  blocking collectives: 57.7 us -> 120 us
  waiting for transfers between devices: 109 us -> 55 us
  starting transfers between devices: 14.5 us -> 5.95 us
    all_to_all x1 -> x2, blocking collectives: 57.7 us -> 120 us  [exchange(): lax.all_to_all(slab, 'expert', split_axis=0, concat_axis=0, tiled=True)]
    all_to_all x2 -> x1, waiting for transfers between devices: 89.6 us -> 35.9 us  [exchange(): lax.all_to_all(slab, 'expert', split_axis=0, concat_axis=0, tiled=True)]
    all_to_all x2 -> x1, starting transfers between devices: 13.6 us -> 5.05 us  [exchange(): lax.all_to_all(slab, 'expert', split_axis=0, concat_axis=0, tiled=True)]
    dot_general x1, matrix products: 4.62 us -> 1.45 us  [per_device(): lax.dot_general(rescaled_input, placement_bf16, pick, preferred_element_t...]
  transfers between devices with their start and end apart: 3 -> 2, of which waited for: 3 -> 2; matrix products, arithmetic and copies ran while one was open for 10% -> 9% of each run, Pallas kernels for 0% -> 0%
where the time goes in v4:
time: 251 us
  blocking collectives  120 us (48%)
  matrix products  61.9 us (25%)
  waiting for transfers between devices  55 us (22%)
  starting transfers between devices  5.95 us (2%)
  other arithmetic  5.19 us (2%)
    all_to_all x2, blocking collectives, exchange(): lax.all_to_all(slab, 'expert', split_axis=0, concat_axis=0, tiled=True)  120 us
    all_to_all x1, waiting for transfers between devices, exchange(): lax.all_to_all(slab, 'expert', split_axis=0, concat_axis=0, tiled=True)  35.9 us
    dot_general x1, matrix products, expert_backward(): preact = jnp.dot(rows_in, gate_up, preferred_element_type=jnp.float32)  21.4 us
    ppermute x1, waiting for transfers between devices, shifted(): return lax.ppermute(value, axis, pairs)  19.1 us
    dot_general x1, matrix products, expert_backward(): lax.dot_general(gate_up, dpre, (((1,), (1,)), ((), ())), preferred_elemen...  18.4 us
    dot_general x1, matrix products, expert_backward(): lax.dot_general(grad_rows, down_proj, (((1,), (1,)), ((), ())), preferred...  13.9 us
    all_to_all x1, starting transfers between devices, exchange(): lax.all_to_all(slab, 'expert', split_axis=0, concat_axis=0, tiled=True)  5.05 us
  transfers between devices with their start and end apart: 2, of which 2 were waited for; matrix products, arithmetic and copies ran while one was open for 9% of the time, Pallas kernels for 0%

profile of v4, /device:TPU:6, one launch (start us, length us, event | category | flops | bytes accessed | tf_op | source)
XLA Modules:
  0.0 250.7 jit_solution(5429118895277471692)
XLA Ops:
  0.0 0.8 copy.15
  0.8 0.1 eq.42
  0.9 0.1 eq.38
  1.0 1.5 fusion.25
  2.5 1.2 reduce-window.6
  3.7 0.2 slice_reduce_fusion
  4.0 0.1 fusion.36
  4.1 0.1 reduce_sum.40
  4.2 0.0 copy-start
  4.2 0.1 copy.19
  4.3 0.3 fusion.18
  4.6 0.9 select_reduce_fusion
  5.5 0.7 reduce.1
  6.3 4.8 %multiply_convert_fusion = bf16[768,2880]{1,0:T(8,128)(2,1)} fusion(f32[768]{0:T(1024)S(1)} %select_reduce_fusion, bf16[1,128,2880]{1,2,0:T(8,128)(2,1)} %param.9, pred[128,768]{1,0:T(8,128)(4,1)S(1)} %fusion.18), kind=kOutput, calls=%fused_computation.4 | convolution fusion | flops 570753024 | bytes 5262336 | tf_op jit(solution)/shard_map/dot_general | solution.py:80
  11.0 0.0 copy-done
  11.0 1.4 convolution_convert_fusion
  12.5 62.8 %all_to_all.15 = bf16[32,24,2880]{2,1,0:T(8,128)(2,1)} all-to-all(bf16[32,24,2880]{2,1,0:T(8,128)(2,1)S(1)} %bitcast.61), channel_id=1, replica_groups=mesh['section'=4,'expert'=32] {'expert'}, dimensions={0} | all-to-all | bytes 8847360 | tf_op jit(solution)/shard_map/all_to_all | solution.py:41
  75.3 5.0 %all-to-all-start = ((bf16[32,24,2880]{2,1,0:T(8,128)(2,1)}), bf16[32,24,2880]{2,1,0:T(8,128)(2,1)}, u32[]{:S(2)}, u32[]{:S(2)}) async-start(bf16[32,24,2880]{2,1,0:T(8,128)(2,1)} %bitcast.59), calls=%async_computation | async-start | bytes 9043968 | tf_op jit(solution)/shard_map/all_to_all | solution.py:41
  80.3 21.4 %fusion.2 = f32[768,2880]{0,1:T(8,128)} fusion(bf16[768,2880]{1,0:T(8,128)(2,1)} %bitcast.62, bf16[1,1,2880,2880]{3,2,1,0:T(8,128)(2,1)} %param.12), kind=kOutput, calls=%fused_computation.2 | convolution fusion | flops 12740198400 | bytes 29859840 | tf_op jit(solution)/shard_map/dot_general | solution.py:19
  101.7 35.9 %all-to-all-done = bf16[32,24,2880]{2,1,0:T(8,128)(2,1)} async-done(((bf16[32,24,2880]{2,1,0:T(8,128)(2,1)}), bf16[32,24,2880]{2,1,0:T(8,128)(2,1)}, u32[]{:S(2)}, u32[]{:S(2)}) %all-to-all-start) | async-done | bytes 4423712 | tf_op jit(solution)/shard_map/all_to_all | solution.py:41
  137.6 13.9 %fusion.11 = (bf16[768,1440]{0,1:T(8,128)(2,1)S(1)}, bf16[768,1440]{0,1:T(8,128)(2,1)S(1)}) fusion(f32[768,2880]{0,1:T(8,128)} %fusion.2, bf16[768,2880]{1,0:T(8,128)(2,1)} %bitcast.7, bf16[1,1,1440,2880]{3,2,1,0:T(8,128)(2,1)} %param.13), kind=kOutput, calls=%fused_computation.12 | convolution fusion | flops 6386688000 | bytes 25989120 | tf_op jit(solution)/shard_map/dot_general | solution.py:20
  151.5 18.4 %fusion.6 = bf16[768,2880]{1,0:T(8,128)(2,1)S(1)} fusion(bf16[1,1,2880,2880]{3,2,1,0:T(8,128)(2,1)} %param.12, bf16[768,1440]{0,1:T(8,128)(2,1)S(1)} %get-tuple-element.10, bf16[768,1440]{0,1:T(8,128)(2,1)S(1)} %get-tuple-element.9), kind=kOutput, calls=%fused_computation.7 | convolution fusion | flops 12751257600 | bytes 25436160 | tf_op jit(solution)/shard_map/dot_general | solution.py:30
  169.9 57.6 %all_to_all.16 = bf16[32,24,2880]{2,1,0:T(8,128)(2,1)S(1)} all-to-all(bf16[32,24,2880]{2,1,0:T(8,128)(2,1)S(1)} %bitcast.63), channel_id=1, replica_groups=mesh['section'=4,'expert'=32] {'expert'}, dimensions={0} | all-to-all | bytes 8847360 | tf_op jit(solution)/shard_map/all_to_all | solution.py:41
  227.5 0.0 copy-start.1
  227.5 2.0 fusion.20
  229.5 0.0 copy-done.1
  229.5 0.4 fusion.26
  229.9 0.9 collective-permute-start
  230.8 19.1 %collective-permute-done = bf16[1,128,2880]{1,2,0:T(8,128)(2,1)S(1)} collective-permute-done((bf16[1,128,2880]{1,2,0:T(8,128)(2,1)S(1)}, bf16[1,128,2880]{1,2,0:T(8,128)(2,1)S(1)}, u32[]{:S(2)}, u32[]{:S(2)}) %collective-permute-start) | collective-permute-done | bytes 737312 | tf_op jit(solution)/shard_map/ppermute | solution.py:15
  249.8 0.9 copy.23
  (6 shorter events, 0.1 us)
Async XLA Ops:
  4.2 6.8 %copy-start = (bf16[1,128,2880]{1,2,0:T(8,128)(2,1)S(1)}, bf16[1,128,2880]{1,2,0:T(8,128)(2,1)}, u32[]{:S(2)}) copy-start(bf16[1,128,2880]{1,2,0:T(8,128)(2,1)} %param.7) | copy-start | bytes 2211844
  75.3 62.3 %all-to-all-start = ((bf16[32,24,2880]{2,1,0:T(8,128)(2,1)}), bf16[32,24,2880]{2,1,0:T(8,128)(2,1)}, u32[]{:S(2)}, u32[]{:S(2)}) async-start(bf16[32,24,2880]{2,1,0:T(8,128)(2,1)} %bitcast.59), calls=%async_computation | async-start | bytes 9043968 | tf_op jit(solution)/shard_map/all_to_all | solution.py:41
  227.5 2.0 copy-start.1
  229.9 20.0 %collective-permute-start = (bf16[1,128,2880]{1,2,0:T(8,128)(2,1)S(1)}, bf16[1,128,2880]{1,2,0:T(8,128)(2,1)S(1)}, u32[]{:S(2)}, u32[]{:S(2)}) collective-permute-start(bf16[1,128,2880]{1,2,0:T(8,128)(2,1)S(1)} %fusion.26), channel_id=1, source_target_pairs={{0,96},{32,0},{64,32},{96,64},{1,97},{33,1},{65,33},{97,65},{2,98}... | collective-permute-start | bytes 2211848 | tf_op jit(solution)/shard_map/ppermute | solution.py:15

commit v5 on v4

--- a/solution.py
+++ b/solution.py
@@ -1,5 +1,7 @@
 import jax
 import jax.numpy as jnp
+from jax.experimental import pallas as pl
+from jax.experimental.pallas import tpu as pltpu
 from jax import lax
 from jax.experimental.layout import Layout, with_layout_constraint
 from jax.sharding import PartitionSpec as P
@@ -7,6 +9,7 @@
 glu_alpha = 1.702
 norm_eps = 1e-05
 ROW_TILE = 8
+COL_TILE = 512
 
 
 def shifted(value, axis, steps):
@@ -27,14 +30,37 @@
     dgate = dact * (up_part + 1.0) * (sig + glu_alpha * gate * sig * (1.0 - sig))
     dup = dact * gate * sig
     dpre = jnp.concatenate([dgate, dup], axis=1).astype(jnp.bfloat16)
-    result_t = lax.dot_general(
-        gate_up, dpre, (((1,), (1,)), ((), ())), preferred_element_type=jnp.float32
-    )
-    return row_major(result_t.astype(jnp.bfloat16).T)
+    return nt_matmul(dpre, gate_up)
 
 
 def row_major(value):
     return with_layout_constraint(value, Layout(tuple(range(value.ndim))))
+
+
+def nt_kernel(lhs_ref, rhs_ref, out_ref):
+    out_ref[...] = lax.dot_general(
+        lhs_ref[...], rhs_ref[...], (((1,), (1,)), ((), ())), preferred_element_type=jnp.float32
+    ).astype(out_ref.dtype)
+
+
+def nt_matmul(lhs, rhs):
+    rows, depth = lhs.shape
+    cols = rhs.shape[0]
+    return pl.pallas_call(
+        nt_kernel,
+        grid=(pl.cdiv(cols, COL_TILE),),
+        in_specs=[
+            pl.BlockSpec((rows, depth), lambda j: (0, 0)),
+            pl.BlockSpec((COL_TILE, depth), lambda j: (j, 0)),
+        ],
+        out_specs=pl.BlockSpec((rows, COL_TILE), lambda j: (0, j)),
+        out_shape=jax.ShapeDtypeStruct((rows, cols), jnp.bfloat16),
+        cost_estimate=pl.CostEstimate(
+            flops=2 * rows * cols * depth,
+            bytes_accessed=2 * (rows * depth + cols * depth + rows * cols),
+            transcendentals=0,
+        ),
+    )(lhs, rhs)
 
 
 def exchange(slab):

time: 251 us -> 261 us (1.040)
  Pallas kernels: 0 us -> 20 us
  matrix products: 61.9 us -> 44.9 us
  other arithmetic: 5.19 us -> 10.3 us
    pallas_call x0 -> x1, Pallas kernels: none -> 20 us  [nt_matmul(): pl.pallas_call(nt_kernel, grid=(pl.cdiv(cols, COL_TILE),), in_specs=[pl.B...]
    dot_general x1 -> x0, matrix products: 18.4 us -> none  [expert_backward(): lax.dot_general(gate_up, dpre, (((1,), (1,)), ((), ())), preferred_elemen...]
    concatenate x0 -> x1, other arithmetic: none -> 5.13 us  [expert_backward(): dpre = jnp.concatenate([dgate, dup], axis=1).astype(jnp.bfloat16)]
  transfers between devices with their start and end apart: 2 -> 2, of which waited for: 2 -> 2; matrix products, arithmetic and copies ran while one was open for 9% -> 8% of each run, Pallas kernels for 0% -> 0%
where the time goes in v5:
time: 261 us
  blocking collectives  121 us (46%)
  waiting for transfers between devices  55.6 us (21%)
  matrix products  44.9 us (17%)
  Pallas kernels  20 us (8%)
  other arithmetic  10.3 us (4%)
  starting transfers between devices  5.93 us (2%)
    all_to_all x2, blocking collectives, exchange(): lax.all_to_all(slab, 'expert', split_axis=0, concat_axis=0, tiled=True)  121 us
    all_to_all x1, waiting for transfers between devices, exchange(): lax.all_to_all(slab, 'expert', split_axis=0, concat_axis=0, tiled=True)  36.5 us
    dot_general x1, matrix products, expert_backward(): preact = jnp.dot(rows_in, gate_up, preferred_element_type=jnp.float32)  20.7 us
    pallas_call x1, Pallas kernels, nt_matmul(): pl.pallas_call(nt_kernel, grid=(pl.cdiv(cols, COL_TILE),), in_specs=[pl.B...  20 us
    ppermute x1, waiting for transfers between devices, shifted(): return lax.ppermute(value, axis, pairs)  19.1 us
    dot_general x1, matrix products, expert_backward(): lax.dot_general(grad_rows, down_proj, (((1,), (1,)), ((), ())), preferred...  16.1 us
  transfers between devices with their start and end apart: 2, of which 2 were waited for; matrix products, arithmetic and copies ran while one was open for 8% of the time, Pallas kernels for 0%

profile of v5, /device:TPU:6, one launch (start us, length us, event | category | flops | bytes accessed | tf_op | source)
XLA Modules:
  0.0 260.5 jit_solution(7077580585590269879)
XLA Ops:
  0.0 0.8 copy.23
  0.8 0.1 eq.42
  0.9 0.1 eq.38
  1.0 1.5 fusion.15
  2.5 1.2 reduce-window.6
  3.7 0.0 copy-start
  3.7 0.2 slice_reduce_fusion
  4.0 0.1 fusion.26
  4.1 0.1 reduce_sum.40
  4.2 0.1 copy.27
  4.3 0.3 fusion.8
  4.6 0.9 select_reduce_fusion
  5.5 0.7 reduce.1
  6.2 4.7 %multiply_convert_fusion = bf16[768,2880]{1,0:T(8,128)(2,1)} fusion(f32[768]{0:T(1024)S(1)} %select_reduce_fusion, bf16[1,128,2880]{1,2,0:T(8,128)(2,1)} %param.9, pred[128,768]{1,0:T(8,128)(4,1)S(1)} %fusion.8), kind=kOutput, calls=%fused_computation | convolution fusion | flops 570753024 | bytes 5262336 | tf_op jit(solution)/shard_map/dot_general | solution.py:106
  10.9 0.0 copy-done
  10.9 1.4 convolution_convert_fusion
  12.4 62.8 %all_to_all.15 = bf16[32,24,2880]{2,1,0:T(8,128)(2,1)} all-to-all(bf16[32,24,2880]{2,1,0:T(8,128)(2,1)S(1)} %bitcast.57), channel_id=1, replica_groups=mesh['section'=4,'expert'=32] {'expert'}, dimensions={0} | all-to-all | bytes 8847360 | tf_op jit(solution)/shard_map/all_to_all | solution.py:67
  75.2 5.0 %all-to-all-start = ((bf16[32,24,2880]{2,1,0:T(8,128)(2,1)}), bf16[32,24,2880]{2,1,0:T(8,128)(2,1)}, u32[]{:S(2)}, u32[]{:S(2)}) async-start(bf16[32,24,2880]{2,1,0:T(8,128)(2,1)} %bitcast.55), calls=%async_computation | async-start | bytes 9043968 | tf_op jit(solution)/shard_map/all_to_all | solution.py:67
  80.2 20.7 %fusion.28 = f32[768,2880]{1,0:T(8,128)} fusion(bf16[768,2880]{1,0:T(8,128)(2,1)} %bitcast.58, bf16[1,1,2880,2880]{3,2,1,0:T(8,128)(2,1)} %param.12), kind=kOutput, calls=%fused_computation.47 | convolution fusion | flops 12740198400 | bytes 29859840 | tf_op jit(solution)/shard_map/dot_general | solution.py:22
  101.0 36.5 %all-to-all-done = bf16[32,24,2880]{2,1,0:T(8,128)(2,1)} async-done(((bf16[32,24,2880]{2,1,0:T(8,128)(2,1)}), bf16[32,24,2880]{2,1,0:T(8,128)(2,1)}, u32[]{:S(2)}, u32[]{:S(2)}) %all-to-all-start) | async-done | bytes 4423712 | tf_op jit(solution)/shard_map/all_to_all | solution.py:67
  137.5 16.1 %fusion.4 = (bf16[768,1440]{1,0:T(8,128)(2,1)S(1)}, bf16[768,1440]{1,0:T(8,128)(2,1)}) fusion(f32[768,2880]{1,0:T(8,128)} %fusion.28, bf16[768,2880]{1,0:T(8,128)(2,1)} %bitcast.7, bf16[1,1,1440,2880]{3,2,1,0:T(8,128)(2,1)} %param.13), kind=kOutput, calls=%fused_computation.7 | convolution fusion | flops 6386688000 | bytes 25989120 | tf_op jit(solution)/shard_map/dot_general | solution.py:23
  153.6 5.1 %pad_maximum_fusion.lhs_ref = bf16[768,2880]{1,0:T(8,128)(2,1)} fusion(bf16[768,1440]{1,0:T(8,128)(2,1)} %get-tuple-element.10, bf16[768,1440]{1,0:T(8,128)(2,1)S(1)} %get-tuple-element.9), kind=kLoop, calls=%fused_computation.10 | loop fusion | flops 8847360 | bytes 8847360 | tf_op jit(solution)/shard_map/concatenate | solution.py:32
  158.8 20.0 %shard_map.73 = bf16[768,2880]{1,0:T(8,128)(2,1)} custom-call(bf16[768,2880]{1,0:T(8,128)(2,1)} %pad_maximum_fusion.lhs_ref, bf16[2880,2880]{1,0:T(8,128)(2,1)} %bitcast.61), custom_call_target="tpu_custom_call" | custom-call | flops 12740198400 | bytes 25436160 | tf_op jit(solution)/shard_map/pallas_call | solution.py:49
  178.7 58.6 %all_to_all.16 = bf16[32,24,2880]{2,1,0:T(8,128)(2,1)S(1)} all-to-all(bf16[32,24,2880]{2,1,0:T(8,128)(2,1)} %bitcast.59), channel_id=1, replica_groups=mesh['section'=4,'expert'=32] {'expert'}, dimensions={0} | all-to-all | bytes 8847360 | tf_op jit(solution)/shard_map/all_to_all | solution.py:67
  237.4 0.0 copy-start.1
  237.4 1.9 fusion.10
  239.3 0.0 copy-done.1
  239.3 0.4 fusion.16
  239.7 0.9 collective-permute-start
  240.6 19.1 %collective-permute-done = bf16[1,128,2880]{1,2,0:T(8,128)(2,1)S(1)} collective-permute-done((bf16[1,128,2880]{1,2,0:T(8,128)(2,1)S(1)}, bf16[1,128,2880]{1,2,0:T(8,128)(2,1)S(1)}, u32[]{:S(2)}, u32[]{:S(2)}) %collective-permute-start) | collective-permute-done | bytes 737312 | tf_op jit(solution)/shard_map/ppermute | solution.py:18
  259.7 0.9 copy.37
  (6 shorter events, 0.1 us)
Async XLA Ops:
  3.7 7.2 %copy-start = (bf16[1,128,2880]{1,2,0:T(8,128)(2,1)S(1)}, bf16[1,128,2880]{1,2,0:T(8,128)(2,1)}, u32[]{:S(2)}) copy-start(bf16[1,128,2880]{1,2,0:T(8,128)(2,1)} %param.7) | copy-start | bytes 2211844
  75.2 62.3 %all-to-all-start = ((bf16[32,24,2880]{2,1,0:T(8,128)(2,1)}), bf16[32,24,2880]{2,1,0:T(8,128)(2,1)}, u32[]{:S(2)}, u32[]{:S(2)}) async-start(bf16[32,24,2880]{2,1,0:T(8,128)(2,1)} %bitcast.55), calls=%async_computation | async-start | bytes 9043968 | tf_op jit(solution)/shard_map/all_to_all | solution.py:67
  237.4 1.9 copy-start.1
  239.7 20.0 %collective-permute-start = (bf16[1,128,2880]{1,2,0:T(8,128)(2,1)S(1)}, bf16[1,128,2880]{1,2,0:T(8,128)(2,1)S(1)}, u32[]{:S(2)}, u32[]{:S(2)}) collective-permute-start(bf16[1,128,2880]{1,2,0:T(8,128)(2,1)S(1)} %fusion.16), channel_id=1, source_target_pairs={{0,96},{32,0},{64,32},{96,64},{1,97},{33,1},{65,33},{97,65},{2,98}... | collective-permute-start | bytes 2211848 | tf_op jit(solution)/shard_map/ppermute | solution.py:18

commit v6 on v4

--- a/solution.py
+++ b/solution.py
@@ -38,7 +38,10 @@
 
 
 def exchange(slab):
-    return lax.all_to_all(slab, "expert", split_axis=0, concat_axis=0, tiled=True)
+    groups, slots, width = slab.shape
+    quad = slab.reshape(groups, slots // 4, 4, width)
+    moved = lax.all_to_all(quad, "expert", split_axis=0, concat_axis=0, tiled=True)
+    return moved.reshape(groups, slots, width)
 
 
 def per_device(hidden_in, norm_gain, out_grad, expert_ids, route_weights, w_gate_up, w_down):
@@ -53,7 +56,7 @@
     top_count = routes.shape[1]
     experts = lax.axis_size("expert")
     bound = max(2, tok_count * top_count * 5 // (4 * experts))
-    capacity = -(-bound // ROW_TILE) * ROW_TILE
+    capacity = bound
 
     input_single_precision = tokens.astype(jnp.float32)
     inverse_root_mean = lax.rsqrt(

time: 251 us -> 262 us (1.044)
  blocking collectives: 120 us -> 51.4 us
  local copies, waits for them, and re-layouts: 2.27 us -> 44.8 us
  waiting for transfers between devices: 55 us -> 81.9 us
  starting transfers between devices: 5.95 us -> 14.3 us
    all_to_all x2 -> x1, blocking collectives: 120 us -> 51.4 us  [exchange(): lax.all_to_all(quad, 'expert', split_axis=0, concat_axis=0, tiled=True)]
    another operation x1 -> x7, local copies, waits for them, and re-layouts: 0.01 us -> 42.5 us  [the longest x3 21.7 us: exchange(): quad = slab.reshape(groups, slots // 4, 4, width)]
    all_to_all x1 -> x2, waiting for transfers between devices: 35.9 us -> 63.2 us  [exchange(): lax.all_to_all(quad, 'expert', split_axis=0, concat_axis=0, tiled=True)]
    all_to_all x1 -> x2, starting transfers between devices: 5.05 us -> 13.5 us  [exchange(): lax.all_to_all(quad, 'expert', split_axis=0, concat_axis=0, tiled=True)]
  transfers between devices with their start and end apart: 2 -> 3, of which waited for: 2 -> 3; matrix products, arithmetic and copies ran while one was open for 9% -> 13% of each run, Pallas kernels for 0% -> 0%
where the time goes in v6:
time: 262 us; the launch traced here: 261 us
  waiting for transfers between devices  81.9 us (31%)
  matrix products  63.2 us (24%)
  blocking collectives  51.4 us (20%)
  local copies, waits for them, and re-layouts  44.8 us (17%)
  starting transfers between devices  14.3 us (5%)
  other arithmetic  5.16 us (2%)
    all_to_all x2, waiting for transfers between devices, exchange(): lax.all_to_all(quad, 'expert', split_axis=0, concat_axis=0, tiled=True)  63.2 us
    all_to_all x1, blocking collectives, exchange(): lax.all_to_all(quad, 'expert', split_axis=0, concat_axis=0, tiled=True)  51.4 us
    another operation x3, local copies, waits for them, and re-layouts, exchange(): quad = slab.reshape(groups, slots // 4, 4, width)  21.7 us
    dot_general x1, matrix products, expert_backward(): preact = jnp.dot(rows_in, gate_up, preferred_element_type=jnp.float32)  20 us
    ppermute x1, waiting for transfers between devices, shifted(): return lax.ppermute(value, axis, pairs)  18.7 us
    dot_general x1, matrix products, expert_backward(): lax.dot_general(gate_up, dpre, (((1,), (1,)), ((), ())), preferred_elemen...  18.2 us
    dot_general x1, matrix products, expert_backward(): lax.dot_general(grad_rows, down_proj, (((1,), (1,)), ((), ())), preferred...  13.9 us
    all_to_all x2, starting transfers between devices, exchange(): lax.all_to_all(quad, 'expert', split_axis=0, concat_axis=0, tiled=True)  13.5 us
  transfers between devices with their start and end apart: 3, of which 3 were waited for; matrix products, arithmetic and copies ran while one was open for 13% of the time, Pallas kernels for 0%

profile of v6, /device:TPU:6, one launch (start us, length us, event | category | flops | bytes accessed | tf_op | source)
XLA Modules:
  0.0 261.0 jit_solution(16044634516071230620)
XLA Ops:
  0.0 0.8 copy.15
  0.8 0.1 eq.42
  0.9 0.1 eq.38
  1.0 1.5 fusion.24
  2.5 1.2 reduce-window.6
  3.7 0.2 slice_reduce_fusion
  4.0 0.1 fusion.36
  4.1 0.1 reduce_sum.40
  4.3 0.3 fusion.25
  4.6 0.9 select_reduce_fusion
  5.5 0.7 reduce.1
  6.2 4.3 %multiply_convert_fusion = bf16[640,2880]{1,0:T(8,128)(2,1)} fusion(f32[640]{0:T(1024)S(1)} %select_reduce_fusion, bf16[1,128,2880]{1,2,0:T(8,128)(2,1)} %param.9, pred[128,640]{1,0:T(8,128)(4,1)S(1)} %fusion.25), kind=kOutput, calls=%fused_computation.6 | convolution fusion | flops 475627520 | bytes 4508160 | tf_op jit(solution)/shard_map/dot_general | solution.py:83
  10.5 3.1 %convolution_convert_fusion = bf16[640,2880]{1,0:T(8,128)(2,1)} fusion(bf16[1,128,2880]{1,2,0:T(8,128)(2,1)S(1)} %copy-done, f32[2880]{0:T(1024)S(1)} %reduce.1, f32[128]{0:T(128)S(1)} %add_rsqrt_fusion, pred[128,640]{1,0:T(8,128)(4,1)S(1)} %fusion.25), kind=kOutput, calls=%fused_computation.7 | convolution fusion | flops 475258880 | bytes 4517632 | tf_op jit(solution)/shard_map/dot_general | solution.py:78
  13.6 7.2 %reshape_reshape.20 = bf16[32,5,4,2880]{3,2,1,0:T(4,128)(2,1)} reshape(bf16[640,2880]{1,0:T(8,128)(2,1)} %convolution_convert_fusion) | data formatting | bytes 7372800 | tf_op jit(solution)/shard_map/reshape;reshape | solution.py:42
  20.8 8.4 %all-to-all-start.1 = ((bf16[32,5,4,2880]{3,2,1,0:T(4,128)(2,1)}), bf16[32,5,4,2880]{3,2,1,0:T(4,128)(2,1)}, u32[]{:S(2)}, u32[]{:S(2)}) async-start(bf16[32,5,4,2880]{3,2,1,0:T(4,128)(2,1)} %reshape_reshape.20), calls=%async_computation.1 | async-start | bytes 7536640 | tf_op jit(solution)/shard_map/all_to_all | solution.py:43
  29.3 7.2 %reshape_reshape.18 = bf16[32,5,4,2880]{3,2,1,0:T(4,128)(2,1)} reshape(bf16[640,2880]{1,0:T(8,128)(2,1)} %multiply_convert_fusion) | data formatting | bytes 7372800 | tf_op jit(solution)/shard_map/reshape;reshape | solution.py:42
  36.5 41.5 %all-to-all-done.1 = bf16[32,5,4,2880]{3,2,1,0:T(4,128)(2,1)} async-done(((bf16[32,5,4,2880]{3,2,1,0:T(4,128)(2,1)}), bf16[32,5,4,2880]{3,2,1,0:T(4,128)(2,1)}, u32[]{:S(2)}, u32[]{:S(2)}) %all-to-all-start.1) | async-done | bytes 3686432 | tf_op jit(solution)/shard_map/all_to_all | solution.py:43
  78.1 5.0 %all-to-all-start = ((bf16[32,5,4,2880]{3,2,1,0:T(4,128)(2,1)}), bf16[32,5,4,2880]{3,2,1,0:T(4,128)(2,1)}, u32[]{:S(2)}, u32[]{:S(2)}) async-start(bf16[32,5,4,2880]{3,2,1,0:T(4,128)(2,1)} %reshape_reshape.18), calls=%async_computation | async-start | bytes 7536640 | tf_op jit(solution)/shard_map/all_to_all | solution.py:43
  83.1 6.9 %reshape_reshape.21 = bf16[640,2880]{1,0:T(8,128)(2,1)} reshape(bf16[32,5,4,2880]{3,2,1,0:T(4,128)(2,1)} %all-to-all-done.1) | data formatting | bytes 7372800 | tf_op jit(solution)/shard_map/reshape;reshape | solution.py:91
  90.0 20.0 %fusion.2 = f32[640,2880]{0,1:T(8,128)} fusion(bf16[640,2880]{1,0:T(8,128)(2,1)} %reshape_reshape.21, bf16[1,1,2880,2880]{3,2,1,0:T(8,128)(2,1)} %param.12), kind=kOutput, calls=%fused_computation.2 | convolution fusion | flops 10616832000 | bytes 27648000 | tf_op jit(solution)/shard_map/dot_general | solution.py:19
  110.0 21.7 %all-to-all-done = bf16[32,5,4,2880]{3,2,1,0:T(4,128)(2,1)} async-done(((bf16[32,5,4,2880]{3,2,1,0:T(4,128)(2,1)}), bf16[32,5,4,2880]{3,2,1,0:T(4,128)(2,1)}, u32[]{:S(2)}, u32[]{:S(2)}) %all-to-all-start) | async-done | bytes 3686432 | tf_op jit(solution)/shard_map/all_to_all | solution.py:43
  131.7 7.0 %reshape_reshape.19 = bf16[640,2880]{1,0:T(8,128)(2,1)} reshape(bf16[32,5,4,2880]{3,2,1,0:T(4,128)(2,1)} %all-to-all-done) | data formatting | bytes 7372800 | tf_op jit(solution)/shard_map/reshape;reshape | solution.py:92
  138.6 13.9 %fusion.11 = (bf16[640,1440]{0,1:T(8,128)(2,1)S(1)}, bf16[640,1440]{0,1:T(8,128)(2,1)}) fusion(f32[640,2880]{0,1:T(8,128)} %fusion.2, bf16[640,2880]{1,0:T(8,128)(2,1)} %reshape_reshape.19, bf16[1,1,1440,2880]{3,2,1,0:T(8,128)(2,1)} %param.13), kind=kOutput, calls=%fused_computation.13 | convolution fusion | flops 5322240000 | bytes 23040000 | tf_op jit(solution)/shard_map/dot_general | solution.py:20
  152.6 18.2 %fusion.6 = bf16[640,2880]{1,0:T(8,128)(2,1)} fusion(bf16[1,1,2880,2880]{3,2,1,0:T(8,128)(2,1)} %param.12, bf16[640,1440]{0,1:T(8,128)(2,1)} %get-tuple-element.10, bf16[640,1440]{0,1:T(8,128)(2,1)S(1)} %get-tuple-element.9), kind=kOutput, calls=%fused_computation.8 | convolution fusion | flops 10626048000 | bytes 23961600 | tf_op jit(solution)/shard_map/dot_general | solution.py:30
  170.7 7.2 %reshape_reshape.22 = bf16[32,5,4,2880]{3,2,1,0:T(4,128)(2,1)} reshape(bf16[640,2880]{1,0:T(8,128)(2,1)} %fusion.6) | data formatting | bytes 7372800 | tf_op jit(solution)/shard_map/reshape;reshape | solution.py:42
  177.9 51.4 %all_to_all.15 = bf16[32,5,4,2880]{3,2,1,0:T(4,128)(2,1)} all-to-all(bf16[32,5,4,2880]{3,2,1,0:T(4,128)(2,1)} %reshape_reshape.22), channel_id=1, replica_groups=mesh['section'=4,'expert'=32] {'expert'}, dimensions={0} | all-to-all | bytes 7372800 | tf_op jit(solution)/shard_map/all_to_all | solution.py:43
  229.4 6.9 %reshape_reshape.23 = bf16[640,2880]{1,0:T(8,128)(2,1)} reshape(bf16[32,5,4,2880]{3,2,1,0:T(4,128)(2,1)} %all_to_all.15) | data formatting | bytes 7372800 | tf_op jit(solution)/shard_map/reshape;reshape | solution.py:96
  236.3 3.7 %fusion.19 = (f32[128]{0:T(128)S(1)}, f32[128,2880]{0,1:T(8,128)S(1)}) fusion(bf16[1,128,2880]{1,2,0:T(8,128)(2,1)S(1)} %copy-done, f32[128]{0:T(128)S(1)} %add_rsqrt_fusion, f32[2880]{0:T(1024)S(1)} %reduce.1, pred[128,640]{1,0:T(8,128)(4,1)S(1)} %fusion.25, bf16[640,2880]{1,0:T(8,128)(2,1)} %reshape_reshape.23), kind=kOutput, calls=%fused_computation.26 | convolution fusion | flops 473702272 | bytes 5992704 | tf_op jit(solution)/shard_map/dot_general | solution.py:99
  240.1 0.4 fusion.26
  240.5 0.9 collective-permute-start
  241.4 18.7 %collective-permute-done = bf16[1,128,2880]{1,2,0:T(8,128)(2,1)S(1)} collective-permute-done((bf16[1,128,2880]{1,2,0:T(8,128)(2,1)S(1)}, bf16[1,128,2880]{1,2,0:T(8,128)(2,1)S(1)}, u32[]{:S(2)}, u32[]{:S(2)}) %collective-permute-start) | collective-permute-done | bytes 737312 | tf_op jit(solution)/shard_map/ppermute | solution.py:15
  260.1 0.9 copy.23
  (11 shorter events, 0.1 us)
Async XLA Ops:
  4.1 6.4 %copy-start = (bf16[1,128,2880]{1,2,0:T(8,128)(2,1)S(1)}, bf16[1,128,2880]{1,2,0:T(8,128)(2,1)}, u32[]{:S(2)}) copy-start(bf16[1,128,2880]{1,2,0:T(8,128)(2,1)} %param.7) | copy-start | bytes 2211844
  20.8 57.2 %all-to-all-start.1 = ((bf16[32,5,4,2880]{3,2,1,0:T(4,128)(2,1)}), bf16[32,5,4,2880]{3,2,1,0:T(4,128)(2,1)}, u32[]{:S(2)}, u32[]{:S(2)}) async-start(bf16[32,5,4,2880]{3,2,1,0:T(4,128)(2,1)} %reshape_reshape.20), calls=%async_computation.1 | async-start | bytes 7536640 | tf_op jit(solution)/shard_map/all_to_all | solution.py:43
  78.1 53.6 %all-to-all-start = ((bf16[32,5,4,2880]{3,2,1,0:T(4,128)(2,1)}), bf16[32,5,4,2880]{3,2,1,0:T(4,128)(2,1)}, u32[]{:S(2)}, u32[]{:S(2)}) async-start(bf16[32,5,4,2880]{3,2,1,0:T(4,128)(2,1)} %reshape_reshape.18), calls=%async_computation | async-start | bytes 7536640 | tf_op jit(solution)/shard_map/all_to_all | solution.py:43
  236.3 3.8 %copy-start.1 = (bf16[1,128,2880]{1,2,0:T(8,128)(2,1)S(1)}, bf16[1,128,2880]{1,2,0:T(8,128)(2,1)}, u32[]{:S(2)}) copy-start(bf16[1,128,2880]{1,2,0:T(8,128)(2,1)} %param.9) | copy-start | bytes 2211844
  240.5 19.6 %collective-permute-start = (bf16[1,128,2880]{1,2,0:T(8,128)(2,1)S(1)}, bf16[1,128,2880]{1,2,0:T(8,128)(2,1)S(1)}, u32[]{:S(2)}, u32[]{:S(2)}) collective-permute-start(bf16[1,128,2880]{1,2,0:T(8,128)(2,1)S(1)} %fusion.26), channel_id=1, source_target_pairs={{0,96},{32,0},{64,32},{96,64},{1,97},{33,1},{65,33},{97,65},{2,98}... | collective-permute-start | bytes 2211848 | tf_op jit(solution)/shard_map/ppermute | solution.py:15

commit v7 on v3

--- a/solution.py
+++ b/solution.py
@@ -7,7 +7,7 @@
 glu_alpha = 1.702
 norm_eps = 1e-05
 ROW_TILE = 8
-LANES = 128
+QUAD = 4
 
 
 def shifted(value, axis, steps):
@@ -17,33 +17,35 @@
 
 
 def expert_backward(rows_in, grad_rows, gate_up, down_proj):
-    preact = jnp.dot(rows_in, gate_up, preferred_element_type=jnp.float32)
+    last = rows_in.ndim - 1
+    preact = lax.dot_general(
+        rows_in, gate_up, (((last,), (0,)), ((), ())), preferred_element_type=jnp.float32
+    )
     dact = lax.dot_general(
-        grad_rows, down_proj, (((1,), (1,)), ((), ())), preferred_element_type=jnp.float32
+        grad_rows, down_proj, (((last,), (1,)), ((), ())), preferred_element_type=jnp.float32
     )
     half = down_proj.shape[0]
-    gate = preact[:, :half]
-    up_part = preact[:, half:]
+    gate = preact[..., :half]
+    up_part = preact[..., half:]
     sig = jax.nn.sigmoid(glu_alpha * gate)
     dgate = dact * (up_part + 1.0) * (sig + glu_alpha * gate * sig * (1.0 - sig))
     dup = dact * gate * sig
-    dpre = jnp.concatenate([dgate, dup], axis=1).astype(jnp.bfloat16)
-    result_t = lax.dot_general(
-        gate_up, dpre, (((1,), (1,)), ((), ())), preferred_element_type=jnp.float32
+    dpre = jnp.concatenate([dgate, dup], axis=last).astype(jnp.bfloat16)
+    result = lax.dot_general(
+        dpre, gate_up, (((last,), (1,)), ((), ())), preferred_element_type=jnp.float32
     )
-    return row_major(result_t.astype(jnp.bfloat16).T)
+    return row_major(result.astype(jnp.bfloat16))
 
 
 def row_major(value):
     return with_layout_constraint(value, Layout(tuple(range(value.ndim))))
 
 
-def exchange(rows, groups):
-    width = rows.shape[1]
-    per_group = rows.shape[0] // groups
-    dense = rows.reshape(groups, per_group * width // LANES, LANES)
-    moved = lax.all_to_all(dense, "expert", split_axis=0, concat_axis=0, tiled=True)
-    return moved.reshape(groups * per_group, width)
+def exchange(slab, experts):
+    groups, quad, width = slab.shape
+    parted = slab.reshape(experts, groups // experts, quad, width)
+    moved = lax.all_to_all(parted, "expert", split_axis=0, concat_axis=0, tiled=True)
+    return moved.reshape(groups, quad, width)
 
 
 def per_device(hidden_in, norm_gain, out_grad, expert_ids, route_weights, w_gate_up, w_down):
@@ -75,22 +77,27 @@
     hits = slot_index[:, :, None] == slot_ids[None, None, :]
     placement = jnp.any(hits, axis=1)
     slot_weight = jnp.sum(jnp.where(hits, weights[:, :, None], 0.0), axis=(0, 1))
-    placement_bf16 = placement.astype(jnp.bfloat16)
+    groups = experts * capacity // QUAD
+    placement_quads = placement.astype(jnp.bfloat16).reshape(tok_count, groups, QUAD)
     pick = (((0,), (0,)), ((), ()))
-    inputs_slab = lax.dot_general(
-        rescaled_input, placement_bf16, pick, preferred_element_type=jnp.float32
-    ).astype(jnp.bfloat16).T
-    inputs_slab = row_major(inputs_slab)
-    grads_slab = (
-        lax.dot_general(incoming_gradient, placement_bf16, pick, preferred_element_type=jnp.float32)
-        * slot_weight[None, :]
-    ).astype(jnp.bfloat16).T
-    grads_slab = row_major(grads_slab)
+    inputs_slab = row_major(
+        lax.dot_general(placement_quads, rescaled_input, pick, preferred_element_type=jnp.float32)
+        .astype(jnp.bfloat16)
+    )
+    grads_slab = row_major(
+        (
+            lax.dot_general(placement_quads, incoming_gradient, pick, preferred_element_type=jnp.float32)
+            * slot_weight.reshape(groups, QUAD)[:, :, None]
+        ).astype(jnp.bfloat16)
+    )
+    inputs_slab, grads_slab = lax.optimization_barrier((inputs_slab, grads_slab))
     arrived_inputs = exchange(inputs_slab, experts)
     arrived_grads = exchange(grads_slab, experts)
     computed = expert_backward(arrived_inputs, arrived_grads, gate_up, down_proj)
     returned = exchange(computed, experts)
-    dnorm = jnp.dot(placement_bf16, returned, preferred_element_type=jnp.float32)
+    dnorm = lax.dot_general(
+        placement_quads, returned, (((1, 2), (0, 1)), ((), ())), preferred_element_type=jnp.float32
+    )
     normalized_input_gradient = dnorm * gain_vector_row[None, :]
     projected_rows = jnp.mean(normalized_input_gradient * normalized_input, axis=-1, keepdims=True)
     section_gradient = (

time: 258 us -> 237 us (0.919)
  blocking collectives: 51 us -> 105 us
  local copies, waits for them, and re-layouts: 46.3 us -> 8.53 us
  waiting for transfers between devices: 77.4 us -> 49.5 us
  starting transfers between devices: 14.5 us -> 5.93 us
  other arithmetic: 4.47 us -> 12.7 us
  matrix products: 63.1 us -> 54.9 us
    all_to_all x1 -> x2, blocking collectives: 51 us -> 105 us  [exchange(): lax.all_to_all(parted, 'expert', split_axis=0, concat_axis=0, tiled=True)]
    reshape x6 -> x0, local copies, waits for them, and re-layouts: 44.1 us -> none  [the longest x3 23.7 us: exchange(): dense = rows.reshape(groups, per_group * width // LANES, LANES)]
    all_to_all x2 -> x1, waiting for transfers between devices: 58.6 us -> 30.8 us  [exchange(): lax.all_to_all(parted, 'expert', split_axis=0, concat_axis=0, tiled=True)]
    all_to_all x2 -> x1, starting transfers between devices: 13.6 us -> 5.02 us  [exchange(): lax.all_to_all(parted, 'expert', split_axis=0, concat_axis=0, tiled=True)]
    dot_general x6, matrix products: 63.1 us -> 54.9 us  [the longest x1 18.1 us: expert_backward(): lax.dot_general(dpre, gate_up, (((last,), (1,)), ((), ())), preferred_ele...]
    convert_element_type x0 -> x1, other arithmetic: none -> 7.52 us  [per_device(): grads_slab = row_major((lax.dot_general(placement_quads, incoming_gradien...]
    unnamed x8 -> x7, local copies, waits for them, and re-layouts: 1.66 us -> 5.67 us
  transfers between devices with their start and end apart: 3 -> 2, of which waited for: 3 -> 2; matrix products, arithmetic and copies ran while one was open for 15% -> 8% of each run, Pallas kernels for 0% -> 0%
where the time goes in v7:
time: 237 us; the launch traced here: 236 us
  blocking collectives  105 us (44%)
  matrix products  54.9 us (23%)
  waiting for transfers between devices  49.5 us (21%)
  other arithmetic  12.7 us (5%)
  local copies, waits for them, and re-layouts  8.53 us (4%)
  starting transfers between devices  5.93 us (3%)
    all_to_all x2, blocking collectives, exchange(): lax.all_to_all(parted, 'expert', split_axis=0, concat_axis=0, tiled=True)  105 us
    all_to_all x1, waiting for transfers between devices, exchange(): lax.all_to_all(parted, 'expert', split_axis=0, concat_axis=0, tiled=True)  30.8 us
    ppermute x1, waiting for transfers between devices, shifted(): return lax.ppermute(value, axis, pairs)  18.7 us
    dot_general x1, matrix products, expert_backward(): lax.dot_general(dpre, gate_up, (((last,), (1,)), ((), ())), preferred_ele...  18.1 us
    dot_general x1, matrix products, expert_backward(): lax.dot_general(rows_in, gate_up, (((last,), (0,)), ((), ())), preferred_...  18 us
    dot_general x1, matrix products, expert_backward(): lax.dot_general(grad_rows, down_proj, (((last,), (1,)), ((), ())), prefer...  13.8 us
    convert_element_type x1, other arithmetic, per_device(): grads_slab = row_major((lax.dot_general(placement_quads, incoming_gradien...  7.52 us
    unnamed x7, local copies, waits for them, and re-layouts  5.67 us
  transfers between devices with their start and end apart: 2, of which 2 were waited for; matrix products, arithmetic and copies ran while one was open for 8% of the time, Pallas kernels for 0%

profile of v7, /device:TPU:6, one launch (start us, length us, event | category | flops | bytes accessed | tf_op | source)
XLA Modules:
  0.0 236.3 jit_solution(11020887792535175149)
XLA Ops:
  0.0 0.8 copy.30
  0.8 0.1 eq.42
  0.9 0.1 eq.38
  1.0 1.5 fusion.35
  2.5 1.2 reduce-window.6
  3.7 0.2 slice_reduce_fusion
  4.0 0.1 fusion.52
  4.1 0.1 reduce_sum.40
  4.2 0.1 copy.34
  4.3 0.3 fusion.38
  4.5 0.9 select_reduce_fusion
  5.4 0.1 mul.111
  5.6 0.2 copy.35
  5.8 0.7 reduce.1
  6.5 2.3 fusion.40
  8.9 0.0 copy-start.1
  8.9 1.9 copy.68
  10.8 1.1 fusion.43
  12.0 7.5 %fusion.6 = bf16[160,4,2880]{2,1,0:T(4,128)(2,1)} fusion(f32[160,4,2880]{2,0,1:T(8,128)S(1)} %fusion.43, f32[160,4]{1,0:T(8,128)S(1)} %mul.111), kind=kLoop, calls=%fused_computation.7 | loop fusion | flops 3686400 | bytes 11061760 | tf_op jit(solution)/shard_map/convert_element_type | solution.py:91
  19.5 54.8 %all_to_all.15 = bf16[32,5,4,2880]{3,2,1,0:T(4,128)(2,1)} all-to-all(bf16[32,5,4,2880]{3,2,1,0:T(4,128)(2,1)S(1)} %bitcast.85), channel_id=1, replica_groups=mesh['section'=4,'expert'=32] {'expert'}, dimensions={0} | all-to-all | bytes 7372800 | tf_op jit(solution)/shard_map/all_to_all | solution.py:47
  74.3 5.0 %all-to-all-start = ((bf16[32,5,4,2880]{3,2,1,0:T(4,128)(2,1)}), bf16[32,5,4,2880]{3,2,1,0:T(4,128)(2,1)}, u32[]{:S(2)}, u32[]{:S(2)}) async-start(bf16[32,5,4,2880]{3,2,1,0:T(4,128)(2,1)} %bitcast.84), calls=%async_computation | async-start | bytes 7536640 | tf_op jit(solution)/shard_map/all_to_all | solution.py:47
  79.4 18.0 %fusion.2 = f32[160,4,2880]{2,0,1:T(8,128)} fusion(bf16[1,1,2880,2880]{3,2,1,0:T(8,128)(2,1)} %param.12, bf16[160,4,2880]{2,1,0:T(4,128)(2,1)} %bitcast.87), kind=kOutput, calls=%fused_computation.2 | convolution fusion | flops 10616832000 | bytes 27648000 | tf_op jit(solution)/shard_map/dot_general | solution.py:21
  97.3 30.8 %all-to-all-done = bf16[32,5,4,2880]{3,2,1,0:T(4,128)(2,1)} async-done(((bf16[32,5,4,2880]{3,2,1,0:T(4,128)(2,1)}), bf16[32,5,4,2880]{3,2,1,0:T(4,128)(2,1)}, u32[]{:S(2)}, u32[]{:S(2)}) %all-to-all-start) | async-done | bytes 3686432 | tf_op jit(solution)/shard_map/all_to_all | solution.py:47
  128.1 13.8 %fusion.12 = (bf16[160,4,1440]{2,0,1:T(8,128)(2,1)S(1)}, bf16[160,4,1440]{2,0,1:T(8,128)(2,1)}) fusion(f32[160,4,2880]{2,0,1:T(8,128)} %fusion.2, bf16[1,1,1440,2880]{3,2,1,0:T(8,128)(2,1)} %param.13, bf16[160,4,2880]{2,1,0:T(4,128)(2,1)} %bitcast.10), kind=kOutput, calls=%fused_computation.13 | convolution fusion | flops 5322240000 | bytes 23040000 | tf_op jit(solution)/shard_map/dot_general | solution.py:24
  141.9 18.1 %fusion.7 = bf16[160,4,2880]{2,0,1:T(8,128)(2,1)} fusion(bf16[1,1,2880,2880]{3,2,1,0:T(8,128)(2,1)} %param.12, bf16[160,4,1440]{2,0,1:T(8,128)(2,1)} %get-tuple-element.10, bf16[160,4,1440]{2,0,1:T(8,128)(2,1)S(1)} %get-tuple-element.9), kind=kOutput, calls=%fused_computation.9 | convolution fusion | flops 10626048000 | bytes 23961600 | tf_op jit(solution)/shard_map/dot_general | solution.py:34
  160.0 4.0 %copy.46 = bf16[160,4,2880]{2,1,0:T(4,128)(2,1)S(1)} copy(bf16[160,4,2880]{2,0,1:T(8,128)(2,1)} %fusion.7) | data formatting | bytes 7372800
  164.0 49.8 %all_to_all.16 = bf16[32,5,4,2880]{3,2,1,0:T(4,128)(2,1)S(1)} all-to-all(bf16[32,5,4,2880]{3,2,1,0:T(4,128)(2,1)S(1)} %bitcast.86), channel_id=1, replica_groups=mesh['section'=4,'expert'=32] {'expert'}, dimensions={0} | all-to-all | bytes 7372800 | tf_op jit(solution)/shard_map/all_to_all | solution.py:47
  213.8 1.6 fusion.30
  215.4 0.4 fusion.42
  215.8 0.9 collective-permute-start
  216.7 18.7 %collective-permute-done = bf16[1,128,2880]{1,2,0:T(8,128)(2,1)S(1)} collective-permute-done((bf16[1,128,2880]{1,2,0:T(8,128)(2,1)S(1)}, bf16[1,128,2880]{1,2,0:T(8,128)(2,1)S(1)}, u32[]{:S(2)}, u32[]{:S(2)}) %collective-permute-start) | collective-permute-done | bytes 737312 | tf_op jit(solution)/shard_map/ppermute | solution.py:16
  235.4 0.9 copy.76
  (9 shorter events, 0.1 us)
Async XLA Ops:
  8.9 2.0 copy-start.1
  74.3 53.8 %all-to-all-start = ((bf16[32,5,4,2880]{3,2,1,0:T(4,128)(2,1)}), bf16[32,5,4,2880]{3,2,1,0:T(4,128)(2,1)}, u32[]{:S(2)}, u32[]{:S(2)}) async-start(bf16[32,5,4,2880]{3,2,1,0:T(4,128)(2,1)} %bitcast.84), calls=%async_computation | async-start | bytes 7536640 | tf_op jit(solution)/shard_map/all_to_all | solution.py:47
  164.0 49.8 %copy-start = (bf16[1,128,2880]{1,2,0:T(8,128)(2,1)S(1)}, bf16[1,128,2880]{1,2,0:T(8,128)(2,1)}, u32[]{:S(2)}) copy-start(bf16[1,128,2880]{1,2,0:T(8,128)(2,1)} %param.7) | copy-start | bytes 2211844
  215.8 19.6 %collective-permute-start = (bf16[1,128,2880]{1,2,0:T(8,128)(2,1)S(1)}, bf16[1,128,2880]{1,2,0:T(8,128)(2,1)S(1)}, u32[]{:S(2)}, u32[]{:S(2)}) collective-permute-start(bf16[1,128,2880]{1,2,0:T(8,128)(2,1)S(1)} %fusion.42), channel_id=1, source_target_pairs={{0,96},{32,0},{64,32},{96,64},{1,97},{33,1},{65,33},{97,65},{2,98}... | collective-permute-start | bytes 2211848 | tf_op jit(solution)/shard_map/ppermute | solution.py:16

commit v8 on v7

--- a/solution.py
+++ b/solution.py
@@ -84,11 +84,17 @@
         lax.dot_general(placement_quads, rescaled_input, pick, preferred_element_type=jnp.float32)
         .astype(jnp.bfloat16)
     )
+    scaled_rows = (weights[:, :, None] * incoming_gradient[:, None, :].astype(jnp.float32)).astype(
+        jnp.bfloat16
+    ).reshape(tok_count * top_count, feat_width)
+    assignment_quads = (
+        (slot_index.reshape(-1)[:, None] == slot_ids[None, :])
+        .astype(jnp.bfloat16)
+        .reshape(tok_count * top_count, groups, QUAD)
+    )
     grads_slab = row_major(
-        (
-            lax.dot_general(placement_quads, incoming_gradient, pick, preferred_element_type=jnp.float32)
-            * slot_weight.reshape(groups, QUAD)[:, :, None]
-        ).astype(jnp.bfloat16)
+        lax.dot_general(assignment_quads, scaled_rows, pick, preferred_element_type=jnp.float32)
+        .astype(jnp.bfloat16)
     )
     inputs_slab, grads_slab = lax.optimization_barrier((inputs_slab, grads_slab))
     arrived_inputs = exchange(inputs_slab, experts)

time: 237 us -> 250 us (1.055)
  local copies, waits for them, and re-layouts: 8.53 us -> 26.2 us
  other arithmetic: 12.7 us -> 4.36 us
  matrix products: 54.9 us -> 58.8 us
    mul x1 -> x3, local copies, waits for them, and re-layouts: 0.11 us -> 11.5 us  [per_device(): weights[:, :, None] * incoming_gradient[:, None, :].astype(jnp.float32)]
    convert_element_type x1, other arithmetic: 7.52 us -> 0.1 us  [per_device(): incoming_gradient.astype(jnp.float32)]
    dot_general x1, matrix products: 1.14 us -> 5.03 us  [per_device(): lax.dot_general(assignment_quads, scaled_rows, pick, preferred_element_ty...]
    dot_general x0 -> x1, local copies, waits for them, and re-layouts: none -> 3.88 us  [per_device(): lax.dot_general(assignment_quads, scaled_rows, pick, preferred_element_ty...]
    unnamed x7 -> x14, local copies, waits for them, and re-layouts: 5.67 us -> 5.79 us
  transfers between devices with their start and end apart: 2 -> 2, of which waited for: 2 -> 2; matrix products, arithmetic and copies ran while one was open for 8% -> 7% of each run, Pallas kernels for 0% -> 0%
where the time goes in v8:
time: 250 us; the launch traced here: 249 us
  blocking collectives  105 us (42%)
  matrix products  58.8 us (24%)
  waiting for transfers between devices  49.3 us (20%)
  local copies, waits for them, and re-layouts  26.2 us (10%)
  starting transfers between devices  5.9 us (2%)
  other arithmetic  4.36 us (2%)
    all_to_all x2, blocking collectives, exchange(): lax.all_to_all(parted, 'expert', split_axis=0, concat_axis=0, tiled=True)  105 us
    all_to_all x1, waiting for transfers between devices, exchange(): lax.all_to_all(parted, 'expert', split_axis=0, concat_axis=0, tiled=True)  30.6 us
    ppermute x1, waiting for transfers between devices, shifted(): return lax.ppermute(value, axis, pairs)  18.7 us
    dot_general x1, matrix products, expert_backward(): lax.dot_general(dpre, gate_up, (((last,), (1,)), ((), ())), preferred_ele...  18.1 us
    dot_general x1, matrix products, expert_backward(): lax.dot_general(rows_in, gate_up, (((last,), (0,)), ((), ())), preferred_...  18 us
    dot_general x1, matrix products, expert_backward(): lax.dot_general(grad_rows, down_proj, (((last,), (1,)), ((), ())), prefer...  13.8 us
    mul x3, local copies, waits for them, and re-layouts, per_device(): weights[:, :, None] * incoming_gradient[:, None, :].astype(jnp.float32)  11.5 us
    unnamed x14, local copies, waits for them, and re-layouts  5.79 us
  transfers between devices with their start and end apart: 2, of which 2 were waited for; matrix products, arithmetic and copies ran while one was open for 7% of the time, Pallas kernels for 0%

profile of v8, /device:TPU:6, one launch (start us, length us, event | category | flops | bytes accessed | tf_op | source)
XLA Modules:
  0.0 249.3 jit_solution(1120224311111760629)
XLA Ops:
  0.0 0.8 copy.30
  0.9 0.1 eq.62
  1.0 1.2 reduce-window.6
  2.2 0.2 slice_reduce_fusion
  2.5 0.1 fusion.55
  2.6 0.1 reduce_sum.31
  2.8 0.3 fusion.41
  3.0 0.2 copy.35
  3.3 1.5 fusion.38
  4.8 0.7 reduce.1
  5.5 2.3 fusion.44
  7.9 3.8 %copy.69 = bf16[160,4,2880]{2,1,0:T(4,128)(2,1)} copy(bf16[160,4,2880]{2,0,1:T(8,128)(2,1)S(1)} %fusion.44) | data formatting | bytes 7372800 | tf_op jit(solution)/shard_map/dot_general | solution.py:84
  11.8 0.5 copy.39
  12.3 3.6 %mul.133 = f32[128,4,2880]{2,1,0:T(4,128)} broadcast(f32[128,2880]{1,0:T(8,128)S(1)} %copy.39), dimensions={0,2} | broadcast | bytes 7372800 | tf_op jit(solution)/shard_map/mul | solution.py:87
  15.9 7.8 %mul.134 = f32[512,2880]{1,0:T(8,128)} reshape(f32[128,4,2880]{2,1,0:T(4,128)} %mul.133) | data formatting | bytes 11796480 | tf_op jit(solution)/shard_map/mul | solution.py:87
  23.6 0.1 copy.38
  23.7 0.1 mul.131
  23.9 5.0 %fusion.26 = bf16[160,4,2880]{2,0,1:T(8,128)(2,1)S(1)} fusion(f32[512,2880]{1,0:T(8,128)} %mul.134, f32[512]{0:T(512)S(1)} %mul.131, s32[160,4]{0,1:T(4,128)S(1)} %multiply_add_fusion, s32[512]{0:T(512)S(1)} %multiply_add_fusion.1), kind=kOutput, calls=%fused_computation.27 | convolution fusion | flops 1890713600 | bytes 9591296 | tf_op jit(solution)/shard_map/dot_general | solution.py:96
  28.9 3.9 %copy.68 = bf16[160,4,2880]{2,1,0:T(4,128)(2,1)} copy(bf16[160,4,2880]{2,0,1:T(8,128)(2,1)S(1)} %fusion.26) | data formatting | bytes 7372800 | tf_op jit(solution)/shard_map/dot_general | solution.py:96
  32.8 54.8 %all_to_all.15 = bf16[32,5,4,2880]{3,2,1,0:T(4,128)(2,1)} all-to-all(bf16[32,5,4,2880]{3,2,1,0:T(4,128)(2,1)S(1)} %bitcast.86), channel_id=1, replica_groups=mesh['section'=4,'expert'=32] {'expert'}, dimensions={0} | all-to-all | bytes 7372800 | tf_op jit(solution)/shard_map/all_to_all | solution.py:47
  87.6 5.0 %all-to-all-start = ((bf16[32,5,4,2880]{3,2,1,0:T(4,128)(2,1)}), bf16[32,5,4,2880]{3,2,1,0:T(4,128)(2,1)}, u32[]{:S(2)}, u32[]{:S(2)}) async-start(bf16[32,5,4,2880]{3,2,1,0:T(4,128)(2,1)} %bitcast.87), calls=%async_computation | async-start | bytes 7536640 | tf_op jit(solution)/shard_map/all_to_all | solution.py:47
  92.6 18.0 %fusion.2 = f32[160,4,2880]{2,0,1:T(8,128)} fusion(bf16[1,1,2880,2880]{3,2,1,0:T(8,128)(2,1)} %param.12, bf16[160,4,2880]{2,1,0:T(4,128)(2,1)} %bitcast.89), kind=kOutput, calls=%fused_computation.2 | convolution fusion | flops 10616832000 | bytes 27648000 | tf_op jit(solution)/shard_map/dot_general | solution.py:21
  110.6 30.6 %all-to-all-done = bf16[32,5,4,2880]{3,2,1,0:T(4,128)(2,1)} async-done(((bf16[32,5,4,2880]{3,2,1,0:T(4,128)(2,1)}), bf16[32,5,4,2880]{3,2,1,0:T(4,128)(2,1)}, u32[]{:S(2)}, u32[]{:S(2)}) %all-to-all-start) | async-done | bytes 3686432 | tf_op jit(solution)/shard_map/all_to_all | solution.py:47
  141.2 13.8 %fusion.11 = (bf16[160,4,1440]{2,0,1:T(8,128)(2,1)S(1)}, bf16[160,4,1440]{2,0,1:T(8,128)(2,1)}) fusion(f32[160,4,2880]{2,0,1:T(8,128)} %fusion.2, bf16[1,1,1440,2880]{3,2,1,0:T(8,128)(2,1)} %param.13, bf16[160,4,2880]{2,1,0:T(4,128)(2,1)} %bitcast.10), kind=kOutput, calls=%fused_computation.13 | convolution fusion | flops 5322240000 | bytes 23040000 | tf_op jit(solution)/shard_map/dot_general | solution.py:24
  155.0 18.1 %fusion.6 = bf16[160,4,2880]{2,0,1:T(8,128)(2,1)} fusion(bf16[1,1,2880,2880]{3,2,1,0:T(8,128)(2,1)} %param.12, bf16[160,4,1440]{2,0,1:T(8,128)(2,1)} %get-tuple-element.10, bf16[160,4,1440]{2,0,1:T(8,128)(2,1)S(1)} %get-tuple-element.9), kind=kOutput, calls=%fused_computation.9 | convolution fusion | flops 10626048000 | bytes 23961600 | tf_op jit(solution)/shard_map/dot_general | solution.py:34
  173.1 4.0 %copy.50 = bf16[160,4,2880]{2,1,0:T(4,128)(2,1)S(1)} copy(bf16[160,4,2880]{2,0,1:T(8,128)(2,1)} %fusion.6) | data formatting | bytes 7372800
  177.1 49.8 %all_to_all.16 = bf16[32,5,4,2880]{3,2,1,0:T(4,128)(2,1)S(1)} all-to-all(bf16[32,5,4,2880]{3,2,1,0:T(4,128)(2,1)S(1)} %bitcast.88), channel_id=1, replica_groups=mesh['section'=4,'expert'=32] {'expert'}, dimensions={0} | all-to-all | bytes 7372800 | tf_op jit(solution)/shard_map/all_to_all | solution.py:47
  226.8 1.6 fusion.33
  228.5 0.4 fusion.46
  228.9 0.9 collective-permute-start
  229.8 18.7 %collective-permute-done = bf16[1,128,2880]{1,2,0:T(8,128)(2,1)S(1)} collective-permute-done((bf16[1,128,2880]{1,2,0:T(8,128)(2,1)S(1)}, bf16[1,128,2880]{1,2,0:T(8,128)(2,1)S(1)}, u32[]{:S(2)}, u32[]{:S(2)}) %collective-permute-start) | collective-permute-done | bytes 737312 | tf_op jit(solution)/shard_map/ppermute | solution.py:16
  248.5 0.9 copy.77
  (21 shorter events, 0.4 us)
Async XLA Ops:
  7.9 3.8 %copy-start.2 = (bf16[1,128,2880]{1,2,0:T(8,128)(2,1)S(1)}, bf16[1,128,2880]{1,2,0:T(8,128)(2,1)}, u32[]{:S(2)}) copy-start(bf16[1,128,2880]{1,2,0:T(8,128)(2,1)} %param.9) | copy-start | bytes 2211844
  15.9 7.8 %copy-start.4 = (f32[1,128,4]{1,2,0:T(4,128)S(1)}, f32[1,128,4]{1,2,0:T(4,128)}, u32[]{:S(2)}) copy-start(f32[1,128,4]{1,2,0:T(4,128)} %param.11) | copy-start | bytes 6148
  28.9 3.9 %copy-start = (bf16[160,4,2880]{2,1,0:T(4,128)(2,1)S(1)}, bf16[160,4,2880]{2,1,0:T(4,128)(2,1)}, u32[]{:S(2)}) copy-start(bf16[160,4,2880]{2,1,0:T(4,128)(2,1)} %copy.69) | copy-start | bytes 11059204
  87.6 53.6 %all-to-all-start = ((bf16[32,5,4,2880]{3,2,1,0:T(4,128)(2,1)}), bf16[32,5,4,2880]{3,2,1,0:T(4,128)(2,1)}, u32[]{:S(2)}, u32[]{:S(2)}) async-start(bf16[32,5,4,2880]{3,2,1,0:T(4,128)(2,1)} %bitcast.87), calls=%async_computation | async-start | bytes 7536640 | tf_op jit(solution)/shard_map/all_to_all | solution.py:47
  177.1 49.8 %copy-start.1 = (bf16[1,128,2880]{1,2,0:T(8,128)(2,1)S(1)}, bf16[1,128,2880]{1,2,0:T(8,128)(2,1)}, u32[]{:S(2)}) copy-start(bf16[1,128,2880]{1,2,0:T(8,128)(2,1)} %param.7) | copy-start | bytes 2211844
  226.8 1.6 copy-start.3
  228.9 19.6 %collective-permute-start = (bf16[1,128,2880]{1,2,0:T(8,128)(2,1)S(1)}, bf16[1,128,2880]{1,2,0:T(8,128)(2,1)S(1)}, u32[]{:S(2)}, u32[]{:S(2)}) collective-permute-start(bf16[1,128,2880]{1,2,0:T(8,128)(2,1)S(1)} %fusion.46), channel_id=1, source_target_pairs={{0,96},{32,0},{64,32},{96,64},{1,97},{33,1},{65,33},{97,65},{2,98}... | collective-permute-start | bytes 2211848 | tf_op jit(solution)/shard_map/ppermute | solution.py:16

commit v9 on v7

--- a/solution.py
+++ b/solution.py
@@ -90,7 +90,6 @@
             * slot_weight.reshape(groups, QUAD)[:, :, None]
         ).astype(jnp.bfloat16)
     )
-    inputs_slab, grads_slab = lax.optimization_barrier((inputs_slab, grads_slab))
     arrived_inputs = exchange(inputs_slab, experts)
     arrived_grads = exchange(grads_slab, experts)
     computed = expert_backward(arrived_inputs, arrived_grads, gate_up, down_proj)

time: 237 us -> 231 us (0.975)
  blocking collectives: 105 us -> 49.8 us
  waiting for transfers between devices: 49.5 us -> 89.4 us
  starting transfers between devices: 5.93 us -> 14.5 us
    all_to_all x2 -> x1, blocking collectives: 105 us -> 49.8 us  [exchange(): lax.all_to_all(parted, 'expert', split_axis=0, concat_axis=0, tiled=True)]
    all_to_all x1 -> x2, waiting for transfers between devices: 30.8 us -> 70.7 us  [exchange(): lax.all_to_all(parted, 'expert', split_axis=0, concat_axis=0, tiled=True)]
    all_to_all x1 -> x2, starting transfers between devices: 5.02 us -> 13.6 us  [exchange(): lax.all_to_all(parted, 'expert', split_axis=0, concat_axis=0, tiled=True)]
    unnamed x7 -> x10, local copies, waits for them, and re-layouts: 5.67 us -> 9.43 us
  transfers between devices with their start and end apart: 2 -> 3, of which waited for: 2 -> 3; matrix products, arithmetic and copies ran while one was open for 8% -> 12% of each run, Pallas kernels for 0% -> 0%
where the time goes in v9:
time: 231 us
  waiting for transfers between devices  89.4 us (39%)
  matrix products  54.9 us (24%)
  blocking collectives  49.8 us (22%)
  starting transfers between devices  14.5 us (6%)
  other arithmetic  11.9 us (5%)
  local copies, waits for them, and re-layouts  10.4 us (5%)
    all_to_all x2, waiting for transfers between devices, exchange(): lax.all_to_all(parted, 'expert', split_axis=0, concat_axis=0, tiled=True)  70.7 us
    all_to_all x1, blocking collectives, exchange(): lax.all_to_all(parted, 'expert', split_axis=0, concat_axis=0, tiled=True)  49.8 us
    ppermute x1, waiting for transfers between devices, shifted(): return lax.ppermute(value, axis, pairs)  18.7 us
    dot_general x1, matrix products, expert_backward(): lax.dot_general(dpre, gate_up, (((last,), (1,)), ((), ())), preferred_ele...  18.1 us
    dot_general x1, matrix products, expert_backward(): lax.dot_general(rows_in, gate_up, (((last,), (0,)), ((), ())), preferred_...  18 us
    dot_general x1, matrix products, expert_backward(): lax.dot_general(grad_rows, down_proj, (((last,), (1,)), ((), ())), prefer...  13.8 us
    all_to_all x2, starting transfers between devices, exchange(): lax.all_to_all(parted, 'expert', split_axis=0, concat_axis=0, tiled=True)  13.6 us
    unnamed x10, local copies, waits for them, and re-layouts  9.43 us
  transfers between devices with their start and end apart: 3, of which 3 were waited for; matrix products, arithmetic and copies ran while one was open for 12% of the time, Pallas kernels for 0%

profile of v9, /device:TPU:6, one launch (start us, length us, event | category | flops | bytes accessed | tf_op | source)
XLA Modules:
  0.0 230.9 jit_solution(3987342283293391529)
XLA Ops:
  0.0 0.8 copy.30
  0.8 0.1 eq.42
  0.9 0.1 eq.38
  1.0 1.2 reduce-window.6
  2.2 0.2 slice_reduce_fusion
  2.5 0.1 fusion.51
  2.6 0.1 reduce_sum.40
  2.7 0.1 copy.34
  2.8 0.3 fusion.38
  3.0 0.2 copy.35
  3.2 1.5 fusion.35
  4.8 0.7 reduce.1
  5.5 2.3 %convolution_convert_fusion = bf16[160,4,2880]{2,0,1:T(8,128)(2,1)S(1)} fusion(bf16[1,128,2880]{1,2,0:T(8,128)(2,1)} %param.7, f32[2880]{0:T(1024)S(1)} %reduce.1, f32[128]{0:T(128)S(1)} %add_rsqrt_fusion, pred[128,160,4]{0,2,1:T(4,128)(4,1)S(1)} %bitcast.88), kind=kOutput, calls=%fused_computation.9 | convolution fusion | flops 475176960 | bytes 4517632 | tf_op jit(solution)/shard_map/dot_general | solution.py:84
  7.8 3.8 %copy.46 = bf16[160,4,2880]{2,1,0:T(4,128)(2,1)} copy(bf16[160,4,2880]{2,0,1:T(8,128)(2,1)S(1)} %convolution_convert_fusion) | data formatting | bytes 7372800
  11.6 8.6 %all-to-all-start.1 = ((bf16[32,5,4,2880]{3,2,1,0:T(4,128)(2,1)}), bf16[32,5,4,2880]{3,2,1,0:T(4,128)(2,1)}, u32[]{:S(2)}, u32[]{:S(2)}) async-start(bf16[32,5,4,2880]{3,2,1,0:T(4,128)(2,1)} %bitcast.84), calls=%async_computation.1 | async-start | bytes 7536640 | tf_op jit(solution)/shard_map/all_to_all | solution.py:47
  20.2 0.2 select_reduce_fusion
  20.4 0.1 mul.106
  20.6 1.1 fusion.42
  21.7 7.4 %fusion.6 = bf16[160,4,2880]{2,1,0:T(4,128)(2,1)} fusion(f32[160,4,2880]{2,0,1:T(8,128)S(1)} %fusion.42, f32[160,4]{1,0:T(8,128)S(1)} %mul.106), kind=kLoop, calls=%fused_computation.7 | loop fusion | flops 3686400 | bytes 11061760 | tf_op jit(solution)/shard_map/convert_element_type | solution.py:91
  29.1 39.9 %all-to-all-done.1 = bf16[32,5,4,2880]{3,2,1,0:T(4,128)(2,1)} async-done(((bf16[32,5,4,2880]{3,2,1,0:T(4,128)(2,1)}), bf16[32,5,4,2880]{3,2,1,0:T(4,128)(2,1)}, u32[]{:S(2)}, u32[]{:S(2)}) %all-to-all-start.1) | async-done | bytes 3686432 | tf_op jit(solution)/shard_map/all_to_all | solution.py:47
  69.0 5.0 %all-to-all-start = ((bf16[32,5,4,2880]{3,2,1,0:T(4,128)(2,1)}), bf16[32,5,4,2880]{3,2,1,0:T(4,128)(2,1)}, u32[]{:S(2)}, u32[]{:S(2)}) async-start(bf16[32,5,4,2880]{3,2,1,0:T(4,128)(2,1)} %bitcast.85), calls=%async_computation | async-start | bytes 7536640 | tf_op jit(solution)/shard_map/all_to_all | solution.py:47
  74.0 18.0 %fusion.2 = f32[160,4,2880]{2,0,1:T(8,128)} fusion(bf16[1,1,2880,2880]{3,2,1,0:T(8,128)(2,1)} %param.12, bf16[160,4,2880]{2,1,0:T(4,128)(2,1)} %bitcast.14), kind=kOutput, calls=%fused_computation.2 | convolution fusion | flops 10616832000 | bytes 27648000 | tf_op jit(solution)/shard_map/dot_general | solution.py:21
  92.0 30.8 %all-to-all-done = bf16[32,5,4,2880]{3,2,1,0:T(4,128)(2,1)} async-done(((bf16[32,5,4,2880]{3,2,1,0:T(4,128)(2,1)}), bf16[32,5,4,2880]{3,2,1,0:T(4,128)(2,1)}, u32[]{:S(2)}, u32[]{:S(2)}) %all-to-all-start) | async-done | bytes 3686432 | tf_op jit(solution)/shard_map/all_to_all | solution.py:47
  122.8 13.8 %fusion.12 = (bf16[160,4,1440]{2,0,1:T(8,128)(2,1)S(1)}, bf16[160,4,1440]{2,0,1:T(8,128)(2,1)}) fusion(f32[160,4,2880]{2,0,1:T(8,128)} %fusion.2, bf16[1,1,1440,2880]{3,2,1,0:T(8,128)(2,1)} %param.13, bf16[160,4,2880]{2,1,0:T(4,128)(2,1)} %bitcast.8), kind=kOutput, calls=%fused_computation.13 | convolution fusion | flops 5322240000 | bytes 23040000 | tf_op jit(solution)/shard_map/dot_general | solution.py:24
  136.6 18.1 %fusion.7 = bf16[160,4,2880]{2,0,1:T(8,128)(2,1)} fusion(bf16[1,1,2880,2880]{3,2,1,0:T(8,128)(2,1)} %param.12, bf16[160,4,1440]{2,0,1:T(8,128)(2,1)} %get-tuple-element.6, bf16[160,4,1440]{2,0,1:T(8,128)(2,1)S(1)} %get-tuple-element.5), kind=kOutput, calls=%fused_computation.8 | convolution fusion | flops 10626048000 | bytes 23961600 | tf_op jit(solution)/shard_map/dot_general | solution.py:34
  154.6 4.0 %copy.47 = bf16[160,4,2880]{2,1,0:T(4,128)(2,1)S(1)} copy(bf16[160,4,2880]{2,0,1:T(8,128)(2,1)} %fusion.7) | data formatting | bytes 7372800
  158.7 49.8 %all_to_all.15 = bf16[32,5,4,2880]{3,2,1,0:T(4,128)(2,1)S(1)} all-to-all(bf16[32,5,4,2880]{3,2,1,0:T(4,128)(2,1)S(1)} %bitcast.86), channel_id=1, replica_groups=mesh['section'=4,'expert'=32] {'expert'}, dimensions={0} | all-to-all | bytes 7372800 | tf_op jit(solution)/shard_map/all_to_all | solution.py:47
  208.4 1.6 fusion.30
  210.0 0.4 fusion.41
  210.5 0.9 collective-permute-start
  211.4 18.7 %collective-permute-done = bf16[1,128,2880]{1,2,0:T(8,128)(2,1)S(1)} collective-permute-done((bf16[1,128,2880]{1,2,0:T(8,128)(2,1)S(1)}, bf16[1,128,2880]{1,2,0:T(8,128)(2,1)S(1)}, u32[]{:S(2)}, u32[]{:S(2)}) %collective-permute-start) | collective-permute-done | bytes 737312 | tf_op jit(solution)/shard_map/ppermute | solution.py:16
  230.1 0.9 copy.75
  (12 shorter events, 0.1 us)
Async XLA Ops:
  11.6 8.6 %copy-start.2 = (f32[1,128,4]{1,2,0:T(4,128)S(1)}, f32[1,128,4]{1,2,0:T(4,128)}, u32[]{:S(2)}) copy-start(f32[1,128,4]{1,2,0:T(4,128)} %param.11) | copy-start | bytes 6148
  11.6 8.9 %copy-start.1 = (bf16[1,128,2880]{1,2,0:T(8,128)(2,1)S(1)}, bf16[1,128,2880]{1,2,0:T(8,128)(2,1)}, u32[]{:S(2)}) copy-start(bf16[1,128,2880]{1,2,0:T(8,128)(2,1)} %param.9) | copy-start | bytes 2211844
  11.6 57.4 %all-to-all-start.1 = ((bf16[32,5,4,2880]{3,2,1,0:T(4,128)(2,1)}), bf16[32,5,4,2880]{3,2,1,0:T(4,128)(2,1)}, u32[]{:S(2)}, u32[]{:S(2)}) async-start(bf16[32,5,4,2880]{3,2,1,0:T(4,128)(2,1)} %bitcast.84), calls=%async_computation.1 | async-start | bytes 7536640 | tf_op jit(solution)/shard_map/all_to_all | solution.py:47
  69.0 53.8 %all-to-all-start = ((bf16[32,5,4,2880]{3,2,1,0:T(4,128)(2,1)}), bf16[32,5,4,2880]{3,2,1,0:T(4,128)(2,1)}, u32[]{:S(2)}, u32[]{:S(2)}) async-start(bf16[32,5,4,2880]{3,2,1,0:T(4,128)(2,1)} %bitcast.85), calls=%async_computation | async-start | bytes 7536640 | tf_op jit(solution)/shard_map/all_to_all | solution.py:47
  158.6 49.8 %copy-start = (bf16[1,128,2880]{1,2,0:T(8,128)(2,1)S(1)}, bf16[1,128,2880]{1,2,0:T(8,128)(2,1)}, u32[]{:S(2)}) copy-start(bf16[1,128,2880]{1,2,0:T(8,128)(2,1)} %param.7) | copy-start | bytes 2211844
  210.5 19.6 %collective-permute-start = (bf16[1,128,2880]{1,2,0:T(8,128)(2,1)S(1)}, bf16[1,128,2880]{1,2,0:T(8,128)(2,1)S(1)}, u32[]{:S(2)}, u32[]{:S(2)}) collective-permute-start(bf16[1,128,2880]{1,2,0:T(8,128)(2,1)S(1)} %fusion.41), channel_id=1, source_target_pairs={{0,96},{32,0},{64,32},{96,64},{1,97},{33,1},{65,33},{97,65},{2,98}... | collective-permute-start | bytes 2211848 | tf_op jit(solution)/shard_map/ppermute | solution.py:16

commit v10 on v9

--- a/solution.py
+++ b/solution.py
@@ -16,7 +16,14 @@
     return lax.ppermute(value, axis, pairs)
 
 
-def expert_backward(rows_in, grad_rows, gate_up, down_proj):
+def normalized_rows(raw_rows, gain_vector_row):
+    rows = raw_rows.astype(jnp.float32)
+    inverse_root_mean = lax.rsqrt(jnp.mean(rows * rows, axis=-1, keepdims=True) + norm_eps)
+    return ((rows * inverse_root_mean) * gain_vector_row).astype(jnp.bfloat16)
+
+
+def expert_backward(raw_rows, gain_vector_row, grad_rows, gate_up, down_proj):
+    rows_in = normalized_rows(raw_rows, gain_vector_row)
     last = rows_in.ndim - 1
     preact = lax.dot_general(
         rows_in, gate_up, (((last,), (0,)), ((), ())), preferred_element_type=jnp.float32
@@ -67,7 +74,6 @@
         jnp.mean(input_single_precision * input_single_precision, axis=-1, keepdims=True) + norm_eps
     )
     normalized_input = input_single_precision * inverse_root_mean
-    rescaled_input = (normalized_input * gain_vector_row[None, :]).astype(jnp.bfloat16)
 
     flat_ids = routes.reshape(-1)
     one_hot = (flat_ids[:, None] == jnp.arange(experts, dtype=jnp.int32)[None, :]).astype(jnp.int32)
@@ -81,7 +87,7 @@
     placement_quads = placement.astype(jnp.bfloat16).reshape(tok_count, groups, QUAD)
     pick = (((0,), (0,)), ((), ()))
     inputs_slab = row_major(
-        lax.dot_general(placement_quads, rescaled_input, pick, preferred_element_type=jnp.float32)
+        lax.dot_general(placement_quads, tokens, pick, preferred_element_type=jnp.float32)
         .astype(jnp.bfloat16)
     )
     grads_slab = row_major(
@@ -91,8 +97,9 @@
         ).astype(jnp.bfloat16)
     )
     arrived_inputs = exchange(inputs_slab, experts)
+    grads_slab, inverse_root_mean = lax.optimization_barrier((grads_slab, inverse_root_mean))
     arrived_grads = exchange(grads_slab, experts)
-    computed = expert_backward(arrived_inputs, arrived_grads, gate_up, down_proj)
+    computed = expert_backward(arrived_inputs, gain_vector_row, arrived_grads, gate_up, down_proj)
     returned = exchange(computed, experts)
     dnorm = lax.dot_general(
         placement_quads, returned, (((1, 2), (0, 1)), ((), ())), preferred_element_type=jnp.float32

time: 231 us -> 229 us (level)
  waiting for transfers between devices: 89.4 us -> 81.3 us
  other arithmetic: 11.9 us -> 18.7 us
    all_to_all x2, waiting for transfers between devices: 70.7 us -> 62.6 us  [exchange(): lax.all_to_all(parted, 'expert', split_axis=0, concat_axis=0, tiled=True)]
    convert_element_type x0 -> x1, other arithmetic: none -> 4.28 us  [normalized_rows(): return (rows * inverse_root_mean * gain_vector_row).astype(jnp.bfloat16)]
    reduce_sum x0 -> x1, other arithmetic: none -> 4.12 us  [normalized_rows(): jnp.mean(rows * rows, axis=-1, keepdims=True) + norm_eps]
    unnamed x10 -> x12, local copies, waits for them, and re-layouts: 9.43 us -> 9.47 us
  transfers between devices with their start and end apart: 3 -> 3, of which waited for: 3 -> 3; matrix products, arithmetic and copies ran while one was open for 12% -> 15% of each run, Pallas kernels for 0% -> 0%
where the time goes in v10:
time: 229 us; the launch traced here: 228 us
  waiting for transfers between devices  81.3 us (36%)
  matrix products  53.7 us (23%)
  blocking collectives  49.6 us (22%)
  other arithmetic  18.7 us (8%)
  starting transfers between devices  14.5 us (6%)
  local copies, waits for them, and re-layouts  10.4 us (5%)
    all_to_all x2, waiting for transfers between devices, exchange(): lax.all_to_all(parted, 'expert', split_axis=0, concat_axis=0, tiled=True)  62.6 us
    all_to_all x1, blocking collectives, exchange(): lax.all_to_all(parted, 'expert', split_axis=0, concat_axis=0, tiled=True)  49.6 us
    ppermute x1, waiting for transfers between devices, shifted(): return lax.ppermute(value, axis, pairs)  18.7 us
    dot_general x1, matrix products, expert_backward(): lax.dot_general(dpre, gate_up, (((last,), (1,)), ((), ())), preferred_ele...  18.1 us
    dot_general x1, matrix products, expert_backward(): lax.dot_general(rows_in, gate_up, (((last,), (0,)), ((), ())), preferred_...  16.8 us
    dot_general x1, matrix products, expert_backward(): lax.dot_general(grad_rows, down_proj, (((last,), (1,)), ((), ())), prefer...  13.8 us
    all_to_all x2, starting transfers between devices, exchange(): lax.all_to_all(parted, 'expert', split_axis=0, concat_axis=0, tiled=True)  13.6 us
    unnamed x12, local copies, waits for them, and re-layouts  9.47 us
  transfers between devices with their start and end apart: 3, of which 3 were waited for; matrix products, arithmetic and copies ran while one was open for 15% of the time, Pallas kernels for 0%

profile of v10, /device:TPU:6, one launch (start us, length us, event | category | flops | bytes accessed | tf_op | source)
XLA Modules:
  0.0 228.3 jit_solution(10628465536212833566)
XLA Ops:
  0.0 0.8 copy.61
  0.8 0.1 eq.42
  0.9 0.1 eq.38
  1.0 1.2 reduce-window.6
  2.2 0.2 slice_reduce_fusion
  2.5 0.1 fusion.47
  2.6 0.1 reduce_sum.48
  2.8 0.3 fusion.37
  3.0 0.2 copy.66
  3.2 2.3 convolution_convert_fusion
  5.5 3.8 %copy.79 = bf16[160,4,2880]{2,1,0:T(4,128)(2,1)} copy(bf16[160,4,2880]{2,0,1:T(8,128)(2,1)S(1)} %convolution_convert_fusion) | data formatting | bytes 7372800
  9.3 8.6 %all-to-all-start.1 = ((bf16[32,5,4,2880]{3,2,1,0:T(4,128)(2,1)}), bf16[32,5,4,2880]{3,2,1,0:T(4,128)(2,1)}, u32[]{:S(2)}, u32[]{:S(2)}) async-start(bf16[32,5,4,2880]{3,2,1,0:T(4,128)(2,1)} %bitcast.67), calls=%async_computation.1 | async-start | bytes 7536640 | tf_op jit(solution)/shard_map/all_to_all | solution.py:54
  17.9 0.2 select_reduce_fusion
  18.1 0.1 mul.116
  18.3 0.4 fusion.36
  18.7 1.2 fusion.40
  19.8 7.6 %fusion.9 = bf16[160,4,2880]{2,1,0:T(4,128)(2,1)} fusion(f32[160,4,2880]{2,0,1:T(8,128)S(1)} %fusion.40, f32[160,4]{1,0:T(8,128)S(1)} %mul.116), kind=kLoop, calls=%fused_computation.12 | loop fusion | flops 3686400 | bytes 11061760 | tf_op jit(solution)/shard_map/convert_element_type | solution.py:97
  27.5 39.2 %all-to-all-done.1 = bf16[32,5,4,2880]{3,2,1,0:T(4,128)(2,1)} async-done(((bf16[32,5,4,2880]{3,2,1,0:T(4,128)(2,1)}), bf16[32,5,4,2880]{3,2,1,0:T(4,128)(2,1)}, u32[]{:S(2)}, u32[]{:S(2)}) %all-to-all-start.1) | async-done | bytes 3686432 | tf_op jit(solution)/shard_map/all_to_all | solution.py:54
  66.7 5.0 %all-to-all-start = ((bf16[32,5,4,2880]{3,2,1,0:T(4,128)(2,1)}), bf16[32,5,4,2880]{3,2,1,0:T(4,128)(2,1)}, u32[]{:S(2)}, u32[]{:S(2)}) async-start(bf16[32,5,4,2880]{3,2,1,0:T(4,128)(2,1)} %bitcast.66), calls=%async_computation | async-start | bytes 7536640 | tf_op jit(solution)/shard_map/all_to_all | solution.py:54
  71.7 4.1 %fusion.6 = f32[32,5,4]{2,1,0:T(8,128)S(1)} fusion(bf16[32,5,4,2880]{3,2,1,0:T(4,128)(2,1)} %all-to-all-done.1), kind=kLoop, calls=%fused_computation.8 | loop fusion | flops 5528960 | bytes 3688960 | tf_op jit(solution)/shard_map/reduce_sum | solution.py:21
  75.8 4.3 %fusion.8 = bf16[32,5,4,2880]{3,2,1,0:T(4,128)(2,1)S(1)} fusion(bf16[32,5,4,2880]{3,2,1,0:T(4,128)(2,1)} %all-to-all-done.1, f32[2880]{0:T(1024)S(1)} %reduce.2, f32[32,5,4]{2,1,0:T(8,128)S(1)} %add_rsqrt_fusion), kind=kLoop, calls=%fused_computation.10 | loop fusion | flops 7372800 | bytes 7386880 | tf_op jit(solution)/shard_map/convert_element_type | solution.py:22
  80.1 16.8 %fusion.2 = f32[160,4,2880]{2,0,1:T(8,128)} fusion(bf16[1,1,2880,2880]{3,2,1,0:T(8,128)(2,1)} %param.12, bf16[160,4,2880]{2,1,0:T(4,128)(2,1)S(1)} %bitcast.70), kind=kOutput, calls=%fused_computation.2 | convolution fusion | flops 10616832000 | bytes 27648000 | tf_op jit(solution)/shard_map/dot_general | solution.py:28
  96.9 23.3 %all-to-all-done = bf16[32,5,4,2880]{3,2,1,0:T(4,128)(2,1)} async-done(((bf16[32,5,4,2880]{3,2,1,0:T(4,128)(2,1)}), bf16[32,5,4,2880]{3,2,1,0:T(4,128)(2,1)}, u32[]{:S(2)}, u32[]{:S(2)}) %all-to-all-start) | async-done | bytes 3686432 | tf_op jit(solution)/shard_map/all_to_all | solution.py:54
  120.3 13.8 %fusion.15 = (bf16[160,4,1440]{2,0,1:T(8,128)(2,1)S(1)}, bf16[160,4,1440]{2,0,1:T(8,128)(2,1)}) fusion(f32[160,4,2880]{2,0,1:T(8,128)} %fusion.2, bf16[1,1,1440,2880]{3,2,1,0:T(8,128)(2,1)} %param.13, bf16[160,4,2880]{2,1,0:T(4,128)(2,1)} %bitcast.10), kind=kOutput, calls=%fused_computation.18 | convolution fusion | flops 5322240000 | bytes 23040000 | tf_op jit(solution)/shard_map/dot_general | solution.py:31
  134.1 18.1 %fusion.10 = bf16[160,4,2880]{2,0,1:T(8,128)(2,1)} fusion(bf16[1,1,2880,2880]{3,2,1,0:T(8,128)(2,1)} %param.12, bf16[160,4,1440]{2,0,1:T(8,128)(2,1)} %get-tuple-element.10, bf16[160,4,1440]{2,0,1:T(8,128)(2,1)S(1)} %get-tuple-element.9), kind=kOutput, calls=%fused_computation.13 | convolution fusion | flops 10626048000 | bytes 23961600 | tf_op jit(solution)/shard_map/dot_general | solution.py:41
  152.2 4.0 %copy.81 = bf16[160,4,2880]{2,1,0:T(4,128)(2,1)S(1)} copy(bf16[160,4,2880]{2,0,1:T(8,128)(2,1)} %fusion.10) | data formatting | bytes 7372800
  156.2 49.6 %all_to_all.15 = bf16[32,5,4,2880]{3,2,1,0:T(4,128)(2,1)S(1)} all-to-all(bf16[32,5,4,2880]{3,2,1,0:T(4,128)(2,1)S(1)} %bitcast.68), channel_id=1, replica_groups=mesh['section'=4,'expert'=32] {'expert'}, dimensions={0} | all-to-all | bytes 7372800 | tf_op jit(solution)/shard_map/all_to_all | solution.py:54
  205.8 1.6 fusion.31
  207.4 0.4 fusion.38
  207.9 0.9 collective-permute-start
  208.8 18.7 %collective-permute-done = bf16[1,128,2880]{1,2,0:T(8,128)(2,1)S(1)} collective-permute-done((bf16[1,128,2880]{1,2,0:T(8,128)(2,1)S(1)}, bf16[1,128,2880]{1,2,0:T(8,128)(2,1)S(1)}, u32[]{:S(2)}, u32[]{:S(2)}) %collective-permute-start) | collective-permute-done | bytes 737312 | tf_op jit(solution)/shard_map/ppermute | solution.py:16
  227.5 0.9 copy.109
  (17 shorter events, 0.2 us)
Async XLA Ops:
  9.3 8.6 %copy-start.3 = (f32[1,128,4]{1,2,0:T(4,128)S(1)}, f32[1,128,4]{1,2,0:T(4,128)}, u32[]{:S(2)}) copy-start(f32[1,128,4]{1,2,0:T(4,128)} %param.11) | copy-start | bytes 6148
  9.3 8.9 %copy-start = (bf16[1,128,2880]{1,2,0:T(8,128)(2,1)S(1)}, bf16[1,128,2880]{1,2,0:T(8,128)(2,1)}, u32[]{:S(2)}) copy-start(bf16[1,128,2880]{1,2,0:T(8,128)(2,1)} %param.7) | copy-start | bytes 2211844
  9.3 9.3 %copy-start.1 = (bf16[1,128,2880]{1,2,0:T(8,128)(2,1)S(1)}, bf16[1,128,2880]{1,2,0:T(8,128)(2,1)}, u32[]{:S(2)}) copy-start(bf16[1,128,2880]{1,2,0:T(8,128)(2,1)} %param.9) | copy-start | bytes 2211844
  9.3 57.4 %all-to-all-start.1 = ((bf16[32,5,4,2880]{3,2,1,0:T(4,128)(2,1)}), bf16[32,5,4,2880]{3,2,1,0:T(4,128)(2,1)}, u32[]{:S(2)}, u32[]{:S(2)}) async-start(bf16[32,5,4,2880]{3,2,1,0:T(4,128)(2,1)} %bitcast.67), calls=%async_computation.1 | async-start | bytes 7536640 | tf_op jit(solution)/shard_map/all_to_all | solution.py:54
  19.8 7.6 %copy-start.2 = (f32[1,2880]{1,0:T(1,128)S(1)}, f32[1,2880]{1,0:T(1,128)}, u32[]{:S(2)}) copy-start(f32[1,2880]{1,0:T(1,128)} %param.8) | copy-start | bytes 34564
  66.7 53.6 %all-to-all-start = ((bf16[32,5,4,2880]{3,2,1,0:T(4,128)(2,1)}), bf16[32,5,4,2880]{3,2,1,0:T(4,128)(2,1)}, u32[]{:S(2)}, u32[]{:S(2)}) async-start(bf16[32,5,4,2880]{3,2,1,0:T(4,128)(2,1)} %bitcast.66), calls=%async_computation | async-start | bytes 7536640 | tf_op jit(solution)/shard_map/all_to_all | solution.py:54
  207.9 19.6 %collective-permute-start = (bf16[1,128,2880]{1,2,0:T(8,128)(2,1)S(1)}, bf16[1,128,2880]{1,2,0:T(8,128)(2,1)S(1)}, u32[]{:S(2)}, u32[]{:S(2)}) collective-permute-start(bf16[1,128,2880]{1,2,0:T(8,128)(2,1)S(1)} %fusion.38), channel_id=1, source_target_pairs={{0,96},{32,0},{64,32},{96,64},{1,97},{33,1},{65,33},{97,65},{2,98}... | collective-permute-start | bytes 2211848 | tf_op jit(solution)/shard_map/ppermute | solution.py:16

commit v11 on v10

--- a/solution.py
+++ b/solution.py
@@ -76,8 +76,11 @@
     normalized_input = input_single_precision * inverse_root_mean
 
     flat_ids = routes.reshape(-1)
-    one_hot = (flat_ids[:, None] == jnp.arange(experts, dtype=jnp.int32)[None, :]).astype(jnp.int32)
-    slot_rank = jnp.sum((jnp.cumsum(one_hot, axis=0) - one_hot) * one_hot, axis=1)
+    one_hot = (flat_ids[:, None] == jnp.arange(experts, dtype=jnp.int32)[None, :]).astype(jnp.bfloat16)
+    order = jnp.arange(flat_ids.shape[0], dtype=jnp.int32)
+    earlier = (order[:, None] > order[None, :]).astype(jnp.bfloat16)
+    prior = jnp.dot(earlier, one_hot, preferred_element_type=jnp.float32)
+    slot_rank = jnp.sum(prior * one_hot.astype(jnp.float32), axis=1).astype(jnp.int32)
     slot_index = (flat_ids * capacity + slot_rank).reshape(tok_count, top_count)
     slot_ids = jnp.arange(experts * capacity, dtype=jnp.int32)
     hits = slot_index[:, :, None] == slot_ids[None, None, :]

time: 229 us -> 227 us (level)
  no operation moved by 1% of the time
where the time goes in v11:
time: 227 us
  waiting for transfers between devices  81.3 us (36%)
  matrix products  54 us (24%)
  blocking collectives  49.6 us (22%)
  other arithmetic  17.3 us (8%)
  starting transfers between devices  14.5 us (6%)
  local copies, waits for them, and re-layouts  10.1 us (4%)
    all_to_all x2, waiting for transfers between devices, exchange(): lax.all_to_all(parted, 'expert', split_axis=0, concat_axis=0, tiled=True)  62.6 us
    all_to_all x1, blocking collectives, exchange(): lax.all_to_all(parted, 'expert', split_axis=0, concat_axis=0, tiled=True)  49.6 us
    ppermute x1, waiting for transfers between devices, shifted(): return lax.ppermute(value, axis, pairs)  18.7 us
    dot_general x1, matrix products, expert_backward(): lax.dot_general(dpre, gate_up, (((last,), (1,)), ((), ())), preferred_ele...  18.1 us
    dot_general x1, matrix products, expert_backward(): lax.dot_general(rows_in, gate_up, (((last,), (0,)), ((), ())), preferred_...  16.8 us
    dot_general x1, matrix products, expert_backward(): lax.dot_general(grad_rows, down_proj, (((last,), (1,)), ((), ())), prefer...  13.8 us
    all_to_all x2, starting transfers between devices, exchange(): lax.all_to_all(parted, 'expert', split_axis=0, concat_axis=0, tiled=True)  13.6 us
    unnamed x12, local copies, waits for them, and re-layouts  9.47 us
  transfers between devices with their start and end apart: 3, of which 3 were waited for; matrix products, arithmetic and copies ran while one was open for 15% of the time, Pallas kernels for 0%

profile of v11, /device:TPU:6, one launch (start us, length us, event | category | flops | bytes accessed | tf_op | source)
XLA Modules:
  0.0 227.0 jit_solution(12362700678267462815)
XLA Ops:
  0.0 0.8 copy.55
  0.8 0.1 eq.28
  0.9 0.3 fusion.38
  1.2 0.1 convert_element_type.52
  1.3 0.1 copy.57
  1.4 0.3 fusion.37
  1.6 0.2 copy.58
  1.9 2.3 convolution_convert_fusion
  4.1 3.8 %copy.70 = bf16[160,4,2880]{2,1,0:T(4,128)(2,1)} copy(bf16[160,4,2880]{2,0,1:T(8,128)(2,1)S(1)} %convolution_convert_fusion) | data formatting | bytes 7372800
  7.9 8.6 %all-to-all-start.1 = ((bf16[32,5,4,2880]{3,2,1,0:T(4,128)(2,1)}), bf16[32,5,4,2880]{3,2,1,0:T(4,128)(2,1)}, u32[]{:S(2)}, u32[]{:S(2)}) async-start(bf16[32,5,4,2880]{3,2,1,0:T(4,128)(2,1)} %bitcast.48), calls=%async_computation.1 | async-start | bytes 7536640 | tf_op jit(solution)/shard_map/all_to_all | solution.py:54
  16.5 0.2 select_reduce_fusion
  16.8 0.1 mul.116
  16.9 0.4 fusion.36
  17.3 0.0 copy-done.1
  17.3 1.1 fusion.41
  18.4 0.0 copy-start.2
  18.5 7.6 %fusion.9 = bf16[160,4,2880]{2,1,0:T(4,128)(2,1)} fusion(f32[160,4,2880]{2,0,1:T(8,128)S(1)} %fusion.41, f32[160,4]{1,0:T(8,128)S(1)} %mul.116), kind=kLoop, calls=%fused_computation.12 | loop fusion | flops 3686400 | bytes 11061760 | tf_op jit(solution)/shard_map/convert_element_type | solution.py:100
  26.1 39.2 %all-to-all-done.1 = bf16[32,5,4,2880]{3,2,1,0:T(4,128)(2,1)} async-done(((bf16[32,5,4,2880]{3,2,1,0:T(4,128)(2,1)}), bf16[32,5,4,2880]{3,2,1,0:T(4,128)(2,1)}, u32[]{:S(2)}, u32[]{:S(2)}) %all-to-all-start.1) | async-done | bytes 3686432 | tf_op jit(solution)/shard_map/all_to_all | solution.py:54
  65.3 5.0 %all-to-all-start = ((bf16[32,5,4,2880]{3,2,1,0:T(4,128)(2,1)}), bf16[32,5,4,2880]{3,2,1,0:T(4,128)(2,1)}, u32[]{:S(2)}, u32[]{:S(2)}) async-start(bf16[32,5,4,2880]{3,2,1,0:T(4,128)(2,1)} %bitcast.47), calls=%async_computation | async-start | bytes 7536640 | tf_op jit(solution)/shard_map/all_to_all | solution.py:54
  70.3 4.1 %fusion.6 = f32[32,5,4]{2,1,0:T(8,128)S(1)} fusion(bf16[32,5,4,2880]{3,2,1,0:T(4,128)(2,1)} %all-to-all-done.1), kind=kLoop, calls=%fused_computation.8 | loop fusion | flops 5528960 | bytes 3688960 | tf_op jit(solution)/shard_map/reduce_sum | solution.py:21
  74.5 4.3 %fusion.8 = bf16[32,5,4,2880]{3,2,1,0:T(4,128)(2,1)S(1)} fusion(bf16[32,5,4,2880]{3,2,1,0:T(4,128)(2,1)} %all-to-all-done.1, f32[2880]{0:T(1024)S(1)} %reduce.1, f32[32,5,4]{2,1,0:T(8,128)S(1)} %add_rsqrt_fusion), kind=kLoop, calls=%fused_computation.10 | loop fusion | flops 7372800 | bytes 7386880 | tf_op jit(solution)/shard_map/convert_element_type | solution.py:22
  78.8 16.8 %fusion.2 = f32[160,4,2880]{2,0,1:T(8,128)} fusion(bf16[1,1,2880,2880]{3,2,1,0:T(8,128)(2,1)} %param.12, bf16[160,4,2880]{2,1,0:T(4,128)(2,1)S(1)} %bitcast.51), kind=kOutput, calls=%fused_computation.2 | convolution fusion | flops 10616832000 | bytes 27648000 | tf_op jit(solution)/shard_map/dot_general | solution.py:28
  95.6 23.3 %all-to-all-done = bf16[32,5,4,2880]{3,2,1,0:T(4,128)(2,1)} async-done(((bf16[32,5,4,2880]{3,2,1,0:T(4,128)(2,1)}), bf16[32,5,4,2880]{3,2,1,0:T(4,128)(2,1)}, u32[]{:S(2)}, u32[]{:S(2)}) %all-to-all-start) | async-done | bytes 3686432 | tf_op jit(solution)/shard_map/all_to_all | solution.py:54
  118.9 13.8 %fusion.15 = (bf16[160,4,1440]{2,0,1:T(8,128)(2,1)S(1)}, bf16[160,4,1440]{2,0,1:T(8,128)(2,1)}) fusion(f32[160,4,2880]{2,0,1:T(8,128)} %fusion.2, bf16[1,1,1440,2880]{3,2,1,0:T(8,128)(2,1)} %param.13, bf16[160,4,2880]{2,1,0:T(4,128)(2,1)} %bitcast.9), kind=kOutput, calls=%fused_computation.18 | convolution fusion | flops 5322240000 | bytes 23040000 | tf_op jit(solution)/shard_map/dot_general | solution.py:31
  132.7 18.1 %fusion.10 = bf16[160,4,2880]{2,0,1:T(8,128)(2,1)} fusion(bf16[1,1,2880,2880]{3,2,1,0:T(8,128)(2,1)} %param.12, bf16[160,4,1440]{2,0,1:T(8,128)(2,1)} %get-tuple-element.10, bf16[160,4,1440]{2,0,1:T(8,128)(2,1)S(1)} %get-tuple-element.9), kind=kOutput, calls=%fused_computation.13 | convolution fusion | flops 10626048000 | bytes 23961600 | tf_op jit(solution)/shard_map/dot_general | solution.py:41
  150.8 4.0 %copy.72 = bf16[160,4,2880]{2,1,0:T(4,128)(2,1)S(1)} copy(bf16[160,4,2880]{2,0,1:T(8,128)(2,1)} %fusion.10) | data formatting | bytes 7372800
  154.8 49.6 %all_to_all.15 = bf16[32,5,4,2880]{3,2,1,0:T(4,128)(2,1)S(1)} all-to-all(bf16[32,5,4,2880]{3,2,1,0:T(4,128)(2,1)S(1)} %bitcast.49), channel_id=1, replica_groups=mesh['section'=4,'expert'=32] {'expert'}, dimensions={0} | all-to-all | bytes 7372800 | tf_op jit(solution)/shard_map/all_to_all | solution.py:54
  204.4 1.6 fusion.31
  206.1 0.4 fusion.39
  206.5 0.9 collective-permute-start
  207.4 18.7 %collective-permute-done = bf16[1,128,2880]{1,2,0:T(8,128)(2,1)S(1)} collective-permute-done((bf16[1,128,2880]{1,2,0:T(8,128)(2,1)S(1)}, bf16[1,128,2880]{1,2,0:T(8,128)(2,1)S(1)}, u32[]{:S(2)}, u32[]{:S(2)}) %collective-permute-start) | collective-permute-done | bytes 737312 | tf_op jit(solution)/shard_map/ppermute | solution.py:16
  226.1 0.9 copy.99
  (12 shorter events, 0.1 us)
Async XLA Ops:
  7.9 8.6 %copy-start.3 = (f32[1,128,4]{1,2,0:T(4,128)S(1)}, f32[1,128,4]{1,2,0:T(4,128)}, u32[]{:S(2)}) copy-start(f32[1,128,4]{1,2,0:T(4,128)} %param.11) | copy-start | bytes 6148
  7.9 8.9 %copy-start = (bf16[1,128,2880]{1,2,0:T(8,128)(2,1)S(1)}, bf16[1,128,2880]{1,2,0:T(8,128)(2,1)}, u32[]{:S(2)}) copy-start(bf16[1,128,2880]{1,2,0:T(8,128)(2,1)} %param.7) | copy-start | bytes 2211844
  7.9 9.3 %copy-start.1 = (bf16[1,128,2880]{1,2,0:T(8,128)(2,1)S(1)}, bf16[1,128,2880]{1,2,0:T(8,128)(2,1)}, u32[]{:S(2)}) copy-start(bf16[1,128,2880]{1,2,0:T(8,128)(2,1)} %param.9) | copy-start | bytes 2211844
  7.9 57.4 %all-to-all-start.1 = ((bf16[32,5,4,2880]{3,2,1,0:T(4,128)(2,1)}), bf16[32,5,4,2880]{3,2,1,0:T(4,128)(2,1)}, u32[]{:S(2)}, u32[]{:S(2)}) async-start(bf16[32,5,4,2880]{3,2,1,0:T(4,128)(2,1)} %bitcast.48), calls=%async_computation.1 | async-start | bytes 7536640 | tf_op jit(solution)/shard_map/all_to_all | solution.py:54
  18.4 7.6 %copy-start.2 = (f32[1,2880]{1,0:T(1,128)S(1)}, f32[1,2880]{1,0:T(1,128)}, u32[]{:S(2)}) copy-start(f32[1,2880]{1,0:T(1,128)} %param.8) | copy-start | bytes 34564
  65.3 53.6 %all-to-all-start = ((bf16[32,5,4,2880]{3,2,1,0:T(4,128)(2,1)}), bf16[32,5,4,2880]{3,2,1,0:T(4,128)(2,1)}, u32[]{:S(2)}, u32[]{:S(2)}) async-start(bf16[32,5,4,2880]{3,2,1,0:T(4,128)(2,1)} %bitcast.47), calls=%async_computation | async-start | bytes 7536640 | tf_op jit(solution)/shard_map/all_to_all | solution.py:54
  206.5 19.6 %collective-permute-start = (bf16[1,128,2880]{1,2,0:T(8,128)(2,1)S(1)}, bf16[1,128,2880]{1,2,0:T(8,128)(2,1)S(1)}, u32[]{:S(2)}, u32[]{:S(2)}) collective-permute-start(bf16[1,128,2880]{1,2,0:T(8,128)(2,1)S(1)} %fusion.39), channel_id=1, source_target_pairs={{0,96},{32,0},{64,32},{96,64},{1,97},{33,1},{65,33},{97,65},{2,98}... | collective-permute-start | bytes 2211848 | tf_op jit(solution)/shard_map/ppermute | solution.py:16

commit v12 on v11

--- a/solution.py
+++ b/solution.py
@@ -75,13 +75,13 @@
     )
     normalized_input = input_single_precision * inverse_root_mean
 
-    flat_ids = routes.reshape(-1)
+    flat_ids = routes.T.reshape(-1)
     one_hot = (flat_ids[:, None] == jnp.arange(experts, dtype=jnp.int32)[None, :]).astype(jnp.bfloat16)
     order = jnp.arange(flat_ids.shape[0], dtype=jnp.int32)
     earlier = (order[:, None] > order[None, :]).astype(jnp.bfloat16)
     prior = jnp.dot(earlier, one_hot, preferred_element_type=jnp.float32)
     slot_rank = jnp.sum(prior * one_hot.astype(jnp.float32), axis=1).astype(jnp.int32)
-    slot_index = (flat_ids * capacity + slot_rank).reshape(tok_count, top_count)
+    slot_index = (flat_ids * capacity + slot_rank).reshape(top_count, tok_count).T
     slot_ids = jnp.arange(experts * capacity, dtype=jnp.int32)
     hits = slot_index[:, :, None] == slot_ids[None, None, :]
     placement = jnp.any(hits, axis=1)

time: 227 us -> 228 us (level)
    unnamed x12 -> x11, local copies, waits for them, and re-layouts: 9.47 us -> 8.68 us
where the time goes in v12:
time: 228 us; the launch traced here: 227 us
  waiting for transfers between devices  81.4 us (36%)
  matrix products  54.8 us (24%)
  blocking collectives  49.6 us (22%)
  other arithmetic  17.9 us (8%)
  starting transfers between devices  14.5 us (6%)
  local copies, waits for them, and re-layouts  9 us (4%)
    all_to_all x2, waiting for transfers between devices, exchange(): lax.all_to_all(parted, 'expert', split_axis=0, concat_axis=0, tiled=True)  62.6 us
    all_to_all x1, blocking collectives, exchange(): lax.all_to_all(parted, 'expert', split_axis=0, concat_axis=0, tiled=True)  49.6 us
    ppermute x1, waiting for transfers between devices, shifted(): return lax.ppermute(value, axis, pairs)  18.7 us
    dot_general x1, matrix products, expert_backward(): lax.dot_general(dpre, gate_up, (((last,), (1,)), ((), ())), preferred_ele...  18.1 us
    dot_general x1, matrix products, expert_backward(): lax.dot_general(rows_in, gate_up, (((last,), (0,)), ((), ())), preferred_...  16.9 us
    dot_general x1, matrix products, expert_backward(): lax.dot_general(grad_rows, down_proj, (((last,), (1,)), ((), ())), prefer...  13.8 us
    all_to_all x2, starting transfers between devices, exchange(): lax.all_to_all(parted, 'expert', split_axis=0, concat_axis=0, tiled=True)  13.6 us
    unnamed x11, local copies, waits for them, and re-layouts  8.68 us
  transfers between devices with their start and end apart: 3, of which 3 were waited for; matrix products, arithmetic and copies ran while one was open for 15% of the time, Pallas kernels for 0%

profile of v12, /device:TPU:6, one launch (start us, length us, event | category | flops | bytes accessed | tf_op | source)
XLA Modules:
  0.0 227.3 jit_solution(7558940522704756320)
XLA Ops:
  0.0 1.0 fusion.38
  1.0 0.7 fusion.48
  1.7 0.2 fusion.37
  2.0 0.2 copy.48
  2.2 2.3 convolution_convert_fusion
  4.5 3.8 %copy.60 = bf16[160,4,2880]{2,1,0:T(4,128)(2,1)} copy(bf16[160,4,2880]{2,0,1:T(8,128)(2,1)S(1)} %convolution_convert_fusion) | data formatting | bytes 7372800
  8.3 8.6 %all-to-all-start.1 = ((bf16[32,5,4,2880]{3,2,1,0:T(4,128)(2,1)}), bf16[32,5,4,2880]{3,2,1,0:T(4,128)(2,1)}, u32[]{:S(2)}, u32[]{:S(2)}) async-start(bf16[32,5,4,2880]{3,2,1,0:T(4,128)(2,1)} %bitcast.60), calls=%async_computation.1 | async-start | bytes 7536640 | tf_op jit(solution)/shard_map/all_to_all | solution.py:54
  16.8 0.0 copy-done.3
  16.9 0.2 select_reduce_fusion
  17.1 0.1 mul.109
  17.2 0.0 copy-done
  17.2 0.4 fusion.36
  17.6 0.0 copy-done.1
  17.6 1.1 fusion.41
  18.8 0.0 copy-start.2
  18.8 7.5 %fusion.9 = bf16[160,4,2880]{2,1,0:T(4,128)(2,1)} fusion(f32[160,4,2880]{2,0,1:T(8,128)S(1)} %fusion.41, f32[160,4]{1,0:T(8,128)S(1)} %mul.109), kind=kLoop, calls=%fused_computation.12 | loop fusion | flops 3686400 | bytes 11061760 | tf_op jit(solution)/shard_map/convert_element_type | solution.py:100
  26.2 0.0 copy-done.2
  26.3 39.3 %all-to-all-done.1 = bf16[32,5,4,2880]{3,2,1,0:T(4,128)(2,1)} async-done(((bf16[32,5,4,2880]{3,2,1,0:T(4,128)(2,1)}), bf16[32,5,4,2880]{3,2,1,0:T(4,128)(2,1)}, u32[]{:S(2)}, u32[]{:S(2)}) %all-to-all-start.1) | async-done | bytes 3686432 | tf_op jit(solution)/shard_map/all_to_all | solution.py:54
  65.6 5.0 %all-to-all-start = ((bf16[32,5,4,2880]{3,2,1,0:T(4,128)(2,1)}), bf16[32,5,4,2880]{3,2,1,0:T(4,128)(2,1)}, u32[]{:S(2)}, u32[]{:S(2)}) async-start(bf16[32,5,4,2880]{3,2,1,0:T(4,128)(2,1)} %bitcast.59), calls=%async_computation | async-start | bytes 7536640 | tf_op jit(solution)/shard_map/all_to_all | solution.py:54
  70.6 4.1 %fusion.6 = f32[32,5,4]{2,1,0:T(8,128)S(1)} fusion(bf16[32,5,4,2880]{3,2,1,0:T(4,128)(2,1)} %all-to-all-done.1), kind=kLoop, calls=%fused_computation.8 | loop fusion | flops 5528960 | bytes 3688960 | tf_op jit(solution)/shard_map/reduce_sum | solution.py:21
  74.8 4.3 %fusion.8 = bf16[32,5,4,2880]{3,2,1,0:T(4,128)(2,1)S(1)} fusion(bf16[32,5,4,2880]{3,2,1,0:T(4,128)(2,1)} %all-to-all-done.1, f32[2880]{0:T(1024)S(1)} %reduce.1, f32[32,5,4]{2,1,0:T(8,128)S(1)} %add_rsqrt_fusion), kind=kLoop, calls=%fused_computation.10 | loop fusion | flops 7372800 | bytes 7386880 | tf_op jit(solution)/shard_map/convert_element_type | solution.py:22
  79.1 16.9 %fusion.2 = f32[160,4,2880]{2,0,1:T(8,128)} fusion(bf16[1,1,2880,2880]{3,2,1,0:T(8,128)(2,1)} %param.12, bf16[160,4,2880]{2,1,0:T(4,128)(2,1)S(1)} %bitcast.63), kind=kOutput, calls=%fused_computation.2 | convolution fusion | flops 10616832000 | bytes 27648000 | tf_op jit(solution)/shard_map/dot_general | solution.py:28
  95.9 23.3 %all-to-all-done = bf16[32,5,4,2880]{3,2,1,0:T(4,128)(2,1)} async-done(((bf16[32,5,4,2880]{3,2,1,0:T(4,128)(2,1)}), bf16[32,5,4,2880]{3,2,1,0:T(4,128)(2,1)}, u32[]{:S(2)}, u32[]{:S(2)}) %all-to-all-start) | async-done | bytes 3686432 | tf_op jit(solution)/shard_map/all_to_all | solution.py:54
  119.2 13.8 %fusion.15 = (bf16[160,4,1440]{2,0,1:T(8,128)(2,1)S(1)}, bf16[160,4,1440]{2,0,1:T(8,128)(2,1)}) fusion(f32[160,4,2880]{2,0,1:T(8,128)} %fusion.2, bf16[1,1,1440,2880]{3,2,1,0:T(8,128)(2,1)} %param.13, bf16[160,4,2880]{2,1,0:T(4,128)(2,1)} %bitcast.14), kind=kOutput, calls=%fused_computation.18 | convolution fusion | flops 5322240000 | bytes 23040000 | tf_op jit(solution)/shard_map/dot_general | solution.py:31
  133.0 18.1 %fusion.10 = bf16[160,4,2880]{2,0,1:T(8,128)(2,1)} fusion(bf16[1,1,2880,2880]{3,2,1,0:T(8,128)(2,1)} %param.12, bf16[160,4,1440]{2,0,1:T(8,128)(2,1)} %get-tuple-element.10, bf16[160,4,1440]{2,0,1:T(8,128)(2,1)S(1)} %get-tuple-element.9), kind=kOutput, calls=%fused_computation.13 | convolution fusion | flops 10626048000 | bytes 23961600 | tf_op jit(solution)/shard_map/dot_general | solution.py:41
  151.1 4.0 %copy.62 = bf16[160,4,2880]{2,1,0:T(4,128)(2,1)S(1)} copy(bf16[160,4,2880]{2,0,1:T(8,128)(2,1)} %fusion.10) | data formatting | bytes 7372800
  155.1 49.6 %all_to_all.15 = bf16[32,5,4,2880]{3,2,1,0:T(4,128)(2,1)S(1)} all-to-all(bf16[32,5,4,2880]{3,2,1,0:T(4,128)(2,1)S(1)} %bitcast.61), channel_id=1, replica_groups=mesh['section'=4,'expert'=32] {'expert'}, dimensions={0} | all-to-all | bytes 7372800 | tf_op jit(solution)/shard_map/all_to_all | solution.py:54
  204.8 1.6 fusion.31
  206.4 0.4 fusion.39
  206.8 0.9 collective-permute-start
  207.7 18.7 %collective-permute-done = bf16[1,128,2880]{1,2,0:T(8,128)(2,1)S(1)} collective-permute-done((bf16[1,128,2880]{1,2,0:T(8,128)(2,1)S(1)}, bf16[1,128,2880]{1,2,0:T(8,128)(2,1)S(1)}, u32[]{:S(2)}, u32[]{:S(2)}) %collective-permute-start) | collective-permute-done | bytes 737312 | tf_op jit(solution)/shard_map/ppermute | solution.py:16
  226.4 0.9 copy.89
  (7 shorter events, 0.1 us)
Async XLA Ops:
  8.3 8.6 %copy-start.3 = (f32[1,128,4]{1,2,0:T(4,128)S(1)}, f32[1,128,4]{1,2,0:T(4,128)}, u32[]{:S(2)}) copy-start(f32[1,128,4]{1,2,0:T(4,128)} %param.11) | copy-start | bytes 6148
  8.3 8.9 %copy-start = (bf16[1,128,2880]{1,2,0:T(8,128)(2,1)S(1)}, bf16[1,128,2880]{1,2,0:T(8,128)(2,1)}, u32[]{:S(2)}) copy-start(bf16[1,128,2880]{1,2,0:T(8,128)(2,1)} %param.7) | copy-start | bytes 2211844
  8.3 9.3 %copy-start.1 = (bf16[1,128,2880]{1,2,0:T(8,128)(2,1)S(1)}, bf16[1,128,2880]{1,2,0:T(8,128)(2,1)}, u32[]{:S(2)}) copy-start(bf16[1,128,2880]{1,2,0:T(8,128)(2,1)} %param.9) | copy-start | bytes 2211844
  8.3 57.4 %all-to-all-start.1 = ((bf16[32,5,4,2880]{3,2,1,0:T(4,128)(2,1)}), bf16[32,5,4,2880]{3,2,1,0:T(4,128)(2,1)}, u32[]{:S(2)}, u32[]{:S(2)}) async-start(bf16[32,5,4,2880]{3,2,1,0:T(4,128)(2,1)} %bitcast.60), calls=%async_computation.1 | async-start | bytes 7536640 | tf_op jit(solution)/shard_map/all_to_all | solution.py:54
  18.8 7.5 %copy-start.2 = (f32[1,2880]{1,0:T(1,128)S(1)}, f32[1,2880]{1,0:T(1,128)}, u32[]{:S(2)}) copy-start(f32[1,2880]{1,0:T(1,128)} %param.8) | copy-start | bytes 34564
  65.6 53.6 %all-to-all-start = ((bf16[32,5,4,2880]{3,2,1,0:T(4,128)(2,1)}), bf16[32,5,4,2880]{3,2,1,0:T(4,128)(2,1)}, u32[]{:S(2)}, u32[]{:S(2)}) async-start(bf16[32,5,4,2880]{3,2,1,0:T(4,128)(2,1)} %bitcast.59), calls=%async_computation | async-start | bytes 7536640 | tf_op jit(solution)/shard_map/all_to_all | solution.py:54
  206.8 19.6 %collective-permute-start = (bf16[1,128,2880]{1,2,0:T(8,128)(2,1)S(1)}, bf16[1,128,2880]{1,2,0:T(8,128)(2,1)S(1)}, u32[]{:S(2)}, u32[]{:S(2)}) collective-permute-start(bf16[1,128,2880]{1,2,0:T(8,128)(2,1)S(1)} %fusion.39), channel_id=1, source_target_pairs={{0,96},{32,0},{64,32},{96,64},{1,97},{33,1},{65,33},{97,65},{2,98}... | collective-permute-start | bytes 2211848 | tf_op jit(solution)/shard_map/ppermute | solution.py:16
